TPU v7x, 512 devices: a whole 4x8x8 slice. The times are simulated.
512 devices in a mesh: seq: 32 (over x, y), row: 4 (over z_hi, core), col: 4 (over z_lo).
Axes of the slice: x: 4, y: 8, z: 8 (z_hi: 2, z_lo: 4; z = z_hi * 4 + z_lo), core: 2. Of those that a mesh axis runs over, the one named last changes fastest.
Arguments:
- queries: bfloat16 [2048, 8192], P(('seq', 'row', 'col')), may hold values from -6 to 6
- new_keys: bfloat16 [2048, 1024], P(('seq', 'row', 'col')), may hold values from -6 to 6
- new_values: bfloat16 [2048, 1024], P(('seq', 'row', 'col')), may hold values from -6 to 6
- positions: int32 [2048], P(('seq', 'row', 'col')), may hold values from 0 to 2047, each once
- cache_keys: bfloat16 [4096, 1024], P(('row', 'col')), may hold values from -6 to 6
- cache_values: bfloat16 [4096, 1024], P(('row', 'col')), may hold values from -6 to 6
- slab_start: int32 [1], replicated, may hold values from 2048 to 4096
Outputs:
- context: bfloat16 [2048, 8192], P(('seq', 'row', 'col'))
Inputs may be any that keep to these rules, and one draw needn't show every extreme that they name: positions holds every number of 0 to 2047 once.
All inputs are finite; a program needn't handle non-finite values.
Results may differ from a plain program's by a relative error of at most 0.0065.
Values may be sent and summed in bfloat16 or wider, within the bound.
No kernel may reach another device: no remote copies, remote signals or barrier semaphores. Data moves between devices by JAX's collectives and lax.ppermute only.
A program may use at most 64 MiB of HBM per device.

v0:
```python
import math

import jax
import jax.numpy as jnp
from jax import lax
from jax.sharding import PartitionSpec as P

HQ = 64
KVH = 8
HD = 128


far_position = 1073741824
masked_score = -1e30


def attend(carried, query_block, query_pos, key_rows, value_rows, key_pos, kv_dev):
    running_max, running_sum, running_out = carried
    key_count = key_rows.shape[0]
    head_size = query_block.shape[-1]
    score_scale = 1.0 / math.sqrt(head_size)
    block_size = 1024
    for offset in range(0, key_count, block_size):
        finish = min(key_count, offset + block_size)
        key_block = key_rows[offset:finish].reshape(finish - offset, kv_dev, head_size)
        value_block = value_rows[offset:finish].reshape(finish - offset, kv_dev, head_size)
        scores = (
            jnp.einsum("qghd,ngd->qghn", query_block, key_block, preferred_element_type=jnp.float32)
            * score_scale
        )
        allowed = (key_pos[offset:finish][None, :] <= query_pos[:, None])[:, None, None, :]
        updated = jnp.maximum(
            running_max, jnp.max(jnp.where(allowed, scores, masked_score), axis=-1)
        )
        exponent = jnp.where(allowed, jnp.exp(scores - updated[..., None]), 0.0)
        factor = jnp.exp(running_max - updated)
        running_sum = running_sum * factor + jnp.sum(exponent, axis=-1)
        running_out = running_out * factor[..., None] + jnp.einsum(
            "qghn,ngd->qghd",
            exponent.astype(jnp.bfloat16),
            value_block,
            preferred_element_type=jnp.float32,
        )
        running_max = updated
    return (running_max, running_sum, running_out)


def spread_heads(matrix, seq_count, kv_dev, head_size):
    row_count = matrix.shape[0]
    kv_heads = matrix.shape[1] // head_size
    repeat = max(1, seq_count * kv_dev // kv_heads)
    reshaped = matrix.reshape(row_count, kv_heads, head_size)
    reshaped = jnp.repeat(reshaped, repeat, axis=1)
    return reshaped


def on_device(queries, new_keys, new_values, positions, cache_keys, cache_values, slab_start):
    seq_count = lax.axis_size("seq")
    cell_count = lax.axis_size("row") * lax.axis_size("col")
    cell_index = lax.axis_index("row") * lax.axis_size("col") + lax.axis_index("col")
    heads_dev = HQ // seq_count
    group_size = HQ // KVH
    kv_dev = max(1, heads_dev // group_size)
    per_group = heads_dev // kv_dev
    tok_rows = queries.shape[0]
    first_pos = slab_start[0]
    kv_first = lax.axis_index("seq") * heads_dev // group_size
    every_pos = lax.all_gather(positions, ("seq", "row", "col"), axis=0, tiled=True)
    regrouped = lax.all_to_all(queries, "seq", split_axis=1, concat_axis=0, tiled=True)
    query_count = regrouped.shape[0]
    query_block = regrouped.reshape(query_count, kv_dev, per_group, HD)
    own_pos = (
        lax.dynamic_index_in_dim(
            every_pos.reshape(seq_count, cell_count, tok_rows), cell_index, 1, keepdims=False
        ).reshape(query_count)
        + first_pos
    )
    cache_key_head = lax.dynamic_slice_in_dim(cache_keys, kv_first * HD, kv_dev * HD, 1)
    cache_value_head = lax.dynamic_slice_in_dim(cache_values, kv_first * HD, kv_dev * HD, 1)
    carried = (
        jnp.full((query_count, kv_dev, per_group), masked_score, jnp.float32),
        jnp.zeros((query_count, kv_dev, per_group), jnp.float32),
        jnp.zeros((query_count, kv_dev, per_group, HD), jnp.float32),
    )
    grouped = (
        lax.all_gather(new_keys, ("row", "col"), axis=0, tiled=True),
        lax.all_gather(new_values, ("row", "col"), axis=0, tiled=True),
    )
    received = (
        lax.all_to_all(
            spread_heads(grouped[0], seq_count, kv_dev, HD),
            "seq",
            split_axis=1,
            concat_axis=0,
            tiled=True,
        ),
        lax.all_to_all(
            spread_heads(grouped[1], seq_count, kv_dev, HD),
            "seq",
            split_axis=1,
            concat_axis=0,
            tiled=True,
        ),
    )
    slab_keys = received[0].reshape(-1, kv_dev * HD)
    slab_values = received[1].reshape(-1, kv_dev * HD)
    carried = attend(
        carried, query_block, own_pos, slab_keys, slab_values, every_pos + first_pos, kv_dev
    )
    pieces = (
        lax.all_gather(cache_key_head, ("row", "col"), axis=0, tiled=True),
        lax.all_gather(cache_value_head, ("row", "col"), axis=0, tiled=True),
    )
    row_ids = jnp.arange(pieces[0].shape[0], dtype=jnp.int32)
    key_pos = jnp.where(row_ids < first_pos, row_ids, far_position)
    carried = attend(carried, query_block, own_pos, pieces[0], pieces[1], key_pos, kv_dev)
    running_max, running_sum, running_out = carried
    context = (
        (running_out / running_sum[..., None])
        .astype(jnp.bfloat16)
        .reshape(query_count, heads_dev * HD)
    )
    return lax.all_to_all(context, "seq", split_axis=0, concat_axis=1, tiled=True)


def solution(mesh):
    in_specs = (
        P(("seq", "row", "col"), None),
        P(("seq", "row", "col"), None),
        P(("seq", "row", "col"), None),
        P(("seq", "row", "col")),
        P(("row", "col"), None),
        P(("row", "col"), None),
        P(),
    )
    out_specs = P(("seq", "row", "col"), None)
    return jax.shard_map(
        on_device, mesh=mesh, in_specs=in_specs, out_specs=out_specs, check_vma=False
    )
```

profile of v0, /device:TPU:1, one launch (start us, length us, event | category | flops | bytes accessed | tf_op | source)
XLA Modules:
  0.0 255.7 jit_solution(11486921465186553433)
XLA Ops:
  6.5 0.0 copy-start
  6.5 0.0 all-gather.5.cloned.1.call-start
  6.5 1.0 copy-done
  7.6 0.6 constant_dynamic-slice_fusion.1
  8.2 0.0 all-gather.5.cloned.1.call-update
  8.2 0.0 copy-start.12
  8.3 10.5 %all-to-all-start.1 = ((bf16[4,32,256]{2,0,1:T(4,128)(2,1)}), bf16[4,32,256]{2,0,1:T(4,128)(2,1)S(1)}, u32[]{:S(2)}, u32[]{:S(2)}) async-start(bf16[4,32,256]{2,0,1:T(4,128)(2,1)} %bitcast.7), calls=%async_computation.1 | async-start | bytes 131072 | tf_op jit(solution)/shard_map/all_to_all | solution.py:69
  18.8 33.7 %all-gather = bf16[16,4,1024]{2,1,0:T(4,128)(2,1)S(1)} all-gather(bf16[1,4,1024]{2,1,0:T(4,128)(2,1)S(1)} %bitcast.165), channel_id=1, replica_groups=mesh['seq'=32,'row'=4,'col'=4] {'row','col'}, dimensions={0}, use_global_device_ids=true | all-gather | bytes 139264 | tf_op jit(solution)/shard_map/all_gather | solution.py:86
  52.5 0.1 reshape.574
  52.6 0.0 all-to-all-done.1
  52.6 0.9 broadcast_in_dim.118
  53.5 8.9 %all-to-all-start = ((bf16[64,32,128]{2,0,1:T(8,128)(2,1)}), bf16[64,32,128]{2,0,1:T(8,128)(2,1)S(1)}, u32[]{:S(2)}, u32[]{:S(2)}) async-start(bf16[64,32,128]{2,0,1:T(8,128)(2,1)} %bitcast.2), calls=%async_computation | async-start | bytes 1048576 | tf_op jit(solution)/shard_map/all_to_all | solution.py:90
  62.4 0.0 all-gather.7.cloned.1.call-start
  62.5 0.9 constant_dynamic-slice_fusion
  63.3 0.7 copy.73
  64.1 0.0 all-gather.7.cloned.1.call-update
  64.1 0.0 copy-start.16
  64.1 0.6 copy-done.16
  64.8 0.2 dynamic-update-slice
  64.9 99.9 %all-reduce = s32[2048]{0:T(1024)S(1)} all-reduce(s32[2048]{0:T(1024)S(1)} %dynamic-update-slice), channel_id=1, replica_groups=mesh['seq'=32,'row'=4,'col'=4] {'seq','row','col'}, use_global_device_ids=true, to_apply=%add | all-reduce | flops 2048 | bytes 16384
  164.8 0.3 reshape.573
  165.8 0.1 add_reduce_fusion
  165.8 0.0 copy-start.13
  165.8 0.1 add.111
  165.9 0.6 copy-done.13
  166.5 28.9 %all-gather.1 = bf16[16,4,1024]{2,1,0:T(4,128)(2,1)S(1)} all-gather(bf16[1,4,1024]{2,1,0:T(4,128)(2,1)S(1)} %bitcast.166), channel_id=1, replica_groups=mesh['seq'=32,'row'=4,'col'=4] {'row','col'}, dimensions={0}, use_global_device_ids=true | all-gather | bytes 139264 | tf_op jit(solution)/shard_map/all_gather | solution.py:87
  195.4 0.1 reshape.579
  195.5 0.0 all-to-all-done
  195.5 0.9 broadcast_in_dim.122
  196.4 7.4 %all-to-all-start.2 = ((bf16[64,32,128]{2,0,1:T(8,128)(2,1)}), bf16[64,32,128]{2,0,1:T(8,128)(2,1)S(1)}, u32[]{:S(2)}, u32[]{:S(2)}) async-start(bf16[64,32,128]{2,0,1:T(8,128)(2,1)} %bitcast.14), calls=%async_computation.2 | async-start | bytes 1048576 | tf_op jit(solution)/shard_map/all_to_all | solution.py:97
  203.8 2.1 broadcast_compare_fusion.5
  206.0 13.7 %all-to-all-done.2 = bf16[64,32,128]{2,0,1:T(8,128)(2,1)S(1)} async-done(((bf16[64,32,128]{2,0,1:T(8,128)(2,1)}), bf16[64,32,128]{2,0,1:T(8,128)(2,1)S(1)}, u32[]{:S(2)}, u32[]{:S(2)}) %all-to-all-start.2) | async-done | bytes 524320 | tf_op jit(solution)/shard_map/all_to_all | solution.py:97
  219.7 0.8 fusion.77
  220.6 0.3 select_reduce_fusion.5
  220.9 0.3 select_reduce_fusion.4
  221.3 0.0 all-gather.5.cloned.1.call-done
  221.3 0.0 copy-start.15
  221.3 0.0 copy-start.8
  221.3 1.4 select_reduce_fusion.1
  222.7 0.4 select_reduce_fusion.2
  223.1 0.7 copy-done.9
  223.8 0.3 select_reduce_fusion.3
  224.1 0.0 copy-start.7
  224.1 0.0 copy-start.11
  224.2 0.3 select_reduce_fusion
  224.5 0.0 copy-start.3
  224.5 0.7 copy-done.11
  225.3 1.1 convolution_bitcast_fusion.4
  226.3 0.4 fusion.20
  226.8 0.4 fusion.24
  227.2 0.0 copy-done.1
  227.2 0.4 fusion.28
  227.7 0.0 all-gather.7.cloned.1.call-done
  227.8 1.9 convolution_bitcast_fusion.3
  229.7 1.5 convolution_bitcast_fusion.2
  231.2 0.5 convolution_bitcast_fusion.1
  231.7 0.8 copy-done.4
  232.4 0.4 convolution_bitcast_fusion
  232.9 0.5 copy-done.10
  233.4 0.0 copy-done.17
  233.4 0.5 fusion.19
  233.9 0.1 copy.62
  234.1 14.1 %all_to_all.65 = bf16[32,4,256]{2,1,0:T(4,128)(2,1)S(1)} all-to-all(bf16[32,4,256]{2,1,0:T(4,128)(2,1)S(1)} %all_to_all.57), channel_id=1, replica_groups=mesh['seq'=32,'row'=4,'col'=4] {'seq'}, dimensions={0} | all-to-all | bytes 131072 | tf_op jit(solution)/shard_map/all_to_all | solution.py:123
  248.2 0.6 copy.101
  (30 shorter events, 0.3 us)
Async XLA Ops:
  6.5 1.0 copy-start
  6.5 214.7 %all-gather.5.cloned.1.call-start = ((), (), s32[]{:S(2)}) async-start(), calls=%async_computation.4 | async-start | bytes 1114112 | tf_op jit(solution)/shard_map/all_gather | solution.py:111
  8.2 10.5 %copy-start.12 = (bf16[4,1024]{1,0:T(4,128)(2,1)S(1)}, bf16[4,1024]{1,0:T(4,128)(2,1)}, u32[]{:S(2)}) copy-start(bf16[4,1024]{1,0:T(4,128)(2,1)} %param.8) | copy-start | bytes 24580
  8.3 44.3 %all-to-all-start.1 = ((bf16[4,32,256]{2,0,1:T(4,128)(2,1)}), bf16[4,32,256]{2,0,1:T(4,128)(2,1)S(1)}, u32[]{:S(2)}, u32[]{:S(2)}) async-start(bf16[4,32,256]{2,0,1:T(4,128)(2,1)} %bitcast.7), calls=%async_computation.1 | async-start | bytes 131072 | tf_op jit(solution)/shard_map/all_to_all | solution.py:69
  53.5 142.0 %all-to-all-start = ((bf16[64,32,128]{2,0,1:T(8,128)(2,1)}), bf16[64,32,128]{2,0,1:T(8,128)(2,1)S(1)}, u32[]{:S(2)}, u32[]{:S(2)}) async-start(bf16[64,32,128]{2,0,1:T(8,128)(2,1)} %bitcast.2), calls=%async_computation | async-start | bytes 1048576 | tf_op jit(solution)/shard_map/all_to_all | solution.py:90
  62.4 165.3 %all-gather.7.cloned.1.call-start = ((), (), s32[]{:S(2)}) async-start(), calls=%async_computation.5 | async-start | bytes 1114112 | tf_op jit(solution)/shard_map/all_gather | solution.py:112
  64.1 0.7 copy-start.16
  165.8 0.7 copy-start.13
  196.4 23.3 %all-to-all-start.2 = ((bf16[64,32,128]{2,0,1:T(8,128)(2,1)}), bf16[64,32,128]{2,0,1:T(8,128)(2,1)S(1)}, u32[]{:S(2)}, u32[]{:S(2)}) async-start(bf16[64,32,128]{2,0,1:T(8,128)(2,1)} %bitcast.14), calls=%async_computation.2 | async-start | bytes 1048576 | tf_op jit(solution)/shard_map/all_to_all | solution.py:97
  221.3 1.4 copy-start.15
  221.3 1.4 copy-start.8
  222.7 4.5 %copy-start.1 = (f32[128,1,2,1024]{0,3,2,1:T(8,128)}, f32[128,1,2,1024]{0,3,2,1:T(8,128)S(1)}, u32[]{:S(2)}) copy-start(f32[128,1,2,1024]{0,3,2,1:T(8,128)S(1)} %get-tuple-element.37) | copy-start | bytes 3145732
  222.7 1.1 copy-start.9
  223.1 3.7 %copy-start.5 = (f32[128,1,2,1024]{0,3,2,1:T(8,128)}, f32[128,1,2,1024]{0,3,2,1:T(8,128)S(1)}, u32[]{:S(2)}) copy-start(f32[128,1,2,1024]{0,3,2,1:T(8,128)S(1)} %get-tuple-element.39) | copy-start | bytes 3145732
  224.1 2.6 %copy-start.7 = (f32[128,1,2,1024]{0,3,2,1:T(8,128)}, f32[128,1,2,1024]{0,3,2,1:T(8,128)S(1)}, u32[]{:S(2)}) copy-start(f32[128,1,2,1024]{0,3,2,1:T(8,128)S(1)} %get-tuple-element.41) | copy-start | bytes 3145732
  224.1 1.1 copy-start.11
  224.5 2.7 %copy-start.3 = (f32[128,1,2,1024]{0,3,2,1:T(8,128)}, f32[128,1,2,1024]{0,3,2,1:T(8,128)S(1)}, u32[]{:S(2)}) copy-start(f32[128,1,2,1024]{0,3,2,1:T(8,128)S(1)} %get-tuple-element.35) | copy-start | bytes 3145732
  227.7 2.0 copy-start.6
  227.8 3.4 %copy-start.14 = (bf16[4096,128]{0,1:T(8,128)(2,1)S(1)}, bf16[4096,128]{0,1:T(8,128)(2,1)}, u32[]{:S(2)}) copy-start(bf16[4096,128]{0,1:T(8,128)(2,1)} %all-gather.7.cloned.1.call-done) | copy-start | bytes 3145732
  229.7 1.5 copy-start.2
  231.2 1.2 copy-start.4
  232.4 0.9 copy-start.10
  232.4 1.0 copy-start.17
Sparse Core Ops, SparseCore 0:
  9.4 71.4 all-gather.4
  82.9 63.6 all-gather.6
where the time goes:
time: 256 us
  blocking collectives  177 us (69%)
  starting transfers between devices  26.8 us (10%)
  between operations  14.5 us (6%)
  waiting for transfers between devices  13.8 us (5%)
  local copies, waits for them, and re-layouts  11.4 us (4%)
  matrix products  8.99 us (4%)
  other arithmetic  3.52 us (1%)
    unnamed x1, blocking collectives  99.9 us
    all_gather x1, blocking collectives, on_device(): lax.all_gather(new_keys, ('row', 'col'), axis=0, tiled=True)  33.7 us
    all_gather x1, blocking collectives, on_device(): lax.all_gather(new_values, ('row', 'col'), axis=0, tiled=True)  28.9 us
    all_to_all x1, blocking collectives, on_device(): lax.all_to_all(context, 'seq', split_axis=0, concat_axis=1, tiled=True)  14.1 us
    all_to_all x1, waiting for transfers between devices, on_device(): lax.all_to_all(spread_heads(grouped[1], seq_count, kv_dev, HD), 'seq', sp...  13.7 us
    all_to_all x1, starting transfers between devices, on_device(): lax.all_to_all(queries, 'seq', split_axis=1, concat_axis=0, tiled=True)  10.5 us
    all_to_all x1, starting transfers between devices, on_device(): lax.all_to_all(spread_heads(grouped[0], seq_count, kv_dev, HD), 'seq', sp...  8.93 us
    all_to_all x1, starting transfers between devices, on_device(): lax.all_to_all(spread_heads(grouped[1], seq_count, kv_dev, HD), 'seq', sp...  7.36 us
  transfers between devices with their start and end apart: 5, of which 1 were waited for; matrix products, arithmetic and copies ran while one was open for 5% of the time, Pallas kernels for 0%

commit v1 on v0

v1 whole, which is shorter than its diff:
```python
import math

import numpy as np
import jax
import jax.numpy as jnp
from jax import lax
from jax.sharding import PartitionSpec as P

HQ = 64
KVH = 8
HD = 128

far_position = 1073741824
code_base = 256


def gather_cells(block, cell_axes, cell_count):
    spread = jnp.broadcast_to(block[None], (cell_count,) + block.shape)
    return lax.all_to_all(spread, cell_axes, 0, 0, tiled=True)


def on_device(queries, new_keys, new_values, positions, cache_keys, cache_values, slab_start):
    seq_count = lax.axis_size("seq")
    cell_axes = ("row", "col")
    cell_count = lax.axis_size("row") * lax.axis_size("col")
    heads_dev = HQ // seq_count
    group_size = HQ // KVH
    tok_rows = queries.shape[0]
    first_pos = slab_start[0]

    kv_of_peer = np.arange(seq_count) * heads_dev // group_size
    kv_first = lax.axis_index("seq") * heads_dev // group_size

    q_part = queries.reshape(tok_rows, seq_count, heads_dev * HD).transpose(1, 0, 2)
    k_part = jnp.take(new_keys.reshape(tok_rows, KVH, HD), kv_of_peer, axis=1).transpose(1, 0, 2)
    v_part = jnp.take(new_values.reshape(tok_rows, KVH, HD), kv_of_peer, axis=1).transpose(1, 0, 2)
    codes = jnp.stack([positions // code_base, positions % code_base], axis=1).astype(jnp.bfloat16)
    codes = jnp.pad(codes.reshape(1, tok_rows * 2), ((0, 0), (0, 128 - tok_rows * 2)))
    send = jnp.concatenate(
        [
            q_part.reshape(seq_count, -1),
            k_part.reshape(seq_count, -1),
            v_part.reshape(seq_count, -1),
            jnp.broadcast_to(codes, (seq_count, 128)),
        ],
        axis=1,
    )
    recv = lax.all_to_all(send, "seq", 0, 0, tiled=True)
    q_len = tok_rows * heads_dev * HD
    kv_len = tok_rows * HD
    query_block = recv[:, :q_len].reshape(seq_count * tok_rows, heads_dev, HD)
    slab_k = recv[:, q_len : q_len + kv_len].reshape(seq_count * tok_rows, HD)
    slab_v = recv[:, q_len + kv_len : q_len + 2 * kv_len].reshape(seq_count * tok_rows, HD)
    got_codes = recv[:, q_len + 2 * kv_len : q_len + 2 * kv_len + tok_rows * 2]
    got_codes = got_codes.reshape(seq_count * tok_rows, 2).astype(jnp.float32)
    own_pos = got_codes[:, 0] * code_base + got_codes[:, 1]

    code_row = jnp.pad(got_codes.T.reshape(1, -1).astype(jnp.bfloat16), ((0, 0), (0, 2 * HD - 2 * seq_count * tok_rows)))
    slab_block = jnp.concatenate([jnp.concatenate([slab_k, slab_v], axis=1), code_row], axis=0)
    slab_all = gather_cells(slab_block, cell_axes, cell_count)
    slab_rows = seq_count * tok_rows
    keys_new = slab_all[:, :slab_rows, :HD].reshape(-1, HD)
    values_new = slab_all[:, :slab_rows, HD:].reshape(-1, HD)
    key_codes = slab_all[:, slab_rows, : 2 * slab_rows].reshape(cell_count, 2, slab_rows).astype(jnp.float32)
    key_pos_new = (key_codes[:, 0] * code_base + key_codes[:, 1]).reshape(-1)

    cache_block = jnp.concatenate(
        [
            lax.dynamic_slice_in_dim(cache_keys, kv_first * HD, HD, 1),
            lax.dynamic_slice_in_dim(cache_values, kv_first * HD, HD, 1),
        ],
        axis=1,
    )
    cache_all = gather_cells(cache_block, cell_axes, cell_count).reshape(-1, 2 * HD)
    keys = jnp.concatenate([cache_all[:, :HD], keys_new], axis=0)
    values = jnp.concatenate([cache_all[:, HD:], values_new], axis=0)

    cache_rows = cache_all.shape[0]
    row_ids = jnp.arange(cache_rows, dtype=jnp.int32)
    cache_ok = jnp.broadcast_to((row_ids < first_pos)[None, :], (own_pos.shape[0], cache_rows))
    slab_ok = key_pos_new[None, :] <= own_pos[:, None]
    allowed = jnp.concatenate([cache_ok, slab_ok], axis=1)[:, None, :]

    score_scale = 1.0 / math.sqrt(HD)
    scores = jnp.einsum("thd,nd->thn", query_block, keys, preferred_element_type=jnp.float32) * score_scale
    row_max = jnp.max(jnp.where(allowed, scores, -jnp.inf), axis=-1, keepdims=True)
    exponent = jnp.where(allowed, jnp.exp(scores - row_max), 0.0)
    denominator = jnp.sum(exponent, axis=-1, keepdims=True)
    summed = jnp.einsum(
        "thn,nd->thd", exponent.astype(jnp.bfloat16), values, preferred_element_type=jnp.float32
    )
    context = (summed / denominator).astype(jnp.bfloat16).reshape(slab_rows, heads_dev * HD)
    return lax.all_to_all(context, "seq", split_axis=0, concat_axis=1, tiled=True)


def solution(mesh):
    in_specs = (
        P(("seq", "row", "col"), None),
        P(("seq", "row", "col"), None),
        P(("seq", "row", "col"), None),
        P(("seq", "row", "col")),
        P(("row", "col"), None),
        P(("row", "col"), None),
        P(),
    )
    out_specs = P(("seq", "row", "col"), None)
    return jax.shard_map(
        on_device, mesh=mesh, in_specs=in_specs, out_specs=out_specs, check_vma=False
    )
```

time: 256 us -> 141 us (0.55)
  the two profiles are of different devices: /device:TPU:1 before, /device:TPU:8 now
where the time goes in v1:
time: 141 us; the launch traced here: 140 us
  waiting for transfers between devices  73.6 us (52%)
  blocking collectives  33.2 us (24%)
  starting transfers between devices  15 us (11%)
  local copies, waits for them, and re-layouts  9.83 us (7%)
  other arithmetic  5.79 us (4%)
  matrix products  1.96 us (1%)
    all_to_all x2, waiting for transfers between devices, gather_cells(): return lax.all_to_all(spread, cell_axes, 0, 0, tiled=True)  73.6 us
    all_to_all x1, blocking collectives, on_device(): recv = lax.all_to_all(send, 'seq', 0, 0, tiled=True)  20 us
    all_to_all x2, starting transfers between devices, gather_cells(): return lax.all_to_all(spread, cell_axes, 0, 0, tiled=True)  15 us
    all_to_all x1, blocking collectives, on_device(): lax.all_to_all(context, 'seq', split_axis=0, concat_axis=1, tiled=True)  13.3 us
    sub x1, other arithmetic, on_device(): exponent = jnp.where(allowed, jnp.exp(scores - row_max), 0.0)  2.91 us
  transfers between devices with their start and end apart: 2, of which 2 were waited for; matrix products, arithmetic and copies ran while one was open for 2% of the time, Pallas kernels for 0%

profile of v1, /device:TPU:8, one launch (start us, length us, event | category | flops | bytes accessed | tf_op | source)
XLA Modules:
  0.0 140.4 jit_solution(8116870698488704699)
XLA Ops:
  0.0 0.0 copy-start
  0.0 0.7 convert_bitcast_fusion
  0.7 0.1 copy.26
  0.8 0.1 convert_element_type.46
  0.9 0.7 pad_clamp_fusion
  1.6 0.0 copy-done
  1.6 0.6 gather_fusion.1
  2.2 1.3 gather_fusion
  3.5 0.8 copy.32
  4.4 0.5 broadcast.65
  4.9 0.7 reduce.2
  5.6 0.2 reshape.139
  5.8 20.0 %all_to_all.41 = bf16[32,2,1088]{2,1,0:T(2,128)(2,1)S(1)} all-to-all(bf16[32,2,1088]{2,1,0:T(2,128)(2,1)S(1)} %reshape.139), channel_id=1, replica_groups=mesh['seq'=32,'row'=4,'col'=4] {'seq'}, dimensions={0} | all-to-all | bytes 278528 | tf_op jit(solution)/shard_map/all_to_all | solution.py:48
  25.8 0.1 reshape.140
  26.0 0.1 convert_element_type.47
  26.1 0.1 copy.28
  26.2 0.1 reshape.107
  26.3 1.1 broadcast_in_dim.59
  27.3 10.4 %all-to-all-start.1 = ((bf16[16,129,256]{2,1,0:T(8,128)(2,1)}), bf16[16,129,256]{2,1,0:T(8,128)(2,1)S(1)}, u32[]{:S(2)}, u32[]{:S(2)}) async-start(bf16[16,129,256]{2,1,0:T(8,128)(2,1)} %broadcast_in_dim.59), calls=%async_computation.1 | async-start | bytes 2228224 | tf_op jit(solution)/shard_map/all_to_all | solution.py:19
  37.8 0.9 constant_dynamic-slice_fusion
  38.7 27.3 %all-to-all-done.1 = bf16[16,129,256]{2,1,0:T(8,128)(2,1)S(1)} async-done(((bf16[16,129,256]{2,1,0:T(8,128)(2,1)}), bf16[16,129,256]{2,1,0:T(8,128)(2,1)S(1)}, u32[]{:S(2)}, u32[]{:S(2)}) %all-to-all-start.1) | async-done | bytes 1056800 | tf_op jit(solution)/shard_map/all_to_all | solution.py:19
  66.0 1.5 %broadcast_in_dim.61 = bf16[16,256,256]{2,1,0:T(8,128)(2,1)} broadcast(bf16[256,256]{1,0:T(8,128)(2,1)S(1)} %pad_maximum_fusion), dimensions={1,2} | broadcast | bytes 2228224 | tf_op jit(solution)/shard_map/broadcast_in_dim | solution.py:18
  67.5 4.6 %all-to-all-start.2 = ((bf16[16,256,256]{2,1,0:T(8,128)(2,1)}), bf16[16,256,256]{2,1,0:T(8,128)(2,1)S(1)}, u32[]{:S(2)}, u32[]{:S(2)}) async-start(bf16[16,256,256]{2,1,0:T(8,128)(2,1)} %broadcast_in_dim.61), calls=%async_computation.2 | async-start | bytes 4194304 | tf_op jit(solution)/shard_map/all_to_all | solution.py:19
  72.9 0.2 fusion.23
  73.1 1.3 fusion.31
  74.4 0.0 copy-start.1
  74.4 0.2 broadcast_compare_fusion
  74.7 0.4 pad_add_fusion
  75.0 46.3 %all-to-all-done.2 = bf16[16,256,256]{2,1,0:T(8,128)(2,1)S(1)} async-done(((bf16[16,256,256]{2,1,0:T(8,128)(2,1)}), bf16[16,256,256]{2,1,0:T(8,128)(2,1)S(1)}, u32[]{:S(2)}, u32[]{:S(2)}) %all-to-all-start.2) | async-done | bytes 2097184 | tf_op jit(solution)/shard_map/all_to_all | solution.py:19
  121.4 0.1 fusion.30
  121.5 0.0 copy-done.1
  121.5 1.0 convolution_multiply_fusion
  122.5 0.0 copy-start.2
  122.5 2.9 %fusion.33 = (f32[128,2]{0,1:T(2,128)S(1)}, bf16[128,2,6144]{2,0,1:T(8,128)(2,1)S(1)}) fusion(f32[128,2,6144]{2,0,1:T(8,128)S(1)} %convolution_multiply_fusion, pred[128,6144]{1,0:T(8,128)(4,1)S(1)} %pad_add_fusion), kind=kOutput, calls=%fused_computation.57 | output fusion | flops 7870463 | bytes 10224640 | tf_op jit(solution)/shard_map/sub | solution.py:87
  125.4 0.0 copy-done.2
  125.4 1.0 fusion.20
  126.4 0.1 copy.30
  126.5 13.3 %all_to_all.42 = bf16[32,4,256]{2,1,0:T(4,128)(2,1)S(1)} all-to-all(bf16[32,4,256]{2,1,0:T(4,128)(2,1)S(1)} %all_to_all.33), channel_id=1, replica_groups=mesh['seq'=32,'row'=4,'col'=4] {'seq'}, dimensions={0} | all-to-all | bytes 131072 | tf_op jit(solution)/shard_map/all_to_all | solution.py:93
  139.8 0.6 copy.47
  (20 shorter events, 0.3 us)
Async XLA Ops:
  0.0 1.6 %copy-start = (bf16[4,1024]{1,0:T(4,128)(2,1)S(1)}, bf16[4,1024]{1,0:T(4,128)(2,1)}, u32[]{:S(2)}) copy-start(bf16[4,1024]{1,0:T(4,128)(2,1)} %param.12) | copy-start | bytes 24580
  27.3 38.7 %all-to-all-start.1 = ((bf16[16,129,256]{2,1,0:T(8,128)(2,1)}), bf16[16,129,256]{2,1,0:T(8,128)(2,1)S(1)}, u32[]{:S(2)}, u32[]{:S(2)}) async-start(bf16[16,129,256]{2,1,0:T(8,128)(2,1)} %broadcast_in_dim.59), calls=%async_computation.1 | async-start | bytes 2228224 | tf_op jit(solution)/shard_map/all_to_all | solution.py:19
  67.5 53.8 %all-to-all-start.2 = ((bf16[16,256,256]{2,1,0:T(8,128)(2,1)}), bf16[16,256,256]{2,1,0:T(8,128)(2,1)S(1)}, u32[]{:S(2)}, u32[]{:S(2)}) async-start(bf16[16,256,256]{2,1,0:T(8,128)(2,1)} %broadcast_in_dim.61), calls=%async_computation.2 | async-start | bytes 4194304 | tf_op jit(solution)/shard_map/all_to_all | solution.py:19
  74.4 47.1 %copy-start.1 = (bf16[16,128,128]{2,1,0:T(8,128)(2,1)S(1)}, bf16[16,128,128]{2,1,0:T(8,128)(2,1)}, u32[]{:S(2)}) copy-start(bf16[16,128,128]{2,1,0:T(8,128)(2,1)} %get-tuple-element.8) | copy-start | bytes 1572868
  122.5 2.9 %copy-start.2 = (bf16[16,128,128]{2,1,0:T(8,128)(2,1)S(1)}, bf16[16,128,128]{2,1,0:T(8,128)(2,1)}, u32[]{:S(2)}) copy-start(bf16[16,128,128]{2,1,0:T(8,128)(2,1)} %get-tuple-element.9) | copy-start | bytes 1572868

commit v2 on v1

--- a/solution.py
+++ b/solution.py
@@ -19,6 +19,16 @@
     return lax.all_to_all(spread, cell_axes, 0, 0, tiled=True)
 
 
+def pick_heads(rows, kv_of_peer, tok_rows):
+    split = rows.reshape(tok_rows, KVH, 1, HD)
+    repeat = kv_of_peer.shape[0] // KVH
+    if repeat * KVH == kv_of_peer.shape[0] and np.array_equal(kv_of_peer, np.arange(kv_of_peer.shape[0]) // repeat):
+        spread = jnp.broadcast_to(split, (tok_rows, KVH, repeat, HD)).reshape(tok_rows, -1, HD)
+    else:
+        spread = jnp.take(split[:, :, 0], kv_of_peer, axis=1)
+    return spread.transpose(1, 0, 2)
+
+
 def on_device(queries, new_keys, new_values, positions, cache_keys, cache_values, slab_start):
     seq_count = lax.axis_size("seq")
     cell_axes = ("row", "col")
@@ -32,8 +42,8 @@
     kv_first = lax.axis_index("seq") * heads_dev // group_size
 
     q_part = queries.reshape(tok_rows, seq_count, heads_dev * HD).transpose(1, 0, 2)
-    k_part = jnp.take(new_keys.reshape(tok_rows, KVH, HD), kv_of_peer, axis=1).transpose(1, 0, 2)
-    v_part = jnp.take(new_values.reshape(tok_rows, KVH, HD), kv_of_peer, axis=1).transpose(1, 0, 2)
+    k_part = pick_heads(new_keys, kv_of_peer, tok_rows)
+    v_part = pick_heads(new_values, kv_of_peer, tok_rows)
     codes = jnp.stack([positions // code_base, positions % code_base], axis=1).astype(jnp.bfloat16)
     codes = jnp.pad(codes.reshape(1, tok_rows * 2), ((0, 0), (0, 128 - tok_rows * 2)))
     send = jnp.concatenate(
@@ -56,14 +66,6 @@
     own_pos = got_codes[:, 0] * code_base + got_codes[:, 1]
 
     code_row = jnp.pad(got_codes.T.reshape(1, -1).astype(jnp.bfloat16), ((0, 0), (0, 2 * HD - 2 * seq_count * tok_rows)))
-    slab_block = jnp.concatenate([jnp.concatenate([slab_k, slab_v], axis=1), code_row], axis=0)
-    slab_all = gather_cells(slab_block, cell_axes, cell_count)
-    slab_rows = seq_count * tok_rows
-    keys_new = slab_all[:, :slab_rows, :HD].reshape(-1, HD)
-    values_new = slab_all[:, :slab_rows, HD:].reshape(-1, HD)
-    key_codes = slab_all[:, slab_rows, : 2 * slab_rows].reshape(cell_count, 2, slab_rows).astype(jnp.float32)
-    key_pos_new = (key_codes[:, 0] * code_base + key_codes[:, 1]).reshape(-1)
-
     cache_block = jnp.concatenate(
         [
             lax.dynamic_slice_in_dim(cache_keys, kv_first * HD, HD, 1),
@@ -71,7 +73,15 @@
         ],
         axis=1,
     )
-    cache_all = gather_cells(cache_block, cell_axes, cell_count).reshape(-1, 2 * HD)
+    cache_len = cache_block.shape[0]
+    slab_rows = seq_count * tok_rows
+    block = jnp.concatenate([cache_block, jnp.concatenate([slab_k, slab_v], axis=1), code_row], axis=0)
+    every = gather_cells(block, cell_axes, cell_count)
+    cache_all = every[:, :cache_len].reshape(-1, 2 * HD)
+    keys_new = every[:, cache_len : cache_len + slab_rows, :HD].reshape(-1, HD)
+    values_new = every[:, cache_len : cache_len + slab_rows, HD:].reshape(-1, HD)
+    key_codes = every[:, cache_len + slab_rows, : 2 * slab_rows].reshape(cell_count, 2, slab_rows).astype(jnp.float32)
+    key_pos_new = (key_codes[:, 0] * code_base + key_codes[:, 1]).reshape(-1)
     keys = jnp.concatenate([cache_all[:, :HD], keys_new], axis=0)
     values = jnp.concatenate([cache_all[:, HD:], values_new], axis=0)
 

time: 141 us -> 132 us (0.936)
  blocking collectives: 33.2 us -> 13.3 us
  waiting for transfers between devices: 73.6 us -> 81.3 us
  starting transfers between devices: 15 us -> 20.6 us
    all_to_all x1 -> x0, blocking collectives: 20 us -> none  [on_device(): recv = lax.all_to_all(send, 'seq', 0, 0, tiled=True)]
    all_to_all x0 -> x1, starting transfers between devices: none -> 10.2 us  [on_device(): recv = lax.all_to_all(send, 'seq', 0, 0, tiled=True)]
    all_to_all x0 -> x1, waiting for transfers between devices: none -> 9.12 us  [on_device(): recv = lax.all_to_all(send, 'seq', 0, 0, tiled=True)]
    all_to_all x2 -> x1, starting transfers between devices: 15 us -> 10.4 us  [gather_cells(): return lax.all_to_all(spread, cell_axes, 0, 0, tiled=True)]
    gather x2 -> x0, local copies, waits for them, and re-layouts: 1.91 us -> none  [the longest x1 1.31 us: on_device(): jnp.take(new_keys.reshape(tok_rows, KVH, HD), kv_of_peer, axis=1)]
    all_to_all x2 -> x1, waiting for transfers between devices: 73.6 us -> 72.1 us  [gather_cells(): return lax.all_to_all(spread, cell_axes, 0, 0, tiled=True)]
    broadcast_in_dim x0 -> x2, local copies, waits for them, and re-layouts: none -> 1.42 us  [pick_heads(): jnp.broadcast_to(split, (tok_rows, KVH, repeat, HD))]
  transfers between devices with their start and end apart: 2 -> 2, of which waited for: 2 -> 2; matrix products, arithmetic and copies ran while one was open for 2% -> 1% of each run, Pallas kernels for 0% -> 0%
where the time goes in v2:
time: 132 us
  waiting for transfers between devices  81.3 us (62%)
  starting transfers between devices  20.6 us (16%)
  blocking collectives  13.3 us (10%)
  local copies, waits for them, and re-layouts  8.45 us (6%)
  other arithmetic  5.22 us (4%)
  matrix products  1.96 us (1%)
    all_to_all x1, waiting for transfers between devices, gather_cells(): return lax.all_to_all(spread, cell_axes, 0, 0, tiled=True)  72.1 us
    all_to_all x1, blocking collectives, on_device(): lax.all_to_all(context, 'seq', split_axis=0, concat_axis=1, tiled=True)  13.3 us
    all_to_all x1, starting transfers between devices, gather_cells(): return lax.all_to_all(spread, cell_axes, 0, 0, tiled=True)  10.4 us
    all_to_all x1, starting transfers between devices, on_device(): recv = lax.all_to_all(send, 'seq', 0, 0, tiled=True)  10.2 us
    all_to_all x1, waiting for transfers between devices, on_device(): recv = lax.all_to_all(send, 'seq', 0, 0, tiled=True)  9.12 us
    sub x1, other arithmetic, on_device(): exponent = jnp.where(allowed, jnp.exp(scores - row_max), 0.0)  3.02 us
  transfers between devices with their start and end apart: 2, of which 2 were waited for; matrix products, arithmetic and copies ran while one was open for 1% of the time, Pallas kernels for 0%

profile of v2, /device:TPU:8, one launch (start us, length us, event | category | flops | bytes accessed | tf_op | source)
XLA Modules:
  0.0 131.6 jit_solution(13612334375966096757)
XLA Ops:
  0.0 0.7 convert_bitcast_fusion
  0.7 0.1 copy.35
  0.8 0.1 convert_element_type.46
  0.9 0.8 copy.41
  1.8 0.7 broadcast_in_dim.57
  2.5 0.7 broadcast_in_dim.59
  3.2 0.5 broadcast.51
  3.8 0.7 reduce.2
  4.4 0.8 reshape.117
  5.3 10.2 %all-to-all-start = ((bf16[32,2,1088]{2,1,0:T(2,128)(2,1)}), bf16[32,2,1088]{2,1,0:T(2,128)(2,1)S(1)}, u32[]{:S(2)}, u32[]{:S(2)}) async-start(bf16[32,2,1088]{2,1,0:T(2,128)(2,1)} %reshape.117), calls=%async_computation | async-start | bytes 294912 | tf_op jit(solution)/shard_map/all_to_all | solution.py:58
  15.5 0.9 constant_dynamic-slice_fusion
  16.4 9.1 %all-to-all-done = bf16[32,2,1088]{2,1,0:T(2,128)(2,1)S(1)} async-done(((bf16[32,2,1088]{2,1,0:T(2,128)(2,1)}), bf16[32,2,1088]{2,1,0:T(2,128)(2,1)S(1)}, u32[]{:S(2)}, u32[]{:S(2)}) %all-to-all-start) | async-done | bytes 139296 | tf_op jit(solution)/shard_map/all_to_all | solution.py:58
  25.5 0.1 reshape.118
  25.7 0.1 convert_element_type.47
  25.8 0.1 copy.37
  25.8 0.1 reshape.105
  26.0 1.9 %broadcast_in_dim.62 = bf16[16,385,256]{2,1,0:T(8,128)(2,1)} broadcast(bf16[385,256]{1,0:T(8,128)(2,1)S(1)} %pad_maximum_fusion), dimensions={1,2} | broadcast | bytes 3351040 | tf_op jit(solution)/shard_map/broadcast_in_dim | solution.py:18
  27.9 10.4 %all-to-all-start.1 = ((bf16[16,385,256]{2,1,0:T(8,128)(2,1)}), bf16[16,385,256]{2,1,0:T(8,128)(2,1)S(1)}, u32[]{:S(2)}, u32[]{:S(2)}) async-start(bf16[16,385,256]{2,1,0:T(8,128)(2,1)} %broadcast_in_dim.62), calls=%async_computation.1 | async-start | bytes 6422528 | tf_op jit(solution)/shard_map/all_to_all | solution.py:19
  39.0 0.2 fusion.23
  39.2 72.1 %all-to-all-done.1 = bf16[16,385,256]{2,1,0:T(8,128)(2,1)S(1)} async-done(((bf16[16,385,256]{2,1,0:T(8,128)(2,1)}), bf16[16,385,256]{2,1,0:T(8,128)(2,1)S(1)}, u32[]{:S(2)}, u32[]{:S(2)}) %all-to-all-start.1) | async-done | bytes 3153952 | tf_op jit(solution)/shard_map/all_to_all | solution.py:19
  111.4 0.2 slice.65
  111.6 0.1 fusion.31
  111.8 0.2 broadcast_compare_fusion
  112.0 0.4 pad_add_fusion
  112.3 0.3 fusion.30
  112.6 1.0 convolution_multiply_fusion
  113.6 3.0 %fusion.33 = (f32[128,2]{0,1:T(2,128)S(1)}, bf16[128,2,6144]{2,0,1:T(8,128)(2,1)S(1)}) fusion(f32[128,2,6144]{2,0,1:T(8,128)S(1)} %convolution_multiply_fusion, pred[128,6144]{1,0:T(8,128)(4,1)S(1)} %pad_add_fusion), kind=kOutput, calls=%fused_computation.53 | output fusion | flops 7870463 | bytes 10224640 | tf_op jit(solution)/shard_map/sub | solution.py:97
  116.6 1.0 fusion.20
  117.6 0.1 copy.39
  117.7 13.3 %all_to_all.36 = bf16[32,4,256]{2,1,0:T(4,128)(2,1)S(1)} all-to-all(bf16[32,4,256]{2,1,0:T(4,128)(2,1)S(1)} %all_to_all.29), channel_id=1, replica_groups=mesh['seq'=32,'row'=4,'col'=4] {'seq'}, dimensions={0} | all-to-all | bytes 131072 | tf_op jit(solution)/shard_map/all_to_all | solution.py:103
  131.0 0.6 copy.56
  (19 shorter events, 0.3 us)
Async XLA Ops:
  5.3 20.2 %all-to-all-start = ((bf16[32,2,1088]{2,1,0:T(2,128)(2,1)}), bf16[32,2,1088]{2,1,0:T(2,128)(2,1)S(1)}, u32[]{:S(2)}, u32[]{:S(2)}) async-start(bf16[32,2,1088]{2,1,0:T(2,128)(2,1)} %reshape.117), calls=%async_computation | async-start | bytes 294912 | tf_op jit(solution)/shard_map/all_to_all | solution.py:58
  27.9 83.5 %all-to-all-start.1 = ((bf16[16,385,256]{2,1,0:T(8,128)(2,1)}), bf16[16,385,256]{2,1,0:T(8,128)(2,1)S(1)}, u32[]{:S(2)}, u32[]{:S(2)}) async-start(bf16[16,385,256]{2,1,0:T(8,128)(2,1)} %broadcast_in_dim.62), calls=%async_computation.1 | async-start | bytes 6422528 | tf_op jit(solution)/shard_map/all_to_all | solution.py:19

commit v3 on v2

v3 whole, which is shorter than its diff:
```python
import math

import numpy as np
import jax
import jax.numpy as jnp
from jax import lax
from jax.sharding import PartitionSpec as P

HQ = 64
KVH = 8
HD = 128

far_position = 1073741824
code_base = 256


def gather_cells(block, cell_axes, cell_count):
    spread = jnp.broadcast_to(block[None], (cell_count,) + block.shape)
    return lax.all_to_all(spread, cell_axes, 0, 0, tiled=True)


def pick_heads(rows, kv_of_peer, tok_rows, width=HD):
    split = rows.reshape(tok_rows, KVH, 1, width)
    repeat = kv_of_peer.shape[0] // KVH
    if repeat * KVH == kv_of_peer.shape[0] and np.array_equal(kv_of_peer, np.arange(kv_of_peer.shape[0]) // repeat):
        spread = jnp.broadcast_to(split, (tok_rows, KVH, repeat, width)).reshape(tok_rows, -1, width)
    else:
        spread = jnp.take(split[:, :, 0], kv_of_peer, axis=1)
    return spread.transpose(1, 0, 2)


def on_device(queries, new_keys, new_values, positions, cache_keys, cache_values, slab_start):
    seq_count = lax.axis_size("seq")
    cell_axes = ("row", "col")
    cell_count = lax.axis_size("row") * lax.axis_size("col")
    cell_index = lax.axis_index("row") * lax.axis_size("col") + lax.axis_index("col")
    heads_dev = HQ // seq_count
    group_size = HQ // KVH
    tok_rows = queries.shape[0]
    first_pos = slab_start[0]
    kv_of_peer = np.arange(seq_count) * heads_dev // group_size
    kv_first = lax.axis_index("seq") * heads_dev // group_size
    width = 2 * HD

    cache_block = jnp.concatenate(
        [
            lax.dynamic_slice_in_dim(cache_keys, kv_first * HD, HD, 1),
            lax.dynamic_slice_in_dim(cache_values, kv_first * HD, HD, 1),
        ],
        axis=1,
    )
    cache_len = cache_block.shape[0]
    local_kv = jnp.concatenate([new_keys, new_values], axis=1).reshape(-1, width)
    kv_len = local_kv.shape[0]
    codes = jnp.stack([positions // code_base, positions % code_base], axis=1).astype(jnp.bfloat16)
    code_row = jnp.pad(codes.reshape(1, tok_rows * 2), ((0, 0), (0, width - tok_rows * 2)))
    block = jnp.concatenate([cache_block, local_kv, code_row], axis=0)
    every = gather_cells(block, cell_axes, cell_count)
    cache_all = every[:, :cache_len].reshape(-1, width)
    slice_rows = cell_count * tok_rows
    slice_kv = every[:, cache_len : cache_len + kv_len].reshape(slice_rows, 2, KVH, HD)
    slice_codes = every[:, cache_len + kv_len, : tok_rows * 2].reshape(1, slice_rows * 2)

    q_part = queries.reshape(tok_rows, seq_count, heads_dev * HD).transpose(1, 0, 2).reshape(seq_count, -1)
    kv_part = pick_heads(slice_kv.transpose(0, 2, 1, 3).reshape(slice_rows, KVH * width), kv_of_peer, slice_rows, width)
    send = jnp.concatenate(
        [q_part, kv_part.reshape(seq_count, -1), jnp.broadcast_to(slice_codes, (seq_count, slice_rows * 2))],
        axis=1,
    )
    recv = lax.all_to_all(send, "seq", 0, 0, tiled=True)
    q_len = q_part.shape[1]
    kvp_len = slice_rows * width
    query_block = recv[:, :q_len].reshape(seq_count * tok_rows, heads_dev, HD)
    slab_kv = recv[:, q_len : q_len + kvp_len].reshape(seq_count * slice_rows, width)
    key_codes = recv[:, q_len + kvp_len :].reshape(seq_count, cell_count, tok_rows, 2).astype(jnp.float32)
    key_pos_new = (key_codes[..., 0] * code_base + key_codes[..., 1]).reshape(-1)
    own_codes = lax.dynamic_index_in_dim(key_codes, cell_index, 1, keepdims=False).reshape(-1, 2)
    own_pos = own_codes[:, 0] * code_base + own_codes[:, 1]

    keys = jnp.concatenate([cache_all[:, :HD], slab_kv[:, :HD]], axis=0)
    values = jnp.concatenate([cache_all[:, HD:], slab_kv[:, HD:]], axis=0)

    cache_rows = cache_all.shape[0]
    row_ids = jnp.arange(cache_rows, dtype=jnp.int32)
    cache_ok = jnp.broadcast_to((row_ids < first_pos)[None, :], (own_pos.shape[0], cache_rows))
    slab_ok = key_pos_new[None, :] <= own_pos[:, None]
    allowed = jnp.concatenate([cache_ok, slab_ok], axis=1)[:, None, :]

    score_scale = 1.0 / math.sqrt(HD)
    scores = jnp.einsum("thd,nd->thn", query_block, keys, preferred_element_type=jnp.float32) * score_scale
    row_max = jnp.max(jnp.where(allowed, scores, -jnp.inf), axis=-1, keepdims=True)
    exponent = jnp.where(allowed, jnp.exp(scores - row_max), 0.0)
    denominator = jnp.sum(exponent, axis=-1, keepdims=True)
    summed = jnp.einsum(
        "thn,nd->thd", exponent.astype(jnp.bfloat16), values, preferred_element_type=jnp.float32
    )
    context = (summed / denominator).astype(jnp.bfloat16).reshape(seq_count * tok_rows, heads_dev * HD)
    return lax.all_to_all(context, "seq", split_axis=0, concat_axis=1, tiled=True)


def solution(mesh):
    in_specs = (
        P(("seq", "row", "col"), None),
        P(("seq", "row", "col"), None),
        P(("seq", "row", "col"), None),
        P(("seq", "row", "col")),
        P(("row", "col"), None),
        P(("row", "col"), None),
        P(),
    )
    out_specs = P(("seq", "row", "col"), None)
    return jax.shard_map(
        on_device, mesh=mesh, in_specs=in_specs, out_specs=out_specs, check_vma=False
    )
```

time: 132 us -> 157 us (1.19)
  local copies, waits for them, and re-layouts: 8.45 us -> 28.4 us
  other arithmetic: 5.22 us -> 8.28 us
    all_to_all x1, waiting for transfers between devices: 9.12 us -> 25.9 us  [on_device(): recv = lax.all_to_all(send, 'seq', 0, 0, tiled=True)]
    all_to_all x1, waiting for transfers between devices: 72.1 us -> 55.6 us  [gather_cells(): return lax.all_to_all(spread, cell_axes, 0, 0, tiled=True)]
    slice x5 -> x9, local copies, waits for them, and re-layouts: 0.64 us -> 9.88 us  [the longest x2 7.21 us: on_device(): recv[:, q_len:q_len + kvp_len].reshape(seq_count * slice_rows, width)]
    all_to_all x1 -> x2, local copies, waits for them, and re-layouts: 0.51 us -> 5.88 us  [on_device(): recv = lax.all_to_all(send, 'seq', 0, 0, tiled=True)]
    unnamed x6 -> x13, local copies, waits for them, and re-layouts: 2.48 us -> 6.69 us
    all_to_all x2, other arithmetic: 0.71 us -> 3.22 us  [on_device(): recv = lax.all_to_all(send, 'seq', 0, 0, tiled=True)]
  transfers between devices with their start and end apart: 2 -> 2, of which waited for: 2 -> 2; matrix products, arithmetic and copies ran while one was open for 1% -> 2% of each run, Pallas kernels for 0% -> 0%
where the time goes in v3:
time: 157 us; the launch traced here: 156 us
  waiting for transfers between devices  81.5 us (52%)
  local copies, waits for them, and re-layouts  28.4 us (18%)
  starting transfers between devices  20.7 us (13%)
  blocking collectives  14.1 us (9%)
  other arithmetic  8.28 us (5%)
  matrix products  1.95 us (1%)
    all_to_all x1, waiting for transfers between devices, gather_cells(): return lax.all_to_all(spread, cell_axes, 0, 0, tiled=True)  55.6 us
    all_to_all x1, waiting for transfers between devices, on_device(): recv = lax.all_to_all(send, 'seq', 0, 0, tiled=True)  25.9 us
    all_to_all x1, blocking collectives, on_device(): lax.all_to_all(context, 'seq', split_axis=0, concat_axis=1, tiled=True)  14.1 us
    all_to_all x1, starting transfers between devices, gather_cells(): return lax.all_to_all(spread, cell_axes, 0, 0, tiled=True)  10.6 us
    all_to_all x1, starting transfers between devices, on_device(): recv = lax.all_to_all(send, 'seq', 0, 0, tiled=True)  10.2 us
    slice x2, local copies, waits for them, and re-layouts, on_device(): recv[:, q_len:q_len + kvp_len].reshape(seq_count * slice_rows, width)  7.21 us
    unnamed x13, local copies, waits for them, and re-layouts  6.69 us
    all_to_all x2, local copies, waits for them, and re-layouts, on_device(): recv = lax.all_to_all(send, 'seq', 0, 0, tiled=True)  5.88 us
  transfers between devices with their start and end apart: 2, of which 2 were waited for; matrix products, arithmetic and copies ran while one was open for 2% of the time, Pallas kernels for 0%

profile of v3, /device:TPU:8, one launch (start us, length us, event | category | flops | bytes accessed | tf_op | source)
XLA Modules:
  0.0 155.9 jit_solution(7708641772709412635)
XLA Ops:
  0.0 0.7 convert_bitcast_fusion
  0.7 0.1 copy.56
  0.8 0.1 convert_element_type.25
  0.9 0.7 pad_maximum_fusion
  1.6 0.9 constant_dynamic-slice_fusion.1
  2.6 1.6 %broadcast_in_dim.49 = bf16[16,289,256]{2,1,0:T(8,128)(2,1)} broadcast(bf16[289,256]{1,0:T(8,128)(2,1)S(1)} %fusion.24), dimensions={1,2} | broadcast | bytes 2515456 | tf_op jit(solution)/shard_map/broadcast_in_dim | solution.py:18
  4.1 0.0 copy-start.2
  4.1 10.6 %all-to-all-start = ((bf16[16,289,256]{2,1,0:T(8,128)(2,1)}), bf16[16,289,256]{2,1,0:T(8,128)(2,1)S(1)}, u32[]{:S(2)}, u32[]{:S(2)}) async-start(bf16[16,289,256]{2,1,0:T(8,128)(2,1)} %broadcast_in_dim.49), calls=%async_computation | async-start | bytes 4849664 | tf_op jit(solution)/shard_map/all_to_all | solution.py:19
  14.7 0.0 copy-done.2
  14.7 0.6 copy.70
  15.3 55.6 %all-to-all-done = bf16[16,289,256]{2,1,0:T(8,128)(2,1)S(1)} async-done(((bf16[16,289,256]{2,1,0:T(8,128)(2,1)}), bf16[16,289,256]{2,1,0:T(8,128)(2,1)S(1)}, u32[]{:S(2)}, u32[]{:S(2)}) %all-to-all-start) | async-done | bytes 2367520 | tf_op jit(solution)/shard_map/all_to_all | solution.py:19
  70.9 0.1 reshape.91
  71.1 0.1 reshape.79
  71.2 0.1 broadcast_in_dim.51
  71.3 0.6 copy.71
  72.0 1.0 maximum_bitcast_fusion.4
  73.0 0.5 broadcast.55
  73.5 2.2 %reduce.2 = bf16[32,17536]{1,0:T(8,128)(2,1)} reduce(bf16[32,1,17536]{2,0,1:T(8,128)(2,1)S(1)} %maximum_bitcast_fusion.4, bf16[]{:T(256)} %broadcast.55), dimensions={1}, to_apply=%copy.58.reduce_sub_computation | reduce | bytes 2244610 | tf_op jit(solution)/shard_map/all_to_all | solution.py:70
  75.7 3.0 %reshape.92 = bf16[32,2,8768]{2,1,0:T(2,128)(2,1)} reshape(bf16[32,17536]{1,0:T(8,128)(2,1)} %reduce.2) | data formatting | bytes 2244608
  78.7 10.2 %all-to-all-start.1 = ((bf16[32,2,8768]{2,1,0:T(2,128)(2,1)}), bf16[32,2,8768]{2,1,0:T(2,128)(2,1)S(1)}, u32[]{:S(2)}, u32[]{:S(2)}) async-start(bf16[32,2,8768]{2,1,0:T(2,128)(2,1)} %reshape.92), calls=%async_computation.1 | async-start | bytes 2260992 | tf_op jit(solution)/shard_map/all_to_all | solution.py:70
  89.5 0.6 pad.9.clone
  90.1 0.2 slice.62
  90.3 1.5 fusion.31
  91.9 25.9 %all-to-all-done.1 = bf16[32,2,8768]{2,1,0:T(2,128)(2,1)S(1)} async-done(((bf16[32,2,8768]{2,1,0:T(2,128)(2,1)}), bf16[32,2,8768]{2,1,0:T(2,128)(2,1)S(1)}, u32[]{:S(2)}, u32[]{:S(2)}) %all-to-all-start.1) | async-done | bytes 1122336 | tf_op jit(solution)/shard_map/all_to_all | solution.py:70
  117.8 1.8 %reshape.93 = bf16[32,1,17536]{2,1,0:T(2,128)(2,1)S(1)} reshape(bf16[32,2,8768]{2,1,0:T(2,128)(2,1)S(1)} %all-to-all-done.1) | data formatting | bytes 2244608
  119.6 5.4 %copy.59 = bf16[32,1,17536]{0,2,1:T(8,128)(2,1)} copy(bf16[32,1,17536]{2,1,0:T(2,128)(2,1)S(1)} %reshape.93) | data formatting | bytes 2244608 | tf_op jit(solution)/shard_map/all_to_all | solution.py:70
  125.0 0.8 slice.58
  125.8 1.0 slice.61
  126.8 3.7 %slice.64 = bf16[32,16384]{0,1:T(8,128)(2,1)} slice(bf16[32,17536]{0,1:T(8,128)(2,1)} %bitcast.51), slice={[0:32], [1024:17408]} | slice | bytes 2097152 | tf_op jit(solution)/shard_map/slice | solution.py:74
  130.5 0.1 copy.63
  130.6 0.1 reshape.82
  130.8 0.2 copy.62
  131.0 0.2 add.38
  131.1 3.5 %copy.65 = bf16[32,16384]{1,0:T(8,128)(2,1)S(1)} copy(bf16[32,16384]{0,1:T(8,128)(2,1)} %slice.64) | data formatting | bytes 2097152 | tf_op jit(solution)/shard_map/slice | solution.py:74
  134.6 0.0 copy-start.3
  134.7 0.1 copy.64
  134.8 0.0 copy-start
  134.8 0.5 reshape.85
  135.4 0.1 fusion.32
  135.4 0.2 broadcast_compare_fusion
  135.7 0.0 copy-done.3
  135.7 0.4 pad_add_fusion
  136.0 0.0 copy-done
  136.0 1.0 convolution_multiply_fusion
  137.0 0.0 copy-start.1
  137.0 3.0 %fusion.34 = (f32[128,2]{0,1:T(2,128)S(1)}, bf16[128,2,6144]{2,0,1:T(8,128)(2,1)S(1)}) fusion(f32[128,2,6144]{2,0,1:T(8,128)S(1)} %convolution_multiply_fusion, pred[128,6144]{1,0:T(8,128)(4,1)S(1)} %pad_add_fusion), kind=kOutput, calls=%fused_computation.50 | output fusion | flops 7870463 | bytes 10224640 | tf_op jit(solution)/shard_map/sub | solution.py:92
  140.1 0.0 copy-done.1
  140.1 1.0 fusion.20
  141.0 0.1 copy.67
  141.2 14.1 %all_to_all.36 = bf16[32,4,256]{2,1,0:T(4,128)(2,1)S(1)} all-to-all(bf16[32,4,256]{2,1,0:T(4,128)(2,1)S(1)} %all_to_all.29), channel_id=1, replica_groups=mesh['seq'=32,'row'=4,'col'=4] {'seq'}, dimensions={0} | all-to-all | bytes 131072 | tf_op jit(solution)/shard_map/all_to_all | solution.py:98
  155.3 0.6 copy.81
  (15 shorter events, 0.3 us)
Async XLA Ops:
  4.1 10.6 %copy-start.2 = (bf16[4,8192]{1,0:T(4,128)(2,1)S(1)}, bf16[4,8192]{1,0:T(4,128)(2,1)}, u32[]{:S(2)}) copy-start(bf16[4,8192]{1,0:T(4,128)(2,1)} %param.7) | copy-start | bytes 196612
  4.1 66.8 %all-to-all-start = ((bf16[16,289,256]{2,1,0:T(8,128)(2,1)}), bf16[16,289,256]{2,1,0:T(8,128)(2,1)S(1)}, u32[]{:S(2)}, u32[]{:S(2)}) async-start(bf16[16,289,256]{2,1,0:T(8,128)(2,1)} %broadcast_in_dim.49), calls=%async_computation | async-start | bytes 4849664 | tf_op jit(solution)/shard_map/all_to_all | solution.py:19
  78.7 39.1 %all-to-all-start.1 = ((bf16[32,2,8768]{2,1,0:T(2,128)(2,1)}), bf16[32,2,8768]{2,1,0:T(2,128)(2,1)S(1)}, u32[]{:S(2)}, u32[]{:S(2)}) async-start(bf16[32,2,8768]{2,1,0:T(2,128)(2,1)} %reshape.92), calls=%async_computation.1 | async-start | bytes 2260992 | tf_op jit(solution)/shard_map/all_to_all | solution.py:70
  134.6 1.0 copy-start.3
  134.8 1.2 copy-start
  137.0 3.0 %copy-start.1 = (bf16[4096,128]{1,0:T(8,128)(2,1)S(1)}, bf16[4096,128]{1,0:T(8,128)(2,1)}, u32[]{:S(2)}) copy-start(bf16[4096,128]{1,0:T(8,128)(2,1)} %get-tuple-element.6) | copy-start | bytes 3145732

commit v4 on v2

v4 whole, which is shorter than its diff:
```python
import math

import numpy as np
import jax
import jax.numpy as jnp
from jax import lax
from jax.sharding import PartitionSpec as P

HQ = 64
KVH = 8
HD = 128

far_position = 1073741824
code_base = 256


def gather_cells(block, cell_axes, cell_count):
    spread = jnp.broadcast_to(block[None], (cell_count,) + block.shape)
    return lax.all_to_all(spread, cell_axes, 0, 0, tiled=True)


def pick_heads(rows, kv_of_peer, tok_rows):
    split = rows.reshape(tok_rows, KVH, 1, HD)
    repeat = kv_of_peer.shape[0] // KVH
    if repeat * KVH == kv_of_peer.shape[0] and np.array_equal(kv_of_peer, np.arange(kv_of_peer.shape[0]) // repeat):
        spread = jnp.broadcast_to(split, (tok_rows, KVH, repeat, HD)).reshape(tok_rows, -1, HD)
    else:
        spread = jnp.take(split[:, :, 0], kv_of_peer, axis=1)
    return spread.transpose(1, 0, 2)


def partner_swap(x, pairs):
    return lax.ppermute(x, "row", pairs)


def partial_attention(query_block, query_pos, keys, values, key_pos_cache, key_pos_slab, cache_rows, first_pos):
    cache_ok = jnp.broadcast_to((key_pos_cache < first_pos)[None, :], (query_pos.shape[0], cache_rows))
    slab_ok = key_pos_slab[None, :] <= query_pos[:, None]
    allowed = jnp.concatenate([cache_ok, slab_ok], axis=1)[:, None, :]
    score_scale = 1.0 / math.sqrt(HD)
    scores = jnp.einsum("thd,nd->thn", query_block, keys, preferred_element_type=jnp.float32) * score_scale
    row_max = jnp.max(jnp.where(allowed, scores, -jnp.inf), axis=-1)
    exponent = jnp.where(allowed, jnp.exp(scores - row_max[..., None]), 0.0)
    row_sum = jnp.sum(exponent, axis=-1)
    summed = jnp.einsum(
        "thn,nd->thd", exponent.astype(jnp.bfloat16), values, preferred_element_type=jnp.float32
    )
    return row_max, row_sum, summed


def on_device(queries, new_keys, new_values, positions, cache_keys, cache_values, slab_start):
    seq_count = lax.axis_size("seq")
    cell_axes = ("row", "col")
    row_count = lax.axis_size("row")
    col_count = lax.axis_size("col")
    cell_count = row_count * col_count
    heads_dev = HQ // seq_count
    group_size = HQ // KVH
    tok_rows = queries.shape[0]
    first_pos = slab_start[0]
    kv_of_peer = np.arange(seq_count) * heads_dev // group_size
    kv_first = lax.axis_index("seq") * heads_dev // group_size
    core = lax.axis_index("row") % 2
    pairs = [(r, r ^ 1) for r in range(row_count)]
    width = 2 * HD

    q_part = queries.reshape(tok_rows, seq_count, heads_dev * HD).transpose(1, 0, 2)
    k_part = pick_heads(new_keys, kv_of_peer, tok_rows)
    v_part = pick_heads(new_values, kv_of_peer, tok_rows)
    codes = jnp.stack([positions // code_base, positions % code_base], axis=1).astype(jnp.bfloat16)
    codes = jnp.pad(codes.reshape(1, tok_rows * 2), ((0, 0), (0, 128 - tok_rows * 2)))
    send = jnp.concatenate(
        [
            q_part.reshape(seq_count, -1),
            k_part.reshape(seq_count, -1),
            v_part.reshape(seq_count, -1),
            jnp.broadcast_to(codes, (seq_count, 128)),
        ],
        axis=1,
    )
    recv = lax.all_to_all(send, "seq", 0, 0, tiled=True)
    q_len = tok_rows * heads_dev * HD
    kv_len = tok_rows * HD
    slab_rows = seq_count * tok_rows
    query_block = recv[:, :q_len].reshape(slab_rows, heads_dev, HD)
    slab_k = recv[:, q_len : q_len + kv_len].reshape(slab_rows, HD)
    slab_v = recv[:, q_len + kv_len : q_len + 2 * kv_len].reshape(slab_rows, HD)
    got_codes = recv[:, q_len + 2 * kv_len : q_len + 2 * kv_len + tok_rows * 2]
    got_codes = got_codes.reshape(slab_rows, 2)
    own_pos = got_codes[:, 0].astype(jnp.float32) * code_base + got_codes[:, 1].astype(jnp.float32)

    partner_q = partner_swap(jnp.concatenate([query_block.reshape(slab_rows, -1), got_codes], axis=1), pairs)
    partner_block = partner_q[:, : heads_dev * HD].reshape(slab_rows, heads_dev, HD)
    partner_codes = partner_q[:, heads_dev * HD :].astype(jnp.float32)
    partner_pos = partner_codes[:, 0] * code_base + partner_codes[:, 1]

    cache_block = jnp.concatenate(
        [
            lax.dynamic_slice_in_dim(cache_keys, kv_first * HD, HD, 1),
            lax.dynamic_slice_in_dim(cache_values, kv_first * HD, HD, 1),
        ],
        axis=1,
    )
    cache_len = cache_block.shape[0]
    half_cache = cache_len // 2
    half_slab = slab_rows // 2
    slab_kv = jnp.concatenate([slab_k, slab_v], axis=1)
    code_rows = jnp.pad(got_codes.reshape(2, half_slab * 2), ((0, 0), (0, width - half_slab * 2)))
    halves = jnp.stack(
        [
            jnp.concatenate(
                [cache_block[b * half_cache : (b + 1) * half_cache], slab_kv[b * half_slab : (b + 1) * half_slab], code_rows[b : b + 1]],
                axis=0,
            )
            for b in range(2)
        ]
    )
    per_dest = jnp.broadcast_to(
        halves[None, :, None], (row_count // 2, 2, col_count) + halves.shape[1:]
    ).reshape((cell_count,) + halves.shape[1:])
    every = lax.all_to_all(per_dest, cell_axes, 0, 0, tiled=True)
    cache_got = every[:, :half_cache].reshape(-1, width)
    slab_got = every[:, half_cache : half_cache + half_slab].reshape(-1, width)
    key_codes = every[:, half_cache + half_slab, : 2 * half_slab].reshape(-1, 2).astype(jnp.float32)
    key_pos_slab = key_codes[:, 0] * code_base + key_codes[:, 1]
    key_pos_cache = (
        jnp.arange(cell_count, dtype=jnp.int32)[:, None] * cache_len
        + core * half_cache
        + jnp.arange(half_cache, dtype=jnp.int32)[None, :]
    ).reshape(-1)
    keys = jnp.concatenate([cache_got[:, :HD], slab_got[:, :HD]], axis=0)
    values = jnp.concatenate([cache_got[:, HD:], slab_got[:, HD:]], axis=0)

    both_q = jnp.concatenate([query_block, partner_block], axis=0)
    both_pos = jnp.concatenate([own_pos, partner_pos], axis=0)
    row_max, row_sum, summed = partial_attention(
        both_q, both_pos, keys, values, key_pos_cache, key_pos_slab, cache_got.shape[0], first_pos
    )
    theirs = jnp.concatenate(
        [summed[slab_rows:].reshape(slab_rows, -1), row_max[slab_rows:], row_sum[slab_rows:]], axis=1
    )
    got = partner_swap(theirs, pairs)
    other_summed = got[:, : heads_dev * HD].reshape(slab_rows, heads_dev, HD)
    other_max = got[:, heads_dev * HD : heads_dev * HD + heads_dev]
    other_sum = got[:, heads_dev * HD + heads_dev :]
    mine_max = row_max[:slab_rows]
    top = jnp.maximum(mine_max, other_max)
    scale_mine = jnp.exp(mine_max - top)
    scale_other = jnp.exp(other_max - top)
    numerator = summed[:slab_rows] * scale_mine[..., None] + other_summed * scale_other[..., None]
    denominator = row_sum[:slab_rows] * scale_mine + other_sum * scale_other
    context = (numerator / denominator[..., None]).astype(jnp.bfloat16).reshape(slab_rows, heads_dev * HD)
    return lax.all_to_all(context, "seq", split_axis=0, concat_axis=1, tiled=True)


def solution(mesh):
    in_specs = (
        P(("seq", "row", "col"), None),
        P(("seq", "row", "col"), None),
        P(("seq", "row", "col"), None),
        P(("seq", "row", "col")),
        P(("row", "col"), None),
        P(("row", "col"), None),
        P(),
    )
    out_specs = P(("seq", "row", "col"), None)
    return jax.shard_map(
        on_device, mesh=mesh, in_specs=in_specs, out_specs=out_specs, check_vma=False
    )
```

time: 132 us -> 102 us (0.77)
  the two profiles are of different devices: /device:TPU:8 before, /device:TPU:1 now
where the time goes in v4:
time: 102 us
  waiting for transfers between devices  43.2 us (42%)
  starting transfers between devices  28.8 us (28%)
  blocking collectives  12.5 us (12%)
  local copies, waits for them, and re-layouts  8.37 us (8%)
  other arithmetic  4.74 us (5%)
  matrix products  3.07 us (3%)
  between operations  1.05 us (1%)
    all_to_all x1, waiting for transfers between devices, on_device(): every = lax.all_to_all(per_dest, cell_axes, 0, 0, tiled=True)  32.8 us
    all_to_all x1, blocking collectives, on_device(): lax.all_to_all(context, 'seq', split_axis=0, concat_axis=1, tiled=True)  12.5 us
    all_to_all x1, starting transfers between devices, on_device(): every = lax.all_to_all(per_dest, cell_axes, 0, 0, tiled=True)  12.4 us
    all_to_all x1, starting transfers between devices, on_device(): recv = lax.all_to_all(send, 'seq', 0, 0, tiled=True)  10.5 us
    all_to_all x1, waiting for transfers between devices, on_device(): recv = lax.all_to_all(send, 'seq', 0, 0, tiled=True)  8.37 us
    ppermute x2, starting transfers between devices, partner_swap(): return lax.ppermute(x, 'row', pairs)  5.92 us
    unnamed x6, local copies, waits for them, and re-layouts  2.48 us
  transfers between devices with their start and end apart: 4, of which 4 were waited for; matrix products, arithmetic and copies ran while one was open for 2% of the time, Pallas kernels for 0%

profile of v4, /device:TPU:1, one launch (start us, length us, event | category | flops | bytes accessed | tf_op | source)
XLA Modules:
  0.0 101.7 jit_solution(4349187265353521852)
XLA Ops:
  0.0 0.7 convert_bitcast_fusion
  0.7 0.1 copy.50
  0.8 0.1 convert_element_type.38
  0.9 0.8 copy.60
  1.8 0.7 broadcast_in_dim.62
  2.5 0.7 broadcast_in_dim.64
  3.2 0.5 broadcast.90
  3.8 0.7 reduce.10
  4.4 0.8 reshape.155
  5.3 10.5 %all-to-all-start = ((bf16[32,2,1088]{2,1,0:T(2,128)(2,1)}), bf16[32,2,1088]{2,1,0:T(2,128)(2,1)S(1)}, u32[]{:S(2)}, u32[]{:S(2)}) async-start(bf16[32,2,1088]{2,1,0:T(2,128)(2,1)} %reshape.155), calls=%async_computation | async-start | bytes 294912 | tf_op jit(solution)/shard_map/all_to_all | solution.py:81
  15.8 0.9 constant_dynamic-slice_fusion
  16.7 8.4 %all-to-all-done = bf16[32,2,1088]{2,1,0:T(2,128)(2,1)S(1)} async-done(((bf16[32,2,1088]{2,1,0:T(2,128)(2,1)}), bf16[32,2,1088]{2,1,0:T(2,128)(2,1)S(1)}, u32[]{:S(2)}, u32[]{:S(2)}) %all-to-all-start) | async-done | bytes 139296 | tf_op jit(solution)/shard_map/all_to_all | solution.py:81
  25.1 0.1 reshape.156
  25.3 0.1 reshape_reshape.6
  25.6 1.3 %broadcast_in_dim.67 = bf16[2,2,4,193,256]{4,3,2,1,0:T(8,128)(2,1)} broadcast(bf16[2,193,256]{2,1,0:T(8,128)(2,1)S(1)} %pad_maximum_fusion), dimensions={1,3,4} | broadcast | bytes 1778688 | tf_op jit(solution)/shard_map/broadcast_in_dim | solution.py:118
  26.9 12.4 %all-to-all-start.1 = ((bf16[16,193,256]{2,1,0:T(8,128)(2,1)}), bf16[16,193,256]{2,1,0:T(8,128)(2,1)S(1)}, u32[]{:S(2)}, u32[]{:S(2)}) async-start(bf16[16,193,256]{2,1,0:T(8,128)(2,1)} %bitcast.16), calls=%async_computation.1 | async-start | bytes 3276800 | tf_op jit(solution)/shard_map/all_to_all | solution.py:121
  40.0 0.1 fusion.23
  40.0 0.1 reshape.133
  40.2 0.1 reshape_reshape.7
  40.3 2.0 %collective-permute-start = (bf16[128,258]{1,0:T(8,128)(2,1)S(1)}, bf16[128,258]{1,0:T(8,128)(2,1)S(1)}, u32[]{:S(2)}, u32[]{:S(2)}) collective-permute-start(bf16[128,258]{1,0:T(8,128)(2,1)S(1)} %pad_maximum_fusion.3), channel_id=1, source_target_pairs={{0,4},{4,0},{8,12},{12,8},{1,5},{5,1},{9,13},{13,9},{2,6},{6,2},{1... | collective-permute-start | bytes 198152 | tf_op jit(solution)/shard_map/ppermute | solution.py:33
  42.3 0.2 add_reduce_fusion
  42.5 1.0 collective-permute-done
  43.5 0.1 copy.52
  43.6 0.1 copy.54
  43.7 0.2 fusion.21
  43.9 32.8 %all-to-all-done.1 = bf16[16,193,256]{2,1,0:T(8,128)(2,1)S(1)} async-done(((bf16[16,193,256]{2,1,0:T(8,128)(2,1)}), bf16[16,193,256]{2,1,0:T(8,128)(2,1)S(1)}, u32[]{:S(2)}, u32[]{:S(2)}) %all-to-all-start.1) | async-done | bytes 1581088 | tf_op jit(solution)/shard_map/all_to_all | solution.py:121
  76.8 0.5 reshape.140
  77.3 0.4 fusion.10
  77.7 0.1 slice.153
  77.8 0.1 fusion.35
  77.9 0.2 broadcast_compare_fusion
  78.1 0.3 pad_add_fusion
  78.4 1.5 %select_reduce_fusion = (f32[256,2]{0,1:T(2,128)S(1)}, f32[256,2,3072]{2,0,1:T(8,128)S(1)}) fusion(pred[256,3072]{1,0:T(8,128)(4,1)S(1)} %pad_add_fusion, bf16[1024,128]{1,0:T(8,128)(2,1)S(1)} %get-tuple-element.11, bf16[2048,128]{1,0:T(8,128)(2,1)S(1)} %get-tuple-element.9, bf16[128,2,128]{2,0,1:T(8,128)(2,1)S(1)} %copy.54, bf16[128,2,128]{2,0,1:T(8,128)(2,1)S(1)} %copy.53), kind=kOutput, calls=%fused_computation.1 | convolution fusion | flops 409206272 | bytes 7997440 | tf_op jit(solution)/shard_map/thd,nd->thn/dot_general | solution.py:41
  79.9 1.9 %fusion = f32[256,2]{0,1:T(2,128)S(1)} fusion(f32[256,2,3072]{2,0,1:T(8,128)S(1)} %get-tuple-element.21, f32[256,2]{0,1:T(2,128)S(1)} %get-tuple-element.20, pred[256,3072]{1,0:T(8,128)(4,1)S(1)} %pad_add_fusion), kind=kLoop, calls=%fused_computation.2 | loop fusion | flops 6290944 | bytes 7081984 | tf_op jit(solution)/shard_map/reduce_sum | solution.py:44
  81.8 1.6 %fusion.2 = f32[256,2,128]{0,2,1:T(8,128)S(1)} fusion(f32[256,2,3072]{2,0,1:T(8,128)S(1)} %get-tuple-element.21, f32[256,2]{0,1:T(2,128)S(1)} %get-tuple-element.20, pred[256,3072]{1,0:T(8,128)(4,1)S(1)} %pad_add_fusion, bf16[1024,128]{1,0:T(8,128)(2,1)S(1)} %get-tuple-element.10, bf16[2048,128]{1,0:T(8,128)(2,1)S(1)} %get-tuple-element.8), kind=kOutput, calls=%fused_computation.4 | convolution fusion | flops 410517504 | bytes 8128512 | tf_op jit(solution)/shard_map/thn,nd->thd/dot_general | solution.py:45
  83.4 3.9 %collective-permute-start.1 = (f32[128,260]{0,1:T(8,128)S(1)}, f32[128,260]{0,1:T(8,128)S(1)}, u32[]{:S(2)}, u32[]{:S(2)}) collective-permute-start(f32[128,260]{0,1:T(8,128)S(1)} %pad_maximum_fusion.1), channel_id=1, source_target_pairs={{0,4},{4,0},{8,12},{12,8},{1,5},{5,1},{9,13},{13,9},{2,6},{6,2},{1... | collective-permute-start | bytes 399368 | tf_op jit(solution)/shard_map/ppermute | solution.py:33
  87.4 1.0 collective-permute-done.1
  88.4 0.1 copy.56
  88.6 12.5 %all_to_all.36 = bf16[32,4,256]{2,1,0:T(4,128)(2,1)S(1)} all-to-all(bf16[32,4,256]{2,1,0:T(4,128)(2,1)S(1)} %all_to_all.29), channel_id=1, replica_groups=mesh['seq'=32,'row'=4,'col'=4] {'seq'}, dimensions={0} | all-to-all | bytes 131072 | tf_op jit(solution)/shard_map/all_to_all | solution.py:153
  101.0 0.6 copy.71
  (38 shorter events, 0.6 us)
Async XLA Ops:
  5.3 19.8 %all-to-all-start = ((bf16[32,2,1088]{2,1,0:T(2,128)(2,1)}), bf16[32,2,1088]{2,1,0:T(2,128)(2,1)S(1)}, u32[]{:S(2)}, u32[]{:S(2)}) async-start(bf16[32,2,1088]{2,1,0:T(2,128)(2,1)} %reshape.155), calls=%async_computation | async-start | bytes 294912 | tf_op jit(solution)/shard_map/all_to_all | solution.py:81
  26.9 49.9 %all-to-all-start.1 = ((bf16[16,193,256]{2,1,0:T(8,128)(2,1)}), bf16[16,193,256]{2,1,0:T(8,128)(2,1)S(1)}, u32[]{:S(2)}, u32[]{:S(2)}) async-start(bf16[16,193,256]{2,1,0:T(8,128)(2,1)} %bitcast.16), calls=%async_computation.1 | async-start | bytes 3276800 | tf_op jit(solution)/shard_map/all_to_all | solution.py:121
  40.3 3.2 %collective-permute-start = (bf16[128,258]{1,0:T(8,128)(2,1)S(1)}, bf16[128,258]{1,0:T(8,128)(2,1)S(1)}, u32[]{:S(2)}, u32[]{:S(2)}) collective-permute-start(bf16[128,258]{1,0:T(8,128)(2,1)S(1)} %pad_maximum_fusion.3), channel_id=1, source_target_pairs={{0,4},{4,0},{8,12},{12,8},{1,5},{5,1},{9,13},{13,9},{2,6},{6,2},{1... | collective-permute-start | bytes 198152 | tf_op jit(solution)/shard_map/ppermute | solution.py:33
  83.4 4.9 %collective-permute-start.1 = (f32[128,260]{0,1:T(8,128)S(1)}, f32[128,260]{0,1:T(8,128)S(1)}, u32[]{:S(2)}, u32[]{:S(2)}) collective-permute-start(f32[128,260]{0,1:T(8,128)S(1)} %pad_maximum_fusion.1), channel_id=1, source_target_pairs={{0,4},{4,0},{8,12},{12,8},{1,5},{5,1},{9,13},{13,9},{2,6},{6,2},{1... | collective-permute-start | bytes 399368 | tf_op jit(solution)/shard_map/ppermute | solution.py:33

commit v5 on v4

v5 whole, which is shorter than its diff:
```python
import math

import numpy as np
import jax
import jax.numpy as jnp
from jax import lax
from jax.sharding import PartitionSpec as P

HQ = 64
KVH = 8
HD = 128

far_position = 1073741824
code_base = 256


def gather_cells(block, cell_axes, cell_count):
    spread = jnp.broadcast_to(block[None], (cell_count,) + block.shape)
    return lax.all_to_all(spread, cell_axes, 0, 0, tiled=True)


def pick_heads(rows, kv_of_peer, tok_rows):
    split = rows.reshape(tok_rows, KVH, 1, HD)
    repeat = kv_of_peer.shape[0] // KVH
    if repeat * KVH == kv_of_peer.shape[0] and np.array_equal(kv_of_peer, np.arange(kv_of_peer.shape[0]) // repeat):
        spread = jnp.broadcast_to(split, (tok_rows, KVH, repeat, HD)).reshape(tok_rows, -1, HD)
    else:
        spread = jnp.take(split[:, :, 0], kv_of_peer, axis=1)
    return spread.transpose(1, 0, 2)


def partner_swap(x, pairs):
    return lax.ppermute(x, "row", pairs)


def partial_attention(query_block, query_pos, keys, values, key_pos_cache, key_pos_slab, cache_rows, first_pos):
    cache_ok = jnp.broadcast_to((key_pos_cache < first_pos)[None, :], (query_pos.shape[0], cache_rows))
    slab_ok = key_pos_slab[None, :] <= query_pos[:, None]
    allowed = jnp.concatenate([cache_ok, slab_ok], axis=1)[:, None, :]
    score_scale = 1.0 / math.sqrt(HD)
    scores = jnp.einsum("thd,nd->thn", query_block, keys, preferred_element_type=jnp.float32) * score_scale
    row_max = jnp.max(jnp.where(allowed, scores, -jnp.inf), axis=-1)
    exponent = jnp.where(allowed, jnp.exp(scores - row_max[..., None]), 0.0)
    row_sum = jnp.sum(exponent, axis=-1)
    summed = jnp.einsum(
        "thn,nd->thd", exponent.astype(jnp.bfloat16), values, preferred_element_type=jnp.float32
    )
    return row_max, row_sum, summed


def swap(x, axes, pairs):
    return lax.ppermute(x, axes, pairs)


def decode(codes):
    codes = codes.astype(jnp.float32)
    return codes[..., 0] * code_base + codes[..., 1]


def on_device(queries, new_keys, new_values, positions, cache_keys, cache_values, slab_start):
    seq_count = lax.axis_size("seq")
    cell_axes = ("row", "col")
    row_count = lax.axis_size("row")
    col_count = lax.axis_size("col")
    cell_count = row_count * col_count
    heads_dev = HQ // seq_count
    group_size = HQ // KVH
    tok_rows = queries.shape[0]
    first_pos = slab_start[0]
    seq_index = lax.axis_index("seq")
    kv_first = seq_index * heads_dev // group_size
    parity = seq_index % 2
    core = lax.axis_index("row") % 2
    quarter = parity * 2 + core
    core_pairs = [(r, r ^ 1) for r in range(row_count)]
    seq_pairs = [(q, q ^ 1) for q in range(seq_count)]
    diag_pairs = [(q * row_count + r, (q ^ 1) * row_count + (r ^ 1)) for q in range(seq_count) for r in range(row_count)]
    width = 2 * HD
    pair_heads = 2 * heads_dev
    half_tok = tok_rows // 2

    q_pairs = queries.reshape(tok_rows, seq_count // 2, 1, pair_heads * HD)
    q_part = jnp.broadcast_to(q_pairs, (tok_rows, seq_count // 2, 2, pair_heads * HD)).reshape(tok_rows, seq_count, -1)
    kv_local = jnp.concatenate(
        [new_keys.reshape(tok_rows, KVH, 1, HD), new_values.reshape(tok_rows, KVH, 1, HD)], axis=2
    ).reshape(2, half_tok, KVH, 1, width)
    repeat = seq_count // (2 * KVH)
    kv_part = jnp.broadcast_to(
        kv_local.transpose(2, 3, 0, 1, 4)[:, :, None], (KVH, 1, repeat, 2, half_tok, width)
    ).reshape(seq_count, half_tok * width)
    codes = jnp.stack([positions // code_base, positions % code_base], axis=1).astype(jnp.bfloat16)
    codes = jnp.pad(codes.reshape(1, tok_rows * 2), ((0, 0), (0, 128 - tok_rows * 2)))
    send = jnp.concatenate(
        [q_part.transpose(1, 0, 2).reshape(seq_count, -1), kv_part, jnp.broadcast_to(codes, (seq_count, 128))],
        axis=1,
    )
    recv = lax.all_to_all(send, "seq", 0, 0, tiled=True)
    q_len = tok_rows * pair_heads * HD
    kvp_len = half_tok * width
    slab_rows = seq_count * tok_rows
    query_block = recv[:, :q_len].reshape(slab_rows, pair_heads, HD)
    slab_kv = recv[:, q_len : q_len + kvp_len].reshape(seq_count * half_tok, width)
    got_codes = recv[:, q_len + kvp_len : q_len + kvp_len + tok_rows * 2].reshape(seq_count, tok_rows, 2)
    own_pos = decode(got_codes.reshape(slab_rows, 2))
    slab_codes = lax.dynamic_slice_in_dim(got_codes, parity * half_tok, half_tok, 1).reshape(seq_count * half_tok, 2)

    partner_q = swap(
        jnp.concatenate([query_block.reshape(slab_rows, -1), got_codes.reshape(slab_rows, 2)], axis=1), "row", core_pairs
    )
    partner_block = partner_q[:, : pair_heads * HD].reshape(slab_rows, pair_heads, HD)
    partner_pos = decode(partner_q[:, pair_heads * HD :])

    cache_block = jnp.concatenate(
        [
            lax.dynamic_slice_in_dim(cache_keys, kv_first * HD, HD, 1),
            lax.dynamic_slice_in_dim(cache_values, kv_first * HD, HD, 1),
        ],
        axis=1,
    )
    cache_len = cache_block.shape[0]
    part_cache = cache_len // 4
    half_slab = slab_kv.shape[0] // 2
    code_rows = jnp.pad(slab_codes.reshape(2, half_slab * 2), ((0, 0), (0, width - half_slab * 2)))
    cache_pair = lax.dynamic_slice_in_dim(cache_block, parity * 2 * part_cache, 2 * part_cache, 0)
    halves = jnp.stack(
        [
            jnp.concatenate(
                [
                    cache_pair[b * part_cache : (b + 1) * part_cache],
                    slab_kv[b * half_slab : (b + 1) * half_slab],
                    code_rows[b : b + 1],
                ],
                axis=0,
            )
            for b in range(2)
        ]
    )
    per_dest = jnp.broadcast_to(
        halves[None, :, None], (row_count // 2, 2, col_count) + halves.shape[1:]
    ).reshape((cell_count,) + halves.shape[1:])
    every = lax.all_to_all(per_dest, cell_axes, 0, 0, tiled=True)
    cache_got = every[:, :part_cache].reshape(-1, width)
    slab_got = every[:, part_cache : part_cache + half_slab].reshape(-1, width)
    key_pos_slab = decode(every[:, part_cache + half_slab, : 2 * half_slab].reshape(-1, 2))
    key_pos_cache = (
        jnp.arange(cell_count, dtype=jnp.int32)[:, None] * cache_len
        + quarter * part_cache
        + jnp.arange(part_cache, dtype=jnp.int32)[None, :]
    ).reshape(-1)
    keys = jnp.concatenate([cache_got[:, :HD], slab_got[:, :HD]], axis=0)
    values = jnp.concatenate([cache_got[:, HD:], slab_got[:, HD:]], axis=0)

    both_q = jnp.concatenate([query_block, partner_block], axis=0)
    both_pos = jnp.concatenate([own_pos, partner_pos], axis=0)
    row_max, row_sum, summed = partial_attention(
        both_q, both_pos, keys, values, key_pos_cache, key_pos_slab, cache_got.shape[0], first_pos
    )

    def block(rows, pair):
        take = slice(rows * slab_rows, (rows + 1) * slab_rows)
        heads = pl_heads(pair, heads_dev)
        return jnp.concatenate(
            [
                lax.dynamic_slice_in_dim(summed[take], heads, heads_dev, 1).reshape(slab_rows, -1),
                lax.dynamic_slice_in_dim(row_max[take], heads, heads_dev, 1),
                lax.dynamic_slice_in_dim(row_sum[take], heads, heads_dev, 1),
            ],
            axis=1,
        )

    pieces = [
        block(0, parity),
        swap(block(1, parity), "row", core_pairs),
        swap(block(0, 1 - parity), "seq", seq_pairs),
        swap(block(1, 1 - parity), ("seq", "row"), diag_pairs),
    ]
    split_at = heads_dev * HD
    maxes = [p[:, split_at : split_at + heads_dev] for p in pieces]
    top = maxes[0]
    for m in maxes[1:]:
        top = jnp.maximum(top, m)
    numerator = 0.0
    denominator = 0.0
    for p, m in zip(pieces, maxes):
        factor = jnp.exp(m - top)
        numerator = numerator + p[:, :split_at].reshape(slab_rows, heads_dev, HD) * factor[..., None]
        denominator = denominator + p[:, split_at + heads_dev :] * factor
    context = (numerator / denominator[..., None]).astype(jnp.bfloat16).reshape(slab_rows, heads_dev * HD)
    return lax.all_to_all(context, "seq", split_axis=0, concat_axis=1, tiled=True)


def pl_heads(pair, heads_dev):
    return pair * heads_dev


def solution(mesh):
    in_specs = (
        P(("seq", "row", "col"), None),
        P(("seq", "row", "col"), None),
        P(("seq", "row", "col"), None),
        P(("seq", "row", "col")),
        P(("row", "col"), None),
        P(("row", "col"), None),
        P(),
    )
    out_specs = P(("seq", "row", "col"), None)
    return jax.shard_map(
        on_device, mesh=mesh, in_specs=in_specs, out_specs=out_specs, check_vma=False
    )
```

time: 102 us -> 92.7 us (0.909)
  the two profiles are of different devices: /device:TPU:1 before, /device:TPU:8 now
where the time goes in v5:
time: 92.7 us; the launch traced here: 91.9 us
  starting transfers between devices  30.8 us (33%)
  waiting for transfers between devices  30.3 us (33%)
  blocking collectives  13.2 us (14%)
  local copies, waits for them, and re-layouts  9.26 us (10%)
  other arithmetic  4.41 us (5%)
  matrix products  2.81 us (3%)
  between operations  1.19 us (1%)
    all_to_all x1, waiting for transfers between devices, on_device(): every = lax.all_to_all(per_dest, cell_axes, 0, 0, tiled=True)  17.7 us
    all_to_all x1, blocking collectives, on_device(): lax.all_to_all(context, 'seq', split_axis=0, concat_axis=1, tiled=True)  13.2 us
    all_to_all x1, starting transfers between devices, on_device(): every = lax.all_to_all(per_dest, cell_axes, 0, 0, tiled=True)  10.4 us
    ppermute x4, starting transfers between devices, swap(): return lax.ppermute(x, axes, pairs)  10.2 us
    all_to_all x1, starting transfers between devices, on_device(): recv = lax.all_to_all(send, 'seq', 0, 0, tiled=True)  10.2 us
    all_to_all x1, waiting for transfers between devices, on_device(): recv = lax.all_to_all(send, 'seq', 0, 0, tiled=True)  9.7 us
    ppermute x4, waiting for transfers between devices, swap(): return lax.ppermute(x, axes, pairs)  2.89 us
  transfers between devices with their start and end apart: 6, of which 4 were waited for; matrix products, arithmetic and copies ran while one was open for 3% of the time, Pallas kernels for 0%

profile of v5, /device:TPU:8, one launch (start us, length us, event | category | flops | bytes accessed | tf_op | source)
XLA Modules:
  0.0 91.9 jit_solution(619144104955917064)
XLA Ops:
  0.0 0.7 convert_bitcast_fusion
  0.7 0.1 copy.63
  0.8 0.1 convert_element_type.33
  0.9 0.7 copy_bitcast_fusion
  1.7 0.9 broadcast_in_dim.36
  2.7 0.5 broadcast.97
  3.2 0.7 reduce.10
  3.9 0.9 reshape.167
  4.8 10.2 %all-to-all-start = ((bf16[32,2,1344]{2,1,0:T(2,128)(2,1)}), bf16[32,2,1344]{2,1,0:T(2,128)(2,1)S(1)}, u32[]{:S(2)}, u32[]{:S(2)}) async-start(bf16[32,2,1344]{2,1,0:T(2,128)(2,1)} %reshape.167), calls=%async_computation | async-start | bytes 360448 | tf_op jit(solution)/shard_map/all_to_all | solution.py:97
  15.0 0.9 constant_dynamic-slice_fusion.12
  15.9 9.7 %all-to-all-done = bf16[32,2,1344]{2,1,0:T(2,128)(2,1)S(1)} async-done(((bf16[32,2,1344]{2,1,0:T(2,128)(2,1)}), bf16[32,2,1344]{2,1,0:T(2,128)(2,1)S(1)}, u32[]{:S(2)}, u32[]{:S(2)}) %all-to-all-start) | async-done | bytes 172064 | tf_op jit(solution)/shard_map/all_to_all | solution.py:97
  25.6 0.2 reshape.168
  25.8 1.1 %copy.65 = bf16[32,1,2688]{0,2,1:T(8,128)(2,1)S(1)} copy(bf16[32,1,2688]{2,1,0:T(2,128)(2,1)S(1)} %reshape.168) | data formatting | bytes 344064 | tf_op jit(solution)/shard_map/all_to_all | solution.py:97
  26.9 0.1 fusion.28
  27.0 0.1 copy.67
  27.2 0.1 reshape_reshape.10
  27.3 0.1 copy.66
  27.4 0.1 copy.68
  27.6 1.0 %broadcast_in_dim.70 = bf16[2,2,4,97,256]{4,3,2,1,0:T(8,128)(2,1)} broadcast(bf16[2,97,256]{2,1,0:T(8,128)(2,1)S(1)} %pad_maximum_fusion.4), dimensions={1,3,4} | broadcast | bytes 893952 | tf_op jit(solution)/shard_map/broadcast_in_dim | solution.py:138
  28.5 10.4 %all-to-all-start.1 = ((bf16[16,97,256]{2,1,0:T(8,128)(2,1)}), bf16[16,97,256]{2,1,0:T(8,128)(2,1)S(1)}, u32[]{:S(2)}, u32[]{:S(2)}) async-start(bf16[16,97,256]{2,1,0:T(8,128)(2,1)} %bitcast.15), calls=%async_computation.1 | async-start | bytes 1703936 | tf_op jit(solution)/shard_map/all_to_all | solution.py:141
  39.6 0.1 copy.69
  39.8 0.1 reshape_reshape.11
  39.8 0.2 copy.70
  40.0 0.1 reshape_reshape.12
  40.1 2.3 %collective-permute-start = (bf16[128,514]{1,0:T(8,128)(2,1)S(1)}, bf16[128,514]{1,0:T(8,128)(2,1)S(1)}, u32[]{:S(2)}, u32[]{:S(2)}) collective-permute-start(bf16[128,514]{1,0:T(8,128)(2,1)S(1)} %pad_maximum_fusion), channel_id=1, source_target_pairs={{0,4},{4,0},{8,12},{12,8},{1,5},{5,1},{9,13},{13,9},{2,6},{6,2},{1... | collective-permute-start | bytes 394760 | tf_op jit(solution)/shard_map/ppermute | solution.py:52
  42.5 0.1 add_compare_fusion
  42.5 0.1 reshape.164
  42.6 0.1 reshape.142
  42.7 0.2 fusion.16
  42.9 0.5 collective-permute-done
  43.5 0.1 copy.72
  43.6 0.1 copy.74
  43.8 0.2 fusion.15
  44.0 17.7 %all-to-all-done.1 = bf16[16,97,256]{2,1,0:T(8,128)(2,1)S(1)} async-done(((bf16[16,97,256]{2,1,0:T(8,128)(2,1)}), bf16[16,97,256]{2,1,0:T(8,128)(2,1)S(1)}, u32[]{:S(2)}, u32[]{:S(2)}) %all-to-all-start.1) | async-done | bytes 794656 | tf_op jit(solution)/shard_map/all_to_all | solution.py:141
  61.7 0.3 reshape.152
  61.9 0.2 fusion.10
  62.3 0.1 broadcast_compare_fusion
  62.5 0.1 pad_add_fusion
  62.6 1.3 %select_reduce_fusion = (f32[256,4]{0,1:T(4,128)S(1)}, f32[256,4,1536]{2,0,1:T(8,128)S(1)}) fusion(pred[256,1536]{1,0:T(8,128)(4,1)S(1)} %pad_add_fusion, bf16[512,128]{1,0:T(8,128)(2,1)S(1)} %get-tuple-element.19, bf16[1024,128]{1,0:T(8,128)(2,1)S(1)} %get-tuple-element.15, bf16[128,4,128]{2,0,1:T(8,128)(2,1)S(1)} %copy.74, bf16[128,4,128]{2,0,1:T(8,128)(2,1)S(1)} %copy.73), kind=kOutput, calls=%fused_computation.1 | convolution fusion | flops 408681472 | bytes 7344128 | tf_op jit(solution)/shard_map/thd,nd->thn/dot_general | solution.py:41
  63.9 1.8 %fusion = f32[256,4]{0,1:T(4,128)S(1)} fusion(f32[256,4,1536]{2,0,1:T(8,128)S(1)} %get-tuple-element.35, f32[256,4]{0,1:T(4,128)S(1)} %get-tuple-element.34, pred[256,1536]{1,0:T(8,128)(4,1)S(1)} %pad_add_fusion), kind=kLoop, calls=%fused_computation.2 | loop fusion | flops 6290432 | bytes 6692864 | tf_op jit(solution)/shard_map/reduce_sum | solution.py:44
  65.7 1.5 %fusion.2 = f32[256,4,128]{0,2,1:T(8,128)S(1)} fusion(f32[256,4,1536]{2,0,1:T(8,128)S(1)} %get-tuple-element.35, f32[256,4]{0,1:T(4,128)S(1)} %get-tuple-element.34, pred[256,1536]{1,0:T(8,128)(4,1)S(1)} %pad_add_fusion, bf16[512,128]{1,0:T(8,128)(2,1)S(1)} %get-tuple-element.18, bf16[1024,128]{1,0:T(8,128)(2,1)S(1)} %get-tuple-element.14), kind=kOutput, calls=%fused_computation.4 | convolution fusion | flops 409731072 | bytes 7606272 | tf_op jit(solution)/shard_map/thn,nd->thd/dot_general | solution.py:45
  67.5 2.5 %collective-permute-start.2 = (f32[128,260]{0,1:T(8,128)S(1)}, f32[128,260]{0,1:T(8,128)S(1)}, u32[]{:S(2)}, u32[]{:S(2)}) collective-permute-start(f32[128,260]{0,1:T(8,128)S(1)} %pad_maximum_fusion.2), channel_id=1, source_target_pairs={{0,16},{16,0},{32,48},{48,32},{64,80},{80,64},{96,112},{112,96},{1... | collective-permute-start | bytes 399368 | tf_op jit(solution)/shard_map/ppermute | solution.py:52
  70.0 1.9 %collective-permute-start.3 = (f32[128,260]{0,1:T(8,128)S(1)}, f32[128,260]{0,1:T(8,128)S(1)}, u32[]{:S(2)}, u32[]{:S(2)}) collective-permute-start(f32[128,260]{0,1:T(8,128)S(1)} %pad_maximum_fusion.3), channel_id=1, source_target_pairs={{0,20},{4,16},{8,28},{12,24},{16,4},{20,0},{24,12},{28,8},{32,52},... | collective-permute-start | bytes 399368 | tf_op jit(solution)/shard_map/ppermute | solution.py:52
  72.0 3.4 %collective-permute-start.1 = (f32[128,260]{0,1:T(8,128)S(1)}, f32[128,260]{0,1:T(8,128)S(1)}, u32[]{:S(2)}, u32[]{:S(2)}) collective-permute-start(f32[128,260]{0,1:T(8,128)S(1)} %pad_maximum_fusion.1), channel_id=1, source_target_pairs={{0,4},{4,0},{8,12},{12,8},{1,5},{5,1},{9,13},{13,9},{2,6},{6,2},{1... | collective-permute-start | bytes 399368 | tf_op jit(solution)/shard_map/ppermute | solution.py:52
  75.4 0.0 collective-permute-done.2
  75.4 2.3 %collective-permute-done.3 = f32[128,260]{0,1:T(8,128)S(1)} collective-permute-done((f32[128,260]{0,1:T(8,128)S(1)}, f32[128,260]{0,1:T(8,128)S(1)}, u32[]{:S(2)}, u32[]{:S(2)}) %collective-permute-start.3) | collective-permute-done | bytes 133152 | tf_op jit(solution)/shard_map/ppermute | solution.py:52
  77.8 0.0 collective-permute-done.1
  77.8 0.1 divide_convert_fusion
  77.9 0.1 copy.76
  78.1 13.2 %all_to_all.36 = bf16[32,4,256]{2,1,0:T(4,128)(2,1)S(1)} all-to-all(bf16[32,4,256]{2,1,0:T(4,128)(2,1)S(1)} %all_to_all.29), channel_id=1, replica_groups=mesh['seq'=32,'row'=4,'col'=4] {'seq'}, dimensions={0} | all-to-all | bytes 131072 | tf_op jit(solution)/shard_map/all_to_all | solution.py:189
  91.3 0.6 copy.88
  (50 shorter events, 0.8 us)
Async XLA Ops:
  4.8 20.8 %all-to-all-start = ((bf16[32,2,1344]{2,1,0:T(2,128)(2,1)}), bf16[32,2,1344]{2,1,0:T(2,128)(2,1)S(1)}, u32[]{:S(2)}, u32[]{:S(2)}) async-start(bf16[32,2,1344]{2,1,0:T(2,128)(2,1)} %reshape.167), calls=%async_computation | async-start | bytes 360448 | tf_op jit(solution)/shard_map/all_to_all | solution.py:97
  28.5 33.1 %all-to-all-start.1 = ((bf16[16,97,256]{2,1,0:T(8,128)(2,1)}), bf16[16,97,256]{2,1,0:T(8,128)(2,1)S(1)}, u32[]{:S(2)}, u32[]{:S(2)}) async-start(bf16[16,97,256]{2,1,0:T(8,128)(2,1)} %bitcast.15), calls=%async_computation.1 | async-start | bytes 1703936 | tf_op jit(solution)/shard_map/all_to_all | solution.py:141
  40.1 3.3 %collective-permute-start = (bf16[128,514]{1,0:T(8,128)(2,1)S(1)}, bf16[128,514]{1,0:T(8,128)(2,1)S(1)}, u32[]{:S(2)}, u32[]{:S(2)}) collective-permute-start(bf16[128,514]{1,0:T(8,128)(2,1)S(1)} %pad_maximum_fusion), channel_id=1, source_target_pairs={{0,4},{4,0},{8,12},{12,8},{1,5},{5,1},{9,13},{13,9},{2,6},{6,2},{1... | collective-permute-start | bytes 394760 | tf_op jit(solution)/shard_map/ppermute | solution.py:52
  67.5 7.9 %collective-permute-start.2 = (f32[128,260]{0,1:T(8,128)S(1)}, f32[128,260]{0,1:T(8,128)S(1)}, u32[]{:S(2)}, u32[]{:S(2)}) collective-permute-start(f32[128,260]{0,1:T(8,128)S(1)} %pad_maximum_fusion.2), channel_id=1, source_target_pairs={{0,16},{16,0},{32,48},{48,32},{64,80},{80,64},{96,112},{112,96},{1... | collective-permute-start | bytes 399368 | tf_op jit(solution)/shard_map/ppermute | solution.py:52
  70.0 7.7 %collective-permute-start.3 = (f32[128,260]{0,1:T(8,128)S(1)}, f32[128,260]{0,1:T(8,128)S(1)}, u32[]{:S(2)}, u32[]{:S(2)}) collective-permute-start(f32[128,260]{0,1:T(8,128)S(1)} %pad_maximum_fusion.3), channel_id=1, source_target_pairs={{0,20},{4,16},{8,28},{12,24},{16,4},{20,0},{24,12},{28,8},{32,52},... | collective-permute-start | bytes 399368 | tf_op jit(solution)/shard_map/ppermute | solution.py:52
  72.0 5.8 %collective-permute-start.1 = (f32[128,260]{0,1:T(8,128)S(1)}, f32[128,260]{0,1:T(8,128)S(1)}, u32[]{:S(2)}, u32[]{:S(2)}) collective-permute-start(f32[128,260]{0,1:T(8,128)S(1)} %pad_maximum_fusion.1), channel_id=1, source_target_pairs={{0,4},{4,0},{8,12},{12,8},{1,5},{5,1},{9,13},{13,9},{2,6},{6,2},{1... | collective-permute-start | bytes 399368 | tf_op jit(solution)/shard_map/ppermute | solution.py:52

commit v6 on v5

--- a/solution.py
+++ b/solution.py
@@ -156,37 +156,34 @@
         both_q, both_pos, keys, values, key_pos_cache, key_pos_slab, cache_got.shape[0], first_pos
     )
 
-    def block(rows, pair):
-        take = slice(rows * slab_rows, (rows + 1) * slab_rows)
-        heads = pl_heads(pair, heads_dev)
-        return jnp.concatenate(
-            [
-                lax.dynamic_slice_in_dim(summed[take], heads, heads_dev, 1).reshape(slab_rows, -1),
-                lax.dynamic_slice_in_dim(row_max[take], heads, heads_dev, 1),
-                lax.dynamic_slice_in_dim(row_sum[take], heads, heads_dev, 1),
-            ],
-            axis=1,
-        )
-
-    pieces = [
-        block(0, parity),
-        swap(block(1, parity), "row", core_pairs),
-        swap(block(0, 1 - parity), "seq", seq_pairs),
-        swap(block(1, 1 - parity), ("seq", "row"), diag_pairs),
-    ]
-    split_at = heads_dev * HD
-    maxes = [p[:, split_at : split_at + heads_dev] for p in pieces]
-    top = maxes[0]
-    for m in maxes[1:]:
-        top = jnp.maximum(top, m)
-    numerator = 0.0
-    denominator = 0.0
-    for p, m in zip(pieces, maxes):
-        factor = jnp.exp(m - top)
-        numerator = numerator + p[:, :split_at].reshape(slab_rows, heads_dev, HD) * factor[..., None]
-        denominator = denominator + p[:, split_at + heads_dev :] * factor
-    context = (numerator / denominator[..., None]).astype(jnp.bfloat16).reshape(slab_rows, heads_dev * HD)
-    return lax.all_to_all(context, "seq", split_axis=0, concat_axis=1, tiled=True)
+    theirs = jnp.concatenate(
+        [summed[slab_rows:].reshape(slab_rows, -1), row_max[slab_rows:], row_sum[slab_rows:]], axis=1
+    )
+    got = swap(theirs, "row", core_pairs)
+    split_at = pair_heads * HD
+    other_summed = got[:, :split_at].reshape(slab_rows, pair_heads, HD)
+    other_max = got[:, split_at : split_at + pair_heads]
+    other_sum = got[:, split_at + pair_heads :]
+    mine_max = row_max[:slab_rows]
+    top = jnp.maximum(mine_max, other_max)
+    scale_mine = jnp.exp(mine_max - top)
+    scale_other = jnp.exp(other_max - top)
+    numerator = summed[:slab_rows] * scale_mine[..., None] + other_summed * scale_other[..., None]
+    denominator = row_sum[:slab_rows] * scale_mine + other_sum * scale_other
+    partial = jnp.concatenate([numerator.reshape(slab_rows, -1), top, denominator], axis=1)
+
+    back = lax.all_to_all(partial.reshape(seq_count, tok_rows, -1), "seq", 0, 0, tiled=True)
+    back = back.reshape(seq_count // 2, 2, tok_rows, -1)
+    half_num = back[..., :split_at].reshape(seq_count // 2, 2, tok_rows, pair_heads, HD)
+    half_max = back[..., split_at : split_at + pair_heads]
+    half_sum = back[..., split_at + pair_heads :]
+    best = jnp.maximum(half_max[:, 0], half_max[:, 1])
+    f0 = jnp.exp(half_max[:, 0] - best)
+    f1 = jnp.exp(half_max[:, 1] - best)
+    num = half_num[:, 0] * f0[..., None] + half_num[:, 1] * f1[..., None]
+    den = half_sum[:, 0] * f0 + half_sum[:, 1] * f1
+    context = (num / den[..., None]).astype(jnp.bfloat16)
+    return context.transpose(1, 0, 2, 3).reshape(tok_rows, -1)
 
 
 def pl_heads(pair, heads_dev):

time: 92.7 us -> 91.4 us (0.986)
  starting transfers between devices: 30.8 us -> 24.8 us
  blocking collectives: 13.2 us -> 18.1 us
    ppermute x4 -> x2, starting transfers between devices: 10.2 us -> 4.23 us  [swap(): return lax.ppermute(x, axes, pairs)]
    all_to_all x1, blocking collectives: 13.2 us -> 18.1 us  [on_device(): lax.all_to_all(partial.reshape(seq_count, tok_rows, -1), 'seq', 0, 0, til...]
    ppermute x4 -> x2, waiting for transfers between devices: 2.89 us -> 2.05 us  [swap(): return lax.ppermute(x, axes, pairs)]
  transfers between devices with their start and end apart: 6 -> 4, of which waited for: 4 -> 4; matrix products, arithmetic and copies ran while one was open for 3% -> 3% of each run, Pallas kernels for 0% -> 0%
where the time goes in v6:
time: 91.4 us; the launch traced here: 90.9 us
  waiting for transfers between devices  29.4 us (32%)
  starting transfers between devices  24.8 us (27%)
  blocking collectives  18.1 us (20%)
  local copies, waits for them, and re-layouts  9.73 us (11%)
  other arithmetic  4.87 us (5%)
  matrix products  2.81 us (3%)
  between operations  1.14 us (1%)
    all_to_all x1, blocking collectives, on_device(): lax.all_to_all(partial.reshape(seq_count, tok_rows, -1), 'seq', 0, 0, til...  18.1 us
    all_to_all x1, waiting for transfers between devices, on_device(): every = lax.all_to_all(per_dest, cell_axes, 0, 0, tiled=True)  17.7 us
    all_to_all x1, starting transfers between devices, on_device(): every = lax.all_to_all(per_dest, cell_axes, 0, 0, tiled=True)  10.4 us
    all_to_all x1, starting transfers between devices, on_device(): recv = lax.all_to_all(send, 'seq', 0, 0, tiled=True)  10.2 us
    all_to_all x1, waiting for transfers between devices, on_device(): recv = lax.all_to_all(send, 'seq', 0, 0, tiled=True)  9.7 us
    ppermute x2, starting transfers between devices, swap(): return lax.ppermute(x, axes, pairs)  4.23 us
    ppermute x2, waiting for transfers between devices, swap(): return lax.ppermute(x, axes, pairs)  2.05 us
  transfers between devices with their start and end apart: 4, of which 4 were waited for; matrix products, arithmetic and copies ran while one was open for 3% of the time, Pallas kernels for 0%

profile of v6, /device:TPU:8, one launch (start us, length us, event | category | flops | bytes accessed | tf_op | source)
XLA Modules:
  0.0 90.9 jit_solution(16360354640684600280)
XLA Ops:
  0.0 0.7 convert_bitcast_fusion
  0.7 0.1 copy.99
  0.8 0.1 convert_element_type.33
  0.9 0.7 copy_bitcast_fusion.2
  1.7 0.9 broadcast_in_dim.36
  2.7 0.5 broadcast.90
  3.2 0.7 reduce.10
  3.9 0.9 reshape.207
  4.8 10.2 %all-to-all-start = ((bf16[32,2,1344]{2,1,0:T(2,128)(2,1)}), bf16[32,2,1344]{2,1,0:T(2,128)(2,1)S(1)}, u32[]{:S(2)}, u32[]{:S(2)}) async-start(bf16[32,2,1344]{2,1,0:T(2,128)(2,1)} %reshape.207), calls=%async_computation | async-start | bytes 360448 | tf_op jit(solution)/shard_map/all_to_all | solution.py:97
  15.0 0.9 constant_dynamic-slice_fusion.1
  15.9 9.7 %all-to-all-done = bf16[32,2,1344]{2,1,0:T(2,128)(2,1)S(1)} async-done(((bf16[32,2,1344]{2,1,0:T(2,128)(2,1)}), bf16[32,2,1344]{2,1,0:T(2,128)(2,1)S(1)}, u32[]{:S(2)}, u32[]{:S(2)}) %all-to-all-start) | async-done | bytes 172064 | tf_op jit(solution)/shard_map/all_to_all | solution.py:97
  25.6 0.2 reshape.208
  25.8 1.1 %copy.101 = bf16[32,1,2688]{0,2,1:T(8,128)(2,1)S(1)} copy(bf16[32,1,2688]{2,1,0:T(2,128)(2,1)S(1)} %reshape.208) | data formatting | bytes 344064 | tf_op jit(solution)/shard_map/all_to_all | solution.py:97
  26.9 0.1 fusion.39
  27.0 0.1 copy.103
  27.2 0.1 reshape_reshape.10
  27.3 0.1 copy.102
  27.4 0.1 copy.104
  27.6 1.0 %broadcast_in_dim.70 = bf16[2,2,4,97,256]{4,3,2,1,0:T(8,128)(2,1)} broadcast(bf16[2,97,256]{2,1,0:T(8,128)(2,1)S(1)} %pad_maximum_fusion.3), dimensions={1,3,4} | broadcast | bytes 893952 | tf_op jit(solution)/shard_map/broadcast_in_dim | solution.py:138
  28.5 10.4 %all-to-all-start.1 = ((bf16[16,97,256]{2,1,0:T(8,128)(2,1)}), bf16[16,97,256]{2,1,0:T(8,128)(2,1)S(1)}, u32[]{:S(2)}, u32[]{:S(2)}) async-start(bf16[16,97,256]{2,1,0:T(8,128)(2,1)} %bitcast.15), calls=%async_computation.1 | async-start | bytes 1703936 | tf_op jit(solution)/shard_map/all_to_all | solution.py:141
  39.6 0.1 copy.105
  39.7 0.1 reshape_reshape.11
  39.8 0.2 copy.106
  40.0 0.1 reshape_reshape.12
  40.1 2.3 %collective-permute-start = (bf16[128,514]{1,0:T(8,128)(2,1)S(1)}, bf16[128,514]{1,0:T(8,128)(2,1)S(1)}, u32[]{:S(2)}, u32[]{:S(2)}) collective-permute-start(bf16[128,514]{1,0:T(8,128)(2,1)S(1)} %pad_maximum_fusion.2), channel_id=1, source_target_pairs={{0,4},{4,0},{8,12},{12,8},{1,5},{5,1},{9,13},{13,9},{2,6},{6,2},{1... | collective-permute-start | bytes 394760 | tf_op jit(solution)/shard_map/ppermute | solution.py:52
  42.5 0.1 add_compare_fusion
  42.5 0.1 reshape.204
  42.6 0.1 reshape.183
  42.7 0.2 fusion.22
  42.9 0.5 collective-permute-done
  43.5 0.1 copy.108
  43.6 0.1 copy.110
  43.8 0.2 fusion.21
  44.0 17.7 %all-to-all-done.1 = bf16[16,97,256]{2,1,0:T(8,128)(2,1)S(1)} async-done(((bf16[16,97,256]{2,1,0:T(8,128)(2,1)}), bf16[16,97,256]{2,1,0:T(8,128)(2,1)S(1)}, u32[]{:S(2)}, u32[]{:S(2)}) %all-to-all-start.1) | async-done | bytes 794656 | tf_op jit(solution)/shard_map/all_to_all | solution.py:141
  61.7 0.3 reshape.192
  61.9 0.2 fusion.11
  62.3 0.1 broadcast_compare_fusion
  62.5 0.1 pad_add_fusion
  62.6 1.3 %select_reduce_fusion = (f32[256,4]{0,1:T(4,128)S(1)}, f32[256,4,1536]{2,0,1:T(8,128)S(1)}) fusion(pred[256,1536]{1,0:T(8,128)(4,1)S(1)} %pad_add_fusion, bf16[512,128]{1,0:T(8,128)(2,1)S(1)} %get-tuple-element.19, bf16[1024,128]{1,0:T(8,128)(2,1)S(1)} %get-tuple-element.15, bf16[128,4,128]{2,0,1:T(8,128)(2,1)S(1)} %copy.110, bf16[128,4,128]{2,0,1:T(8,128)(2,1)S(1)} %copy.109), kind=kOutput, calls=%fused_computation.1 | convolution fusion | flops 408681472 | bytes 7344128 | tf_op jit(solution)/shard_map/thd,nd->thn/dot_general | solution.py:41
  63.9 1.8 %fusion = f32[256,4]{0,1:T(4,128)S(1)} fusion(f32[256,4,1536]{2,0,1:T(8,128)S(1)} %get-tuple-element.27, f32[256,4]{0,1:T(4,128)S(1)} %get-tuple-element.26, pred[256,1536]{1,0:T(8,128)(4,1)S(1)} %pad_add_fusion), kind=kLoop, calls=%fused_computation.2 | loop fusion | flops 6290432 | bytes 6692864 | tf_op jit(solution)/shard_map/reduce_sum | solution.py:44
  65.8 1.5 %fusion.2 = f32[256,4,128]{0,2,1:T(8,128)S(1)} fusion(f32[256,4,1536]{2,0,1:T(8,128)S(1)} %get-tuple-element.27, f32[256,4]{0,1:T(4,128)S(1)} %get-tuple-element.26, pred[256,1536]{1,0:T(8,128)(4,1)S(1)} %pad_add_fusion, bf16[512,128]{1,0:T(8,128)(2,1)S(1)} %get-tuple-element.18, bf16[1024,128]{1,0:T(8,128)(2,1)S(1)} %get-tuple-element.14), kind=kOutput, calls=%fused_computation.4 | convolution fusion | flops 409731072 | bytes 7606272 | tf_op jit(solution)/shard_map/thn,nd->thd/dot_general | solution.py:45
  67.3 1.9 %collective-permute-start.1 = (f32[128,520]{0,1:T(8,128)S(1)}, f32[128,520]{0,1:T(8,128)S(1)}, u32[]{:S(2)}, u32[]{:S(2)}) collective-permute-start(f32[128,520]{0,1:T(8,128)S(1)} %pad_maximum_fusion.1), channel_id=1, source_target_pairs={{0,4},{4,0},{8,12},{12,8},{1,5},{5,1},{9,13},{13,9},{2,6},{6,2},{1... | collective-permute-start | bytes 798728 | tf_op jit(solution)/shard_map/ppermute | solution.py:52
  69.2 1.5 %collective-permute-done.1 = f32[128,520]{0,1:T(8,128)S(1)} collective-permute-done((f32[128,520]{0,1:T(8,128)S(1)}, f32[128,520]{0,1:T(8,128)S(1)}, u32[]{:S(2)}, u32[]{:S(2)}) %collective-permute-start.1) | collective-permute-done | bytes 266272 | tf_op jit(solution)/shard_map/ppermute | solution.py:52
  70.8 0.1 copy.112
  71.0 0.2 concatenate.58
  71.1 0.1 copy.126
  71.3 0.1 copy.125
  71.4 0.1 pad_maximum_fusion
  71.5 18.1 %all_to_all.22 = f32[32,4,520]{2,1,0:T(4,128)S(1)} all-to-all(f32[32,4,520]{2,1,0:T(4,128)S(1)} %pad_maximum_fusion), channel_id=1, replica_groups=mesh['seq'=32,'row'=4,'col'=4] {'seq'}, dimensions={0} | all-to-all | bytes 532480 | tf_op jit(solution)/shard_map/all_to_all | solution.py:175
  89.6 0.1 fusion.27
  89.7 0.2 reshape.190
  90.0 0.3 fusion.23
  90.2 0.7 reshape.191
  (45 shorter events, 0.7 us)
Async XLA Ops:
  4.8 20.8 %all-to-all-start = ((bf16[32,2,1344]{2,1,0:T(2,128)(2,1)}), bf16[32,2,1344]{2,1,0:T(2,128)(2,1)S(1)}, u32[]{:S(2)}, u32[]{:S(2)}) async-start(bf16[32,2,1344]{2,1,0:T(2,128)(2,1)} %reshape.207), calls=%async_computation | async-start | bytes 360448 | tf_op jit(solution)/shard_map/all_to_all | solution.py:97
  28.5 33.1 %all-to-all-start.1 = ((bf16[16,97,256]{2,1,0:T(8,128)(2,1)}), bf16[16,97,256]{2,1,0:T(8,128)(2,1)S(1)}, u32[]{:S(2)}, u32[]{:S(2)}) async-start(bf16[16,97,256]{2,1,0:T(8,128)(2,1)} %bitcast.15), calls=%async_computation.1 | async-start | bytes 1703936 | tf_op jit(solution)/shard_map/all_to_all | solution.py:141
  40.1 3.3 %collective-permute-start = (bf16[128,514]{1,0:T(8,128)(2,1)S(1)}, bf16[128,514]{1,0:T(8,128)(2,1)S(1)}, u32[]{:S(2)}, u32[]{:S(2)}) collective-permute-start(bf16[128,514]{1,0:T(8,128)(2,1)S(1)} %pad_maximum_fusion.2), channel_id=1, source_target_pairs={{0,4},{4,0},{8,12},{12,8},{1,5},{5,1},{9,13},{13,9},{2,6},{6,2},{1... | collective-permute-start | bytes 394760 | tf_op jit(solution)/shard_map/ppermute | solution.py:52
  67.3 3.4 %collective-permute-start.1 = (f32[128,520]{0,1:T(8,128)S(1)}, f32[128,520]{0,1:T(8,128)S(1)}, u32[]{:S(2)}, u32[]{:S(2)}) collective-permute-start(f32[128,520]{0,1:T(8,128)S(1)} %pad_maximum_fusion.1), channel_id=1, source_target_pairs={{0,4},{4,0},{8,12},{12,8},{1,5},{5,1},{9,13},{13,9},{2,6},{6,2},{1... | collective-permute-start | bytes 798728 | tf_op jit(solution)/shard_map/ppermute | solution.py:52

commit v7 on v6

--- a/solution.py
+++ b/solution.py
@@ -5,6 +5,7 @@
 import jax.numpy as jnp
 from jax import lax
 from jax.sharding import PartitionSpec as P
+from jax.experimental import pallas as pl
 
 HQ = 64
 KVH = 8
@@ -55,6 +56,40 @@
 def decode(codes):
     codes = codes.astype(jnp.float32)
     return codes[..., 0] * code_base + codes[..., 1]
+
+
+def attention_kernel(q_ref, qc_ref, k_ref, v_ref, kc_ref, o_ref, m_ref, l_ref):
+    scores = lax.dot_general(
+        q_ref[...], k_ref[...], (((1,), (1,)), ((), ())), preferred_element_type=jnp.float32
+    ) * (1.0 / math.sqrt(HD))
+    allowed = kc_ref[...] <= qc_ref[...]
+    row_max = jnp.max(jnp.where(allowed, scores, -jnp.inf), axis=1, keepdims=True)
+    exponent = jnp.where(allowed, jnp.exp(scores - row_max), 0.0)
+    l_ref[...] = jnp.sum(exponent, axis=1, keepdims=True)
+    m_ref[...] = row_max
+    o_ref[...] = jnp.dot(exponent.astype(jnp.bfloat16), v_ref[...], preferred_element_type=jnp.float32)
+
+
+def fused_attention(q, q_code, keys, values, key_code, block=256):
+    rows, count = q.shape[0], keys.shape[0]
+    block = min(block, rows)
+    row_spec = pl.BlockSpec((block, HD), lambda i: (i, 0))
+    col_spec = pl.BlockSpec((block, 1), lambda i: (i, 0))
+    whole = pl.BlockSpec((count, HD), lambda i: (0, 0))
+    return pl.pallas_call(
+        attention_kernel,
+        grid=(rows // block,),
+        in_specs=[row_spec, col_spec, whole, whole, pl.BlockSpec((1, count), lambda i: (0, 0))],
+        out_specs=[row_spec, col_spec, col_spec],
+        out_shape=[
+            jax.ShapeDtypeStruct((rows, HD), jnp.float32),
+            jax.ShapeDtypeStruct((rows, 1), jnp.float32),
+            jax.ShapeDtypeStruct((rows, 1), jnp.float32),
+        ],
+        cost_estimate=pl.CostEstimate(
+            flops=4 * rows * count * HD, transcendentals=rows * count, bytes_accessed=2 * (rows + 2 * count) * HD + 4 * rows * HD
+        ),
+    )(q, q_code, keys, values, key_code)
 
 
 def on_device(queries, new_keys, new_values, positions, cache_keys, cache_values, slab_start):
@@ -152,9 +187,14 @@
 
     both_q = jnp.concatenate([query_block, partner_block], axis=0)
     both_pos = jnp.concatenate([own_pos, partner_pos], axis=0)
-    row_max, row_sum, summed = partial_attention(
-        both_q, both_pos, keys, values, key_pos_cache, key_pos_slab, cache_got.shape[0], first_pos
-    )
+    both_rows = both_q.shape[0]
+    cache_code = jnp.where(key_pos_cache < first_pos, -1.0, 1e9).astype(jnp.float32)
+    key_code = jnp.concatenate([cache_code, key_pos_slab])[None, :]
+    q_code = jnp.broadcast_to(both_pos[:, None], (both_rows, pair_heads)).reshape(-1, 1)
+    out, out_max, out_sum = fused_attention(both_q.reshape(-1, HD), q_code, keys, values, key_code)
+    summed = out.reshape(both_rows, pair_heads, HD)
+    row_max = out_max.reshape(both_rows, pair_heads)
+    row_sum = out_sum.reshape(both_rows, pair_heads)
 
     theirs = jnp.concatenate(
         [summed[slab_rows:].reshape(slab_rows, -1), row_max[slab_rows:], row_sum[slab_rows:]], axis=1

time: 91.4 us -> 97.8 us (1.070)
  Pallas kernels: 0 us -> 6.52 us
  local copies, waits for them, and re-layouts: 9.73 us -> 13.6 us
  matrix products: 2.81 us -> 0 us
  waiting for transfers between devices: 29.4 us -> 27.6 us
    pallas_call x0 -> x1, Pallas kernels: none -> 6.52 us  [fused_attention(): pl.pallas_call(attention_kernel, grid=(rows // block,), in_specs=[row_spe...]
    dot_general x2 -> x0, matrix products: 2.81 us -> none  [the longest x1 1.5 us: partial_attention(): jnp.einsum('thn,nd->thd', exponent.astype(jnp.bfloat16), values, preferre...]
    concatenate x1 -> x4, other arithmetic: 0.13 us -> 2.43 us  [the longest x1 0.87 us: on_device(): both_q = jnp.concatenate([query_block, partner_block], axis=0)]
    unnamed x4 -> x14, local copies, waits for them, and re-layouts: 1.11 us -> 3.22 us
    reduce_sum x1 -> x0, other arithmetic: 1.81 us -> none  [partial_attention(): row_sum = jnp.sum(exponent, axis=-1)]
    all_to_all x1, waiting for transfers between devices: 17.7 us -> 16 us  [on_device(): every = lax.all_to_all(per_dest, cell_axes, 0, 0, tiled=True)]
    slice x2 -> x5, local copies, waits for them, and re-layouts: 0.04 us -> 1.58 us  [the longest x2 1.16 us: on_device(): summed[:slab_rows] * scale_mine[..., None]]
    reshape x0 -> x2, local copies, waits for them, and re-layouts: none -> 1.01 us  [the longest x1 0.97 us: on_device(): jnp.broadcast_to(both_pos[:, None], (both_rows, pair_heads)).reshape(-1, 1)]
  transfers between devices with their start and end apart: 4 -> 4, of which waited for: 4 -> 4; matrix products, arithmetic and copies ran while one was open for 3% -> 4% of each run, Pallas kernels for 0% -> 0%
where the time goes in v7:
time: 97.8 us; the launch traced here: 97.2 us
  waiting for transfers between devices  27.6 us (28%)
  starting transfers between devices  24.8 us (25%)
  blocking collectives  18.1 us (19%)
  local copies, waits for them, and re-layouts  13.6 us (14%)
  Pallas kernels  6.52 us (7%)
  other arithmetic  5.41 us (6%)
  between operations  1.17 us (1%)
    all_to_all x1, blocking collectives, on_device(): lax.all_to_all(partial.reshape(seq_count, tok_rows, -1), 'seq', 0, 0, til...  18.1 us
    all_to_all x1, waiting for transfers between devices, on_device(): every = lax.all_to_all(per_dest, cell_axes, 0, 0, tiled=True)  16 us
    all_to_all x1, starting transfers between devices, on_device(): every = lax.all_to_all(per_dest, cell_axes, 0, 0, tiled=True)  10.4 us
    all_to_all x1, starting transfers between devices, on_device(): recv = lax.all_to_all(send, 'seq', 0, 0, tiled=True)  10.2 us
    all_to_all x1, waiting for transfers between devices, on_device(): recv = lax.all_to_all(send, 'seq', 0, 0, tiled=True)  9.7 us
    pallas_call x1, Pallas kernels, fused_attention(): pl.pallas_call(attention_kernel, grid=(rows // block,), in_specs=[row_spe...  6.52 us
    ppermute x2, starting transfers between devices, swap(): return lax.ppermute(x, axes, pairs)  4.23 us
    unnamed x14, local copies, waits for them, and re-layouts  3.22 us
  transfers between devices with their start and end apart: 4, of which 4 were waited for; matrix products, arithmetic and copies ran while one was open for 4% of the time, Pallas kernels for 0%

profile of v7, /device:TPU:8, one launch (start us, length us, event | category | flops | bytes accessed | tf_op | source)
XLA Modules:
  0.0 97.2 jit_solution(4675226001047111916)
XLA Ops:
  0.0 0.7 convert_bitcast_fusion
  0.7 0.1 copy.75
  0.8 0.1 convert_element_type.30
  0.9 0.5 copy-done.3
  1.5 0.8 copy-done.2
  2.4 0.5 broadcast.88
  2.9 0.7 reduce.18
  3.6 0.9 reshape.208
  4.5 10.2 %all-to-all-start = ((bf16[32,2,1344]{2,1,0:T(2,128)(2,1)}), bf16[32,2,1344]{2,1,0:T(2,128)(2,1)S(1)}, u32[]{:S(2)}, u32[]{:S(2)}) async-start(bf16[32,2,1344]{2,1,0:T(2,128)(2,1)} %reshape.208), calls=%async_computation | async-start | bytes 360448 | tf_op jit(solution)/shard_map/all_to_all | solution.py:132
  14.7 0.9 constant_dynamic-slice_fusion.1
  15.6 9.7 %all-to-all-done = bf16[32,2,1344]{2,1,0:T(2,128)(2,1)S(1)} async-done(((bf16[32,2,1344]{2,1,0:T(2,128)(2,1)}), bf16[32,2,1344]{2,1,0:T(2,128)(2,1)S(1)}, u32[]{:S(2)}, u32[]{:S(2)}) %all-to-all-start) | async-done | bytes 172064 | tf_op jit(solution)/shard_map/all_to_all | solution.py:132
  25.3 0.2 reshape.209
  25.6 1.1 %copy.77 = bf16[32,1,2688]{0,2,1:T(8,128)(2,1)S(1)} copy(bf16[32,1,2688]{2,1,0:T(2,128)(2,1)S(1)} %reshape.209) | data formatting | bytes 344064 | tf_op jit(solution)/shard_map/all_to_all | solution.py:132
  26.7 0.1 fusion.23
  26.8 0.1 copy.82
  26.9 0.1 reshape_reshape.12
  27.0 0.1 copy.81
  27.1 0.1 copy.83
  27.3 1.0 broadcast_in_dim.59
  28.3 10.4 %all-to-all-start.1 = ((bf16[16,97,256]{2,1,0:T(8,128)(2,1)}), bf16[16,97,256]{2,1,0:T(8,128)(2,1)S(1)}, u32[]{:S(2)}, u32[]{:S(2)}) async-start(bf16[16,97,256]{2,1,0:T(8,128)(2,1)} %bitcast.15), calls=%async_computation.1 | async-start | bytes 1703936 | tf_op jit(solution)/shard_map/all_to_all | solution.py:176
  39.4 0.1 copy.80
  39.5 0.1 reshape_reshape.11
  39.6 0.2 copy.78
  39.8 0.1 reshape_reshape.10
  39.9 2.3 %collective-permute-start = (bf16[128,514]{1,0:T(8,128)(2,1)S(1)}, bf16[128,514]{1,0:T(8,128)(2,1)S(1)}, u32[]{:S(2)}, u32[]{:S(2)}) collective-permute-start(bf16[128,514]{1,0:T(8,128)(2,1)S(1)} %pad_maximum_fusion.5), channel_id=1, source_target_pairs={{0,4},{4,0},{8,12},{12,8},{1,5},{5,1},{9,13},{13,9},{2,6},{6,2},{1... | collective-permute-start | bytes 394760 | tf_op jit(solution)/shard_map/ppermute | solution.py:53
  42.2 0.1 fusion.18
  42.3 0.1 select_n.52
  42.4 0.1 reshape.178
  42.4 0.2 fusion.10
  42.6 0.6 collective-permute-done
  43.3 0.2 fusion.9
  43.5 0.1 broadcast_in_dim.58
  43.6 1.0 reshape.191.qc_ref
  44.5 0.9 pad_maximum_fusion.4
  45.4 16.0 %all-to-all-done.1 = bf16[16,97,256]{2,1,0:T(8,128)(2,1)S(1)} async-done(((bf16[16,97,256]{2,1,0:T(8,128)(2,1)}), bf16[16,97,256]{2,1,0:T(8,128)(2,1)S(1)}, u32[]{:S(2)}, u32[]{:S(2)}) %all-to-all-start.1) | async-done | bytes 794656 | tf_op jit(solution)/shard_map/all_to_all | solution.py:176
  61.4 0.3 reshape.190
  61.7 0.2 fusion.1
  61.9 0.6 broadcast_in_dim.62.kc_ref
  62.7 0.8 pad_maximum_fusion.1.v_ref
  63.5 0.8 pad_maximum_fusion.k_ref
  64.2 6.5 %shard_map.73 = (f32[1024,128]{1,0:T(8,128)}, f32[1024,1]{1,0:T(8,128)}, f32[1024,1]{1,0:T(8,128)}) custom-call(bf16[1024,128]{1,0:T(8,128)(2,1)} %bitcast.127, f32[1024,1]{1,0:T(8,128)} %reshape.191.qc_ref, bf16[1536,128]{1,0:T(8,128)(2,1)} %pad_maximum_fusion.k_ref, bf16[1536,128]{1,0:T(8,128)(2,1)} %pad_maximum_fusion.1.v_ref, ...), custom_call_target="tpu_custom_call" | custom-call | flops 805306368 | bytes 1572864 | tf_op jit(solution)/shard_map/pallas_call | solution.py:79
  70.7 1.1 %fusion.24 = (f32[512,128]{1,0:T(8,128)S(1)}, f32[512,128]{1,0:T(8,128)S(1)}) fusion(f32[1024,128]{1,0:T(8,128)} %get-tuple-element.8), kind=kLoop, calls=%fused_computation.80 | loop fusion | bytes 1048576 | tf_op jit(solution)/shard_map/slice | solution.py:211
  71.9 0.1 copy-done.1
  71.9 0.2 slice_reduce_fusion.2
  72.2 0.8 copy-done
  72.9 0.2 slice_reduce_fusion
  73.1 0.1 slice.181
  73.3 0.1 slice.183
  73.4 0.1 pad_maximum_fusion.2
  73.5 1.9 %collective-permute-start.1 = (f32[128,520]{1,0:T(8,128)S(1)}, f32[128,520]{1,0:T(8,128)S(1)}, u32[]{:S(2)}, u32[]{:S(2)}) collective-permute-start(f32[128,520]{1,0:T(8,128)S(1)} %pad_maximum_fusion.2), channel_id=1, source_target_pairs={{0,4},{4,0},{8,12},{12,8},{1,5},{5,1},{9,13},{13,9},{2,6},{6,2},{1... | collective-permute-start | bytes 798728 | tf_op jit(solution)/shard_map/ppermute | solution.py:53
  75.5 0.1 slice.187
  75.6 0.1 slice.178
  75.7 1.3 %collective-permute-done.1 = f32[128,520]{1,0:T(8,128)S(1)} collective-permute-done((f32[128,520]{1,0:T(8,128)S(1)}, f32[128,520]{1,0:T(8,128)S(1)}, u32[]{:S(2)}, u32[]{:S(2)}) %collective-permute-start.1) | collective-permute-done | bytes 266272 | tf_op jit(solution)/shard_map/ppermute | solution.py:53
  77.0 0.1 fusion.8
  77.1 0.2 mul.109
  77.3 0.2 mul.112
  77.5 0.1 fusion
  77.6 0.1 concatenate.58
  77.7 0.1 pad_maximum_fusion.3
  77.8 18.1 %all_to_all.22 = f32[32,4,520]{2,1,0:T(4,128)S(1)} all-to-all(f32[32,4,520]{2,1,0:T(4,128)S(1)} %pad_maximum_fusion.3), channel_id=1, replica_groups=mesh['seq'=32,'row'=4,'col'=4] {'seq'}, dimensions={0} | all-to-all | bytes 532480 | tf_op jit(solution)/shard_map/all_to_all | solution.py:215
  95.9 0.1 fusion.15
  96.1 0.2 reshape.192
  96.3 0.3 fusion.11
  96.6 0.7 reshape.189
  (48 shorter events, 0.7 us)
Async XLA Ops:
  0.0 0.9 copy-start.4
  0.7 0.7 copy-start.3
  1.4 0.8 copy-start.2
  4.5 20.8 %all-to-all-start = ((bf16[32,2,1344]{2,1,0:T(2,128)(2,1)}), bf16[32,2,1344]{2,1,0:T(2,128)(2,1)S(1)}, u32[]{:S(2)}, u32[]{:S(2)}) async-start(bf16[32,2,1344]{2,1,0:T(2,128)(2,1)} %reshape.208), calls=%async_computation | async-start | bytes 360448 | tf_op jit(solution)/shard_map/all_to_all | solution.py:132
  28.3 33.1 %all-to-all-start.1 = ((bf16[16,97,256]{2,1,0:T(8,128)(2,1)}), bf16[16,97,256]{2,1,0:T(8,128)(2,1)S(1)}, u32[]{:S(2)}, u32[]{:S(2)}) async-start(bf16[16,97,256]{2,1,0:T(8,128)(2,1)} %bitcast.15), calls=%async_computation.1 | async-start | bytes 1703936 | tf_op jit(solution)/shard_map/all_to_all | solution.py:176
  39.9 3.3 %collective-permute-start = (bf16[128,514]{1,0:T(8,128)(2,1)S(1)}, bf16[128,514]{1,0:T(8,128)(2,1)S(1)}, u32[]{:S(2)}, u32[]{:S(2)}) collective-permute-start(bf16[128,514]{1,0:T(8,128)(2,1)S(1)} %pad_maximum_fusion.5), channel_id=1, source_target_pairs={{0,4},{4,0},{8,12},{12,8},{1,5},{5,1},{9,13},{13,9},{2,6},{6,2},{1... | collective-permute-start | bytes 394760 | tf_op jit(solution)/shard_map/ppermute | solution.py:53
  70.7 1.2 %copy-start.1 = (f32[1024,1]{1,0:T(8,128)S(1)}, f32[1024,1]{1,0:T(8,128)}, u32[]{:S(2)}) copy-start(f32[1024,1]{1,0:T(8,128)} %get-tuple-element.9) | copy-start | bytes 12292
  71.9 1.1 %copy-start = (f32[1024,1]{1,0:T(8,128)S(1)}, f32[1024,1]{1,0:T(8,128)}, u32[]{:S(2)}) copy-start(f32[1024,1]{1,0:T(8,128)} %get-tuple-element.10) | copy-start | bytes 12292
  73.5 3.5 %collective-permute-start.1 = (f32[128,520]{1,0:T(8,128)S(1)}, f32[128,520]{1,0:T(8,128)S(1)}, u32[]{:S(2)}, u32[]{:S(2)}) collective-permute-start(f32[128,520]{1,0:T(8,128)S(1)} %pad_maximum_fusion.2), channel_id=1, source_target_pairs={{0,4},{4,0},{8,12},{12,8},{1,5},{5,1},{9,13},{13,9},{2,6},{6,2},{1... | collective-permute-start | bytes 798728 | tf_op jit(solution)/shard_map/ppermute | solution.py:53

commit v8 on v6

--- a/solution.py
+++ b/solution.py
@@ -170,20 +170,38 @@
     scale_other = jnp.exp(other_max - top)
     numerator = summed[:slab_rows] * scale_mine[..., None] + other_summed * scale_other[..., None]
     denominator = row_sum[:slab_rows] * scale_mine + other_sum * scale_other
-    partial = jnp.concatenate([numerator.reshape(slab_rows, -1), top, denominator], axis=1)
+    normed = (numerator / denominator[..., None]).astype(jnp.bfloat16).reshape(slab_rows, -1)
+    log_weight = top + jnp.log(denominator)
+    pieces = []
+    rest = log_weight
+    for _ in range(3):
+        piece = lax.reduce_precision(rest, exponent_bits=8, mantissa_bits=7)
+        pieces.append(piece.astype(jnp.bfloat16))
+        rest = rest - piece
+    coded = jnp.stack(pieces, axis=1).reshape(slab_rows, -1)
+    code_width = 128 * pl_cdiv(coded.shape[1], 128)
+    coded = jnp.pad(coded, ((0, 0), (0, code_width - coded.shape[1])))
+    partial = jnp.concatenate([normed, coded], axis=1)
 
     back = lax.all_to_all(partial.reshape(seq_count, tok_rows, -1), "seq", 0, 0, tiled=True)
     back = back.reshape(seq_count // 2, 2, tok_rows, -1)
-    half_num = back[..., :split_at].reshape(seq_count // 2, 2, tok_rows, pair_heads, HD)
-    half_max = back[..., split_at : split_at + pair_heads]
-    half_sum = back[..., split_at + pair_heads :]
-    best = jnp.maximum(half_max[:, 0], half_max[:, 1])
-    f0 = jnp.exp(half_max[:, 0] - best)
-    f1 = jnp.exp(half_max[:, 1] - best)
-    num = half_num[:, 0] * f0[..., None] + half_num[:, 1] * f1[..., None]
-    den = half_sum[:, 0] * f0 + half_sum[:, 1] * f1
-    context = (num / den[..., None]).astype(jnp.bfloat16)
+    half_num = back[..., :split_at].astype(jnp.float32).reshape(seq_count // 2, 2, tok_rows, pair_heads, HD)
+    half_log = (
+        back[..., split_at : split_at + 3 * pair_heads]
+        .astype(jnp.float32)
+        .reshape(seq_count // 2, 2, tok_rows, 3, pair_heads)
+        .sum(axis=3)
+    )
+    best = jnp.maximum(half_log[:, 0], half_log[:, 1])
+    w0 = jnp.exp(half_log[:, 0] - best)
+    w1 = jnp.exp(half_log[:, 1] - best)
+    num = half_num[:, 0] * w0[..., None] + half_num[:, 1] * w1[..., None]
+    context = (num / (w0 + w1)[..., None]).astype(jnp.bfloat16)
     return context.transpose(1, 0, 2, 3).reshape(tok_rows, -1)
+
+
+def pl_cdiv(a, b):
+    return (a + b - 1) // b
 
 
 def pl_heads(pair, heads_dev):

time: 91.4 us -> 88.5 us (0.968)
  blocking collectives: 18.1 us -> 14.9 us
    all_to_all x1, blocking collectives: 18.1 us -> 14.9 us  [on_device(): lax.all_to_all(partial.reshape(seq_count, tok_rows, -1), 'seq', 0, 0, til...]
where the time goes in v8:
time: 88.5 us; the launch traced here: 88 us
  waiting for transfers between devices  29.4 us (33%)
  starting transfers between devices  24.8 us (28%)
  blocking collectives  14.9 us (17%)
  local copies, waits for them, and re-layouts  9.99 us (11%)
  other arithmetic  4.82 us (5%)
  matrix products  2.81 us (3%)
  between operations  1.14 us (1%)
    all_to_all x1, waiting for transfers between devices, on_device(): every = lax.all_to_all(per_dest, cell_axes, 0, 0, tiled=True)  17.7 us
    all_to_all x1, blocking collectives, on_device(): lax.all_to_all(partial.reshape(seq_count, tok_rows, -1), 'seq', 0, 0, til...  14.9 us
    all_to_all x1, starting transfers between devices, on_device(): every = lax.all_to_all(per_dest, cell_axes, 0, 0, tiled=True)  10.4 us
    all_to_all x1, starting transfers between devices, on_device(): recv = lax.all_to_all(send, 'seq', 0, 0, tiled=True)  10.2 us
    all_to_all x1, waiting for transfers between devices, on_device(): recv = lax.all_to_all(send, 'seq', 0, 0, tiled=True)  9.7 us
    ppermute x2, starting transfers between devices, swap(): return lax.ppermute(x, axes, pairs)  4.23 us
    ppermute x2, waiting for transfers between devices, swap(): return lax.ppermute(x, axes, pairs)  2.05 us
    reduce_sum x1, other arithmetic, partial_attention(): row_sum = jnp.sum(exponent, axis=-1)  1.81 us
  transfers between devices with their start and end apart: 4, of which 4 were waited for; matrix products, arithmetic and copies ran while one was open for 3% of the time, Pallas kernels for 0%

profile of v8, /device:TPU:8, one launch (start us, length us, event | category | flops | bytes accessed | tf_op | source)
XLA Modules:
  0.0 88.0 jit_solution(2725875818832918640)
XLA Ops:
  0.0 0.7 convert_bitcast_fusion
  0.7 0.1 copy.77
  0.8 0.1 convert_element_type.49
  0.9 0.7 copy_bitcast_fusion.2
  1.7 0.9 broadcast_in_dim.36
  2.7 0.5 broadcast.93
  3.2 0.7 reduce.10
  3.9 0.9 reshape.218
  4.8 10.2 %all-to-all-start = ((bf16[32,2,1344]{2,1,0:T(2,128)(2,1)}), bf16[32,2,1344]{2,1,0:T(2,128)(2,1)S(1)}, u32[]{:S(2)}, u32[]{:S(2)}) async-start(bf16[32,2,1344]{2,1,0:T(2,128)(2,1)} %reshape.218), calls=%async_computation | async-start | bytes 360448 | tf_op jit(solution)/shard_map/all_to_all | solution.py:97
  15.0 0.9 %constant_dynamic-slice_fusion.1 = (bf16[256,128]{1,0:T(8,128)(2,1)S(1)}, bf16[256,128]{1,0:T(8,128)(2,1)S(1)}) fusion(bf16[256,1024]{1,0:T(8,128)(2,1)} %param.12, s32[]{:T(128)S(6)} %select_n.46, bf16[256,1024]{1,0:T(8,128)(2,1)} %param.11), kind=kLoop, calls=%fused_computation.81 | loop fusion | bytes 262148 | tf_op jit(solution)/shard_map/dynamic_slice | solution.py:116
  15.9 9.7 %all-to-all-done = bf16[32,2,1344]{2,1,0:T(2,128)(2,1)S(1)} async-done(((bf16[32,2,1344]{2,1,0:T(2,128)(2,1)}), bf16[32,2,1344]{2,1,0:T(2,128)(2,1)S(1)}, u32[]{:S(2)}, u32[]{:S(2)}) %all-to-all-start) | async-done | bytes 172064 | tf_op jit(solution)/shard_map/all_to_all | solution.py:97
  25.6 0.2 reshape.219
  25.8 1.1 %copy.79 = bf16[32,1,2688]{0,2,1:T(8,128)(2,1)S(1)} copy(bf16[32,1,2688]{2,1,0:T(2,128)(2,1)S(1)} %reshape.219) | data formatting | bytes 344064 | tf_op jit(solution)/shard_map/all_to_all | solution.py:97
  26.9 0.1 fusion.45
  27.0 0.1 copy.81
  27.2 0.1 reshape_reshape.10
  27.3 0.1 copy.80
  27.4 0.1 copy.82
  27.6 1.0 %broadcast_in_dim.71 = bf16[2,2,4,97,256]{4,3,2,1,0:T(8,128)(2,1)} broadcast(bf16[2,97,256]{2,1,0:T(8,128)(2,1)S(1)} %pad_maximum_fusion.3), dimensions={1,3,4} | broadcast | bytes 893952 | tf_op jit(solution)/shard_map/broadcast_in_dim | solution.py:138
  28.5 10.4 %all-to-all-start.1 = ((bf16[16,97,256]{2,1,0:T(8,128)(2,1)}), bf16[16,97,256]{2,1,0:T(8,128)(2,1)S(1)}, u32[]{:S(2)}, u32[]{:S(2)}) async-start(bf16[16,97,256]{2,1,0:T(8,128)(2,1)} %bitcast.15), calls=%async_computation.1 | async-start | bytes 1703936 | tf_op jit(solution)/shard_map/all_to_all | solution.py:141
  39.6 0.1 copy.83
  39.7 0.1 reshape_reshape.11
  39.8 0.2 copy.84
  40.0 0.1 reshape_reshape.12
  40.1 2.3 %collective-permute-start = (bf16[128,514]{1,0:T(8,128)(2,1)S(1)}, bf16[128,514]{1,0:T(8,128)(2,1)S(1)}, u32[]{:S(2)}, u32[]{:S(2)}) collective-permute-start(bf16[128,514]{1,0:T(8,128)(2,1)S(1)} %pad_maximum_fusion.1), channel_id=1, source_target_pairs={{0,4},{4,0},{8,12},{12,8},{1,5},{5,1},{9,13},{13,9},{2,6},{6,2},{1... | collective-permute-start | bytes 394760 | tf_op jit(solution)/shard_map/ppermute | solution.py:52
  42.5 0.1 add_compare_fusion
  42.5 0.1 reshape.214
  42.6 0.1 reshape.185
  42.7 0.2 fusion.24
  42.9 0.5 collective-permute-done
  43.5 0.1 copy.86
  43.6 0.1 copy.88
  43.8 0.2 fusion.23
  44.0 17.7 %all-to-all-done.1 = bf16[16,97,256]{2,1,0:T(8,128)(2,1)S(1)} async-done(((bf16[16,97,256]{2,1,0:T(8,128)(2,1)}), bf16[16,97,256]{2,1,0:T(8,128)(2,1)S(1)}, u32[]{:S(2)}, u32[]{:S(2)}) %all-to-all-start.1) | async-done | bytes 794656 | tf_op jit(solution)/shard_map/all_to_all | solution.py:141
  61.7 0.3 reshape.198
  61.9 0.2 fusion.12
  62.3 0.1 broadcast_compare_fusion
  62.5 0.1 pad_add_fusion
  62.6 1.3 %select_reduce_fusion = (f32[256,4]{0,1:T(4,128)S(1)}, f32[256,4,1536]{2,0,1:T(8,128)S(1)}) fusion(pred[256,1536]{1,0:T(8,128)(4,1)S(1)} %pad_add_fusion, bf16[512,128]{1,0:T(8,128)(2,1)S(1)} %get-tuple-element.20, bf16[1024,128]{1,0:T(8,128)(2,1)S(1)} %get-tuple-element.16, bf16[128,4,128]{2,0,1:T(8,128)(2,1)S(1)} %copy.88, bf16[128,4,128]{2,0,1:T(8,128)(2,1)S(1)} %copy.87), kind=kOutput, calls=%fused_computation.1 | convolution fusion | flops 408681472 | bytes 7344128 | tf_op jit(solution)/shard_map/thd,nd->thn/dot_general | solution.py:41
  63.9 1.8 %fusion = f32[256,4]{0,1:T(4,128)S(1)} fusion(f32[256,4,1536]{2,0,1:T(8,128)S(1)} %get-tuple-element.30, f32[256,4]{0,1:T(4,128)S(1)} %get-tuple-element.29, pred[256,1536]{1,0:T(8,128)(4,1)S(1)} %pad_add_fusion), kind=kLoop, calls=%fused_computation.2 | loop fusion | flops 6290432 | bytes 6692864 | tf_op jit(solution)/shard_map/reduce_sum | solution.py:44
  65.8 1.5 %fusion.2 = f32[256,4,128]{0,2,1:T(8,128)S(1)} fusion(f32[256,4,1536]{2,0,1:T(8,128)S(1)} %get-tuple-element.30, f32[256,4]{0,1:T(4,128)S(1)} %get-tuple-element.29, pred[256,1536]{1,0:T(8,128)(4,1)S(1)} %pad_add_fusion, bf16[512,128]{1,0:T(8,128)(2,1)S(1)} %get-tuple-element.19, bf16[1024,128]{1,0:T(8,128)(2,1)S(1)} %get-tuple-element.15), kind=kOutput, calls=%fused_computation.4 | convolution fusion | flops 409731072 | bytes 7606272 | tf_op jit(solution)/shard_map/thn,nd->thd/dot_general | solution.py:45
  67.3 1.9 %collective-permute-start.1 = (f32[128,520]{0,1:T(8,128)S(1)}, f32[128,520]{0,1:T(8,128)S(1)}, u32[]{:S(2)}, u32[]{:S(2)}) collective-permute-start(f32[128,520]{0,1:T(8,128)S(1)} %pad_maximum_fusion), channel_id=1, source_target_pairs={{0,4},{4,0},{8,12},{12,8},{1,5},{5,1},{9,13},{13,9},{2,6},{6,2},{1... | collective-permute-start | bytes 798728 | tf_op jit(solution)/shard_map/ppermute | solution.py:52
  69.2 1.5 %collective-permute-done.1 = f32[128,520]{0,1:T(8,128)S(1)} collective-permute-done((f32[128,520]{0,1:T(8,128)S(1)}, f32[128,520]{0,1:T(8,128)S(1)}, u32[]{:S(2)}, u32[]{:S(2)}) %collective-permute-start.1) | collective-permute-done | bytes 266272 | tf_op jit(solution)/shard_map/ppermute | solution.py:52
  70.8 0.1 fusion.16
  70.9 0.1 copy.90
  71.0 0.1 concatenate.56
  71.1 0.1 copy.103
  71.3 0.1 pad_maximum_fusion.2
  71.4 14.9 %all_to_all.22 = bf16[32,4,640]{2,1,0:T(4,128)(2,1)S(1)} all-to-all(bf16[32,4,640]{2,1,0:T(4,128)(2,1)S(1)} %pad_maximum_fusion.2), channel_id=1, replica_groups=mesh['seq'=32,'row'=4,'col'=4] {'seq'}, dimensions={0} | all-to-all | bytes 327680 | tf_op jit(solution)/shard_map/all_to_all | solution.py:186
  86.3 0.1 copy.101
  86.5 0.1 copy.97
  86.6 0.1 copy.96
  86.7 0.1 copy.94
  86.8 0.2 reshape.200
  87.0 0.3 fusion.25
  87.3 0.7 reshape.197
  (48 shorter events, 0.8 us)
Async XLA Ops:
  4.8 20.8 %all-to-all-start = ((bf16[32,2,1344]{2,1,0:T(2,128)(2,1)}), bf16[32,2,1344]{2,1,0:T(2,128)(2,1)S(1)}, u32[]{:S(2)}, u32[]{:S(2)}) async-start(bf16[32,2,1344]{2,1,0:T(2,128)(2,1)} %reshape.218), calls=%async_computation | async-start | bytes 360448 | tf_op jit(solution)/shard_map/all_to_all | solution.py:97
  28.5 33.1 %all-to-all-start.1 = ((bf16[16,97,256]{2,1,0:T(8,128)(2,1)}), bf16[16,97,256]{2,1,0:T(8,128)(2,1)S(1)}, u32[]{:S(2)}, u32[]{:S(2)}) async-start(bf16[16,97,256]{2,1,0:T(8,128)(2,1)} %bitcast.15), calls=%async_computation.1 | async-start | bytes 1703936 | tf_op jit(solution)/shard_map/all_to_all | solution.py:141
  40.1 3.3 %collective-permute-start = (bf16[128,514]{1,0:T(8,128)(2,1)S(1)}, bf16[128,514]{1,0:T(8,128)(2,1)S(1)}, u32[]{:S(2)}, u32[]{:S(2)}) collective-permute-start(bf16[128,514]{1,0:T(8,128)(2,1)S(1)} %pad_maximum_fusion.1), channel_id=1, source_target_pairs={{0,4},{4,0},{8,12},{12,8},{1,5},{5,1},{9,13},{13,9},{2,6},{6,2},{1... | collective-permute-start | bytes 394760 | tf_op jit(solution)/shard_map/ppermute | solution.py:52
  67.3 3.4 %collective-permute-start.1 = (f32[128,520]{0,1:T(8,128)S(1)}, f32[128,520]{0,1:T(8,128)S(1)}, u32[]{:S(2)}, u32[]{:S(2)}) collective-permute-start(f32[128,520]{0,1:T(8,128)S(1)} %pad_maximum_fusion), channel_id=1, source_target_pairs={{0,4},{4,0},{8,12},{12,8},{1,5},{5,1},{9,13},{13,9},{2,6},{6,2},{1... | collective-permute-start | bytes 798728 | tf_op jit(solution)/shard_map/ppermute | solution.py:52

commit v9 on v8

--- a/solution.py
+++ b/solution.py
@@ -69,25 +69,22 @@
     first_pos = slab_start[0]
     seq_index = lax.axis_index("seq")
     kv_first = seq_index * heads_dev // group_size
-    parity = seq_index % 2
+    quad = group_size // heads_dev
+    quads = seq_count // quad
+    u = seq_index % quad
     core = lax.axis_index("row") % 2
-    quarter = parity * 2 + core
+    part = u * 2 + core
+    parts = quad * 2
     core_pairs = [(r, r ^ 1) for r in range(row_count)]
-    seq_pairs = [(q, q ^ 1) for q in range(seq_count)]
-    diag_pairs = [(q * row_count + r, (q ^ 1) * row_count + (r ^ 1)) for q in range(seq_count) for r in range(row_count)]
     width = 2 * HD
-    pair_heads = 2 * heads_dev
-    half_tok = tok_rows // 2
-
-    q_pairs = queries.reshape(tok_rows, seq_count // 2, 1, pair_heads * HD)
-    q_part = jnp.broadcast_to(q_pairs, (tok_rows, seq_count // 2, 2, pair_heads * HD)).reshape(tok_rows, seq_count, -1)
+    quad_heads = group_size
+
+    q_quads = queries.reshape(tok_rows, quads, 1, quad_heads * HD)
+    q_part = jnp.broadcast_to(q_quads, (tok_rows, quads, quad, quad_heads * HD)).reshape(tok_rows, seq_count, -1)
     kv_local = jnp.concatenate(
-        [new_keys.reshape(tok_rows, KVH, 1, HD), new_values.reshape(tok_rows, KVH, 1, HD)], axis=2
-    ).reshape(2, half_tok, KVH, 1, width)
-    repeat = seq_count // (2 * KVH)
-    kv_part = jnp.broadcast_to(
-        kv_local.transpose(2, 3, 0, 1, 4)[:, :, None], (KVH, 1, repeat, 2, half_tok, width)
-    ).reshape(seq_count, half_tok * width)
+        [new_keys.reshape(tok_rows, KVH, HD), new_values.reshape(tok_rows, KVH, HD)], axis=2
+    )
+    kv_part = kv_local.transpose(1, 0, 2).reshape(seq_count, width)
     codes = jnp.stack([positions // code_base, positions % code_base], axis=1).astype(jnp.bfloat16)
     codes = jnp.pad(codes.reshape(1, tok_rows * 2), ((0, 0), (0, 128 - tok_rows * 2)))
     send = jnp.concatenate(
@@ -95,20 +92,19 @@
         axis=1,
     )
     recv = lax.all_to_all(send, "seq", 0, 0, tiled=True)
-    q_len = tok_rows * pair_heads * HD
-    kvp_len = half_tok * width
+    q_len = tok_rows * quad_heads * HD
     slab_rows = seq_count * tok_rows
-    query_block = recv[:, :q_len].reshape(slab_rows, pair_heads, HD)
-    slab_kv = recv[:, q_len : q_len + kvp_len].reshape(seq_count * half_tok, width)
-    got_codes = recv[:, q_len + kvp_len : q_len + kvp_len + tok_rows * 2].reshape(seq_count, tok_rows, 2)
+    query_block = recv[:, :q_len].reshape(slab_rows, quad_heads, HD)
+    slab_kv = recv[:, q_len : q_len + width]
+    got_codes = recv[:, q_len + width : q_len + width + tok_rows * 2].reshape(seq_count, tok_rows, 2)
     own_pos = decode(got_codes.reshape(slab_rows, 2))
-    slab_codes = lax.dynamic_slice_in_dim(got_codes, parity * half_tok, half_tok, 1).reshape(seq_count * half_tok, 2)
+    slab_codes = lax.dynamic_index_in_dim(got_codes, u, 1, keepdims=False)
 
     partner_q = swap(
         jnp.concatenate([query_block.reshape(slab_rows, -1), got_codes.reshape(slab_rows, 2)], axis=1), "row", core_pairs
     )
-    partner_block = partner_q[:, : pair_heads * HD].reshape(slab_rows, pair_heads, HD)
-    partner_pos = decode(partner_q[:, pair_heads * HD :])
+    partner_block = partner_q[:, : quad_heads * HD].reshape(slab_rows, quad_heads, HD)
+    partner_pos = decode(partner_q[:, quad_heads * HD :])
 
     cache_block = jnp.concatenate(
         [
@@ -118,10 +114,10 @@
         axis=1,
     )
     cache_len = cache_block.shape[0]
-    part_cache = cache_len // 4
-    half_slab = slab_kv.shape[0] // 2
+    part_cache = cache_len // parts
+    half_slab = seq_count // 2
     code_rows = jnp.pad(slab_codes.reshape(2, half_slab * 2), ((0, 0), (0, width - half_slab * 2)))
-    cache_pair = lax.dynamic_slice_in_dim(cache_block, parity * 2 * part_cache, 2 * part_cache, 0)
+    cache_pair = lax.dynamic_slice_in_dim(cache_block, u * 2 * part_cache, 2 * part_cache, 0)
     halves = jnp.stack(
         [
             jnp.concatenate(
@@ -144,7 +140,7 @@
     key_pos_slab = decode(every[:, part_cache + half_slab, : 2 * half_slab].reshape(-1, 2))
     key_pos_cache = (
         jnp.arange(cell_count, dtype=jnp.int32)[:, None] * cache_len
-        + quarter * part_cache
+        + part * part_cache
         + jnp.arange(part_cache, dtype=jnp.int32)[None, :]
     ).reshape(-1)
     keys = jnp.concatenate([cache_got[:, :HD], slab_got[:, :HD]], axis=0)
@@ -160,16 +156,17 @@
         [summed[slab_rows:].reshape(slab_rows, -1), row_max[slab_rows:], row_sum[slab_rows:]], axis=1
     )
     got = swap(theirs, "row", core_pairs)
-    split_at = pair_heads * HD
-    other_summed = got[:, :split_at].reshape(slab_rows, pair_heads, HD)
-    other_max = got[:, split_at : split_at + pair_heads]
-    other_sum = got[:, split_at + pair_heads :]
+    split_at = quad_heads * HD
+    other_summed = got[:, :split_at].reshape(slab_rows, quad_heads, HD)
+    other_max = got[:, split_at : split_at + quad_heads]
+    other_sum = got[:, split_at + quad_heads :]
     mine_max = row_max[:slab_rows]
     top = jnp.maximum(mine_max, other_max)
     scale_mine = jnp.exp(mine_max - top)
     scale_other = jnp.exp(other_max - top)
     numerator = summed[:slab_rows] * scale_mine[..., None] + other_summed * scale_other[..., None]
     denominator = row_sum[:slab_rows] * scale_mine + other_sum * scale_other
+
     normed = (numerator / denominator[..., None]).astype(jnp.bfloat16).reshape(slab_rows, -1)
     log_weight = top + jnp.log(denominator)
     pieces = []
@@ -184,19 +181,18 @@
     partial = jnp.concatenate([normed, coded], axis=1)
 
     back = lax.all_to_all(partial.reshape(seq_count, tok_rows, -1), "seq", 0, 0, tiled=True)
-    back = back.reshape(seq_count // 2, 2, tok_rows, -1)
-    half_num = back[..., :split_at].astype(jnp.float32).reshape(seq_count // 2, 2, tok_rows, pair_heads, HD)
-    half_log = (
-        back[..., split_at : split_at + 3 * pair_heads]
+    back = back.reshape(quads, quad, tok_rows, -1)
+    part_num = back[..., :split_at].astype(jnp.float32).reshape(quads, quad, tok_rows, quad_heads, HD)
+    part_log = (
+        back[..., split_at : split_at + 3 * quad_heads]
         .astype(jnp.float32)
-        .reshape(seq_count // 2, 2, tok_rows, 3, pair_heads)
+        .reshape(quads, quad, tok_rows, 3, quad_heads)
         .sum(axis=3)
     )
-    best = jnp.maximum(half_log[:, 0], half_log[:, 1])
-    w0 = jnp.exp(half_log[:, 0] - best)
-    w1 = jnp.exp(half_log[:, 1] - best)
-    num = half_num[:, 0] * w0[..., None] + half_num[:, 1] * w1[..., None]
-    context = (num / (w0 + w1)[..., None]).astype(jnp.bfloat16)
+    best = jnp.max(part_log, axis=1, keepdims=True)
+    weight = jnp.exp(part_log - best)
+    num = jnp.sum(part_num * weight[..., None], axis=1)
+    context = (num / jnp.sum(weight, axis=1)[..., None]).astype(jnp.bfloat16)
     return context.transpose(1, 0, 2, 3).reshape(tok_rows, -1)
 
 

time: 88.5 us -> 88.9 us (level)
  the two profiles are of different devices: /device:TPU:8 before, /device:TPU:72 now
where the time goes in v9:
time: 88.9 us; the launch traced here: 88.3 us
  starting transfers between devices  25.6 us (29%)
  waiting for transfers between devices  25.2 us (28%)
  blocking collectives  17.9 us (20%)
  local copies, waits for them, and re-layouts  9.94 us (11%)
  other arithmetic  5.7 us (6%)
  matrix products  2.83 us (3%)
  between operations  1.2 us (1%)
    all_to_all x1, blocking collectives, on_device(): lax.all_to_all(partial.reshape(seq_count, tok_rows, -1), 'seq', 0, 0, til...  17.9 us
    all_to_all x1, waiting for transfers between devices, on_device(): every = lax.all_to_all(per_dest, cell_axes, 0, 0, tiled=True)  12.3 us
    all_to_all x1, waiting for transfers between devices, on_device(): recv = lax.all_to_all(send, 'seq', 0, 0, tiled=True)  11.3 us
    all_to_all x1, starting transfers between devices, on_device(): recv = lax.all_to_all(send, 'seq', 0, 0, tiled=True)  10.2 us
    all_to_all x1, starting transfers between devices, on_device(): every = lax.all_to_all(per_dest, cell_axes, 0, 0, tiled=True)  10.1 us
    ppermute x2, starting transfers between devices, swap(): return lax.ppermute(x, axes, pairs)  5.37 us
    unnamed x6, local copies, waits for them, and re-layouts  2.35 us
    reduce_sum x1, other arithmetic, partial_attention(): row_sum = jnp.sum(exponent, axis=-1)  1.83 us
  transfers between devices with their start and end apart: 4, of which 3 were waited for; matrix products, arithmetic and copies ran while one was open for 3% of the time, Pallas kernels for 0%

profile of v9, /device:TPU:72, one launch (start us, length us, event | category | flops | bytes accessed | tf_op | source)
XLA Modules:
  0.0 88.3 jit_solution(2981849547205419703)
XLA Ops:
  0.0 0.7 convert_bitcast_fusion
  0.7 0.1 copy.81
  0.8 0.1 convert_element_type.52
  0.9 0.7 maximum_bitcast_fusion.7
  1.6 0.9 %broadcast_in_dim.32 = bf16[4,8,4,1024]{3,0,2,1:T(4,128)(2,1)S(1)} broadcast(bf16[4,8,1024]{2,0,1:T(4,128)(2,1)} %bitcast.85), dimensions={0,1,3} | broadcast | bytes 327680 | tf_op jit(solution)/shard_map/broadcast_in_dim | solution.py:83
  2.6 0.1 copy.105
  2.7 0.1 maximum_bitcast_fusion
  2.7 0.5 broadcast.99
  3.2 0.8 reduce.11
  4.0 1.0 %reshape.176 = bf16[32,2,2240]{2,1,0:T(2,128)(2,1)} reshape(bf16[32,4480]{1,0:T(8,128)(2,1)S(1)} %reduce.11) | data formatting | bytes 573440
  5.0 10.2 %all-to-all-start = ((bf16[32,2,2240]{2,1,0:T(2,128)(2,1)}), bf16[32,2,2240]{2,1,0:T(2,128)(2,1)S(1)}, u32[]{:S(2)}, u32[]{:S(2)}) async-start(bf16[32,2,2240]{2,1,0:T(2,128)(2,1)} %reshape.176), calls=%async_computation | async-start | bytes 589824 | tf_op jit(solution)/shard_map/all_to_all | solution.py:94
  15.9 0.9 %constant_dynamic-slice_fusion.1 = (bf16[256,128]{1,0:T(8,128)(2,1)S(1)}, bf16[256,128]{1,0:T(8,128)(2,1)S(1)}) fusion(bf16[256,1024]{1,0:T(8,128)(2,1)} %param.12, s32[]{:T(128)S(6)} %select_n.47, bf16[256,1024]{1,0:T(8,128)(2,1)} %param.11), kind=kLoop, calls=%fused_computation.74 | loop fusion | bytes 262148 | tf_op jit(solution)/shard_map/dynamic_slice | solution.py:112
  16.8 11.3 %all-to-all-done = bf16[32,2,2240]{2,1,0:T(2,128)(2,1)S(1)} async-done(((bf16[32,2,2240]{2,1,0:T(2,128)(2,1)}), bf16[32,2,2240]{2,1,0:T(2,128)(2,1)S(1)}, u32[]{:S(2)}, u32[]{:S(2)}) %all-to-all-start) | async-done | bytes 286752 | tf_op jit(solution)/shard_map/all_to_all | solution.py:94
  28.1 0.4 reshape.177
  28.6 1.3 %copy.83 = bf16[32,1,4480]{0,2,1:T(8,128)(2,1)S(1)} copy(bf16[32,1,4480]{2,1,0:T(2,128)(2,1)S(1)} %reshape.177) | data formatting | bytes 573440 | tf_op jit(solution)/shard_map/all_to_all | solution.py:94
  29.9 0.1 fusion.36
  30.0 0.1 slice.149
  30.0 0.1 copy.87
  30.1 0.1 copy.84
  30.2 0.1 reshape.145
  30.4 0.1 reshape_reshape.7
  30.4 0.3 copy.88
  30.8 0.1 copy.85
  30.8 0.1 copy.86
  30.9 0.2 reshape_reshape.8
  31.1 1.9 %collective-permute-start = (bf16[128,1026]{1,0:T(8,128)(2,1)S(1)}, bf16[128,1026]{1,0:T(8,128)(2,1)S(1)}, u32[]{:S(2)}, u32[]{:S(2)}) collective-permute-start(bf16[128,1026]{1,0:T(8,128)(2,1)S(1)} %pad_maximum_fusion.1), channel_id=1, source_target_pairs={{0,4},{4,0},{8,12},{12,8},{1,5},{5,1},{9,13},{13,9},{2,6},{6,2},{1... | collective-permute-start | bytes 787976 | tf_op jit(solution)/shard_map/ppermute | solution.py:52
  33.1 0.8 broadcast_in_dim.61
  33.9 10.1 %all-to-all-start.1 = ((bf16[16,49,256]{2,1,0:T(8,128)(2,1)}), bf16[16,49,256]{2,1,0:T(8,128)(2,1)S(1)}, u32[]{:S(2)}, u32[]{:S(2)}) async-start(bf16[16,49,256]{2,1,0:T(8,128)(2,1)} %bitcast.15), calls=%async_computation.1 | async-start | bytes 917504 | tf_op jit(solution)/shard_map/all_to_all | solution.py:137
  44.0 0.1 add_compare_fusion
  44.1 0.1 reshape.172
  44.2 0.1 reshape.147
  44.4 0.2 fusion.19
  44.5 0.0 collective-permute-done
  44.6 0.2 copy.90
  44.7 0.2 copy.92
  45.0 0.2 fusion.18
  45.1 12.3 %all-to-all-done.1 = bf16[16,49,256]{2,1,0:T(8,128)(2,1)S(1)} async-done(((bf16[16,49,256]{2,1,0:T(8,128)(2,1)}), bf16[16,49,256]{2,1,0:T(8,128)(2,1)S(1)}, u32[]{:S(2)}, u32[]{:S(2)}) %all-to-all-start.1) | async-done | bytes 401440 | tf_op jit(solution)/shard_map/all_to_all | solution.py:137
  57.5 0.1 reshape.158
  57.6 0.2 fusion.16
  57.9 0.1 broadcast_compare_fusion
  58.0 0.1 pad_add_fusion
  58.1 1.2 %select_reduce_fusion = (f32[256,8]{0,1:T(8,128)S(1)}, f32[256,8,768]{2,0,1:T(8,128)S(1)}) fusion(pred[256,768]{1,0:T(8,128)(4,1)S(1)} %pad_add_fusion, bf16[256,128]{1,0:T(8,128)(2,1)S(1)} %get-tuple-element.17, bf16[512,128]{1,0:T(8,128)(2,1)S(1)} %get-tuple-element.15, bf16[128,8,128]{2,0,1:T(8,128)(2,1)S(1)} %copy.92, bf16[128,8,128]{2,0,1:T(8,128)(2,1)S(1)} %copy.91), kind=kOutput, calls=%fused_computation.1 | convolution fusion | flops 408811520 | bytes 7217152 | tf_op jit(solution)/shard_map/thd,nd->thn/dot_general | solution.py:41
  59.3 1.8 %fusion = f32[256,8]{0,1:T(8,128)S(1)} fusion(f32[256,8,768]{2,0,1:T(8,128)S(1)} %get-tuple-element.27, f32[256,8]{0,1:T(8,128)S(1)} %get-tuple-element.26, pred[256,768]{1,0:T(8,128)(4,1)S(1)} %pad_add_fusion), kind=kLoop, calls=%fused_computation.2 | loop fusion | flops 6289408 | bytes 6504448 | tf_op jit(solution)/shard_map/reduce_sum | solution.py:44
  61.2 1.6 %fusion.2 = f32[256,8,128]{0,2,1:T(8,128)S(1)} fusion(f32[256,8,768]{2,0,1:T(8,128)S(1)} %get-tuple-element.27, f32[256,8]{0,1:T(8,128)S(1)} %get-tuple-element.26, pred[256,768]{1,0:T(8,128)(4,1)S(1)} %pad_add_fusion, bf16[256,128]{1,0:T(8,128)(2,1)S(1)} %get-tuple-element.16, bf16[512,128]{1,0:T(8,128)(2,1)S(1)} %get-tuple-element.14), kind=kOutput, calls=%fused_computation.4 | convolution fusion | flops 409337856 | bytes 7741440 | tf_op jit(solution)/shard_map/thn,nd->thd/dot_general | solution.py:45
  62.9 3.4 %collective-permute-start.1 = (f32[128,1040]{0,1:T(8,128)S(1)}, f32[128,1040]{0,1:T(8,128)S(1)}, u32[]{:S(2)}, u32[]{:S(2)}) collective-permute-start(f32[128,1040]{0,1:T(8,128)S(1)} %pad_maximum_fusion), channel_id=1, source_target_pairs={{0,4},{4,0},{8,12},{12,8},{1,5},{5,1},{9,13},{13,9},{2,6},{6,2},{1... | collective-permute-start | bytes 1597448 | tf_op jit(solution)/shard_map/ppermute | solution.py:52
  66.3 1.5 %collective-permute-done.1 = f32[128,1040]{0,1:T(8,128)S(1)} collective-permute-done((f32[128,1040]{0,1:T(8,128)S(1)}, f32[128,1040]{0,1:T(8,128)S(1)}, u32[]{:S(2)}, u32[]{:S(2)}) %collective-permute-start.1) | collective-permute-done | bytes 532512 | tf_op jit(solution)/shard_map/ppermute | solution.py:52
  67.9 0.1 fusion.11
  68.0 0.2 copy.94
  68.2 0.1 concatenate.56
  68.3 0.1 copy.104
  68.4 0.1 pad_maximum_fusion.2
  68.6 17.9 %all_to_all.22 = bf16[32,4,1152]{2,1,0:T(4,128)(2,1)S(1)} all-to-all(bf16[32,4,1152]{2,1,0:T(4,128)(2,1)S(1)} %pad_maximum_fusion.2), channel_id=1, replica_groups=mesh['seq'=32,'row'=4,'col'=4] {'seq'}, dimensions={0} | all-to-all | bytes 589824 | tf_op jit(solution)/shard_map/all_to_all | solution.py:183
  86.5 0.1 reshape.160
  86.7 0.2 reduce_sum.41
  86.9 0.2 mul.101
  87.1 0.2 mul.102
  87.3 0.2 multiply_reduce_fusion
  87.5 0.1 reduce_sum.43
  87.5 0.1 copy_bitcast_fusion.1
  87.6 0.7 copy.111
  (40 shorter events, 0.5 us)
Async XLA Ops:
  5.0 23.1 %all-to-all-start = ((bf16[32,2,2240]{2,1,0:T(2,128)(2,1)}), bf16[32,2,2240]{2,1,0:T(2,128)(2,1)S(1)}, u32[]{:S(2)}, u32[]{:S(2)}) async-start(bf16[32,2,2240]{2,1,0:T(2,128)(2,1)} %reshape.176), calls=%async_computation | async-start | bytes 589824 | tf_op jit(solution)/shard_map/all_to_all | solution.py:94
  31.1 13.4 %collective-permute-start = (bf16[128,1026]{1,0:T(8,128)(2,1)S(1)}, bf16[128,1026]{1,0:T(8,128)(2,1)S(1)}, u32[]{:S(2)}, u32[]{:S(2)}) collective-permute-start(bf16[128,1026]{1,0:T(8,128)(2,1)S(1)} %pad_maximum_fusion.1), channel_id=1, source_target_pairs={{0,4},{4,0},{8,12},{12,8},{1,5},{5,1},{9,13},{13,9},{2,6},{6,2},{1... | collective-permute-start | bytes 787976 | tf_op jit(solution)/shard_map/ppermute | solution.py:52
  33.9 23.6 %all-to-all-start.1 = ((bf16[16,49,256]{2,1,0:T(8,128)(2,1)}), bf16[16,49,256]{2,1,0:T(8,128)(2,1)S(1)}, u32[]{:S(2)}, u32[]{:S(2)}) async-start(bf16[16,49,256]{2,1,0:T(8,128)(2,1)} %bitcast.15), calls=%async_computation.1 | async-start | bytes 917504 | tf_op jit(solution)/shard_map/all_to_all | solution.py:137
  62.9 5.0 %collective-permute-start.1 = (f32[128,1040]{0,1:T(8,128)S(1)}, f32[128,1040]{0,1:T(8,128)S(1)}, u32[]{:S(2)}, u32[]{:S(2)}) collective-permute-start(f32[128,1040]{0,1:T(8,128)S(1)} %pad_maximum_fusion), channel_id=1, source_target_pairs={{0,4},{4,0},{8,12},{12,8},{1,5},{5,1},{9,13},{13,9},{2,6},{6,2},{1... | collective-permute-start | bytes 1597448 | tf_op jit(solution)/shard_map/ppermute | solution.py:52

commit v10 on v9

--- a/solution.py
+++ b/solution.py
@@ -55,6 +55,28 @@
 def decode(codes):
     codes = codes.astype(jnp.float32)
     return codes[..., 0] * code_base + codes[..., 1]
+
+
+def coded_partial(normed, log_weight):
+    rows = normed.shape[0]
+    pieces = []
+    rest = log_weight
+    for _ in range(3):
+        piece = lax.reduce_precision(rest, exponent_bits=8, mantissa_bits=7)
+        pieces.append(piece.astype(jnp.bfloat16))
+        rest = rest - piece
+    coded = jnp.stack(pieces, axis=1).reshape(rows, -1)
+    code_width = 128 * pl_cdiv(coded.shape[1], 128)
+    coded = jnp.pad(coded, ((0, 0), (0, code_width - coded.shape[1])))
+    return jnp.concatenate([normed.astype(jnp.bfloat16).reshape(rows, -1), coded], axis=1)
+
+
+def decode_partial(packed, heads):
+    rows = packed.shape[0]
+    split_at = heads * HD
+    normed = packed[:, :split_at].astype(jnp.float32).reshape(rows, heads, HD)
+    log_weight = packed[:, split_at : split_at + 3 * heads].astype(jnp.float32).reshape(rows, 3, heads).sum(axis=1)
+    return normed, log_weight
 
 
 def on_device(queries, new_keys, new_values, positions, cache_keys, cache_values, slab_start):
@@ -152,33 +174,18 @@
         both_q, both_pos, keys, values, key_pos_cache, key_pos_slab, cache_got.shape[0], first_pos
     )
 
-    theirs = jnp.concatenate(
-        [summed[slab_rows:].reshape(slab_rows, -1), row_max[slab_rows:], row_sum[slab_rows:]], axis=1
-    )
-    got = swap(theirs, "row", core_pairs)
+    log_all = row_max + jnp.log(row_sum)
+    normed_all = summed / row_sum[..., None]
+    theirs = coded_partial(normed_all[slab_rows:], log_all[slab_rows:])
+    other_normed, other_log = decode_partial(swap(theirs, "row", core_pairs), quad_heads)
+    mine_log = log_all[:slab_rows]
+    top = jnp.maximum(mine_log, other_log)
+    w_mine = jnp.exp(mine_log - top)
+    w_other = jnp.exp(other_log - top)
+    total = w_mine + w_other
+    combined = (normed_all[:slab_rows] * w_mine[..., None] + other_normed * w_other[..., None]) / total[..., None]
+    partial = coded_partial(combined, top + jnp.log(total))
     split_at = quad_heads * HD
-    other_summed = got[:, :split_at].reshape(slab_rows, quad_heads, HD)
-    other_max = got[:, split_at : split_at + quad_heads]
-    other_sum = got[:, split_at + quad_heads :]
-    mine_max = row_max[:slab_rows]
-    top = jnp.maximum(mine_max, other_max)
-    scale_mine = jnp.exp(mine_max - top)
-    scale_other = jnp.exp(other_max - top)
-    numerator = summed[:slab_rows] * scale_mine[..., None] + other_summed * scale_other[..., None]
-    denominator = row_sum[:slab_rows] * scale_mine + other_sum * scale_other
-
-    normed = (numerator / denominator[..., None]).astype(jnp.bfloat16).reshape(slab_rows, -1)
-    log_weight = top + jnp.log(denominator)
-    pieces = []
-    rest = log_weight
-    for _ in range(3):
-        piece = lax.reduce_precision(rest, exponent_bits=8, mantissa_bits=7)
-        pieces.append(piece.astype(jnp.bfloat16))
-        rest = rest - piece
-    coded = jnp.stack(pieces, axis=1).reshape(slab_rows, -1)
-    code_width = 128 * pl_cdiv(coded.shape[1], 128)
-    coded = jnp.pad(coded, ((0, 0), (0, code_width - coded.shape[1])))
-    partial = jnp.concatenate([normed, coded], axis=1)
 
     back = lax.all_to_all(partial.reshape(seq_count, tok_rows, -1), "seq", 0, 0, tiled=True)
     back = back.reshape(quads, quad, tok_rows, -1)

time: 88.9 us -> 88.5 us (level)
  no operation moved by 1% of the time
where the time goes in v10:
time: 88.5 us; the launch traced here: 88 us
  starting transfers between devices  25.6 us (29%)
  waiting for transfers between devices  24.8 us (28%)
  blocking collectives  17.9 us (20%)
  local copies, waits for them, and re-layouts  9.91 us (11%)
  other arithmetic  5.73 us (6%)
  matrix products  2.83 us (3%)
  between operations  1.21 us (1%)
    all_to_all x1, blocking collectives, on_device(): lax.all_to_all(partial.reshape(seq_count, tok_rows, -1), 'seq', 0, 0, til...  17.9 us
    all_to_all x1, waiting for transfers between devices, on_device(): every = lax.all_to_all(per_dest, cell_axes, 0, 0, tiled=True)  12.3 us
    all_to_all x1, waiting for transfers between devices, on_device(): recv = lax.all_to_all(send, 'seq', 0, 0, tiled=True)  11.3 us
    all_to_all x1, starting transfers between devices, on_device(): recv = lax.all_to_all(send, 'seq', 0, 0, tiled=True)  10.2 us
    all_to_all x1, starting transfers between devices, on_device(): every = lax.all_to_all(per_dest, cell_axes, 0, 0, tiled=True)  10.1 us
    ppermute x2, starting transfers between devices, swap(): return lax.ppermute(x, axes, pairs)  5.37 us
    unnamed x6, local copies, waits for them, and re-layouts  2.35 us
    reduce_sum x1, other arithmetic, partial_attention(): row_sum = jnp.sum(exponent, axis=-1)  1.83 us
  transfers between devices with their start and end apart: 4, of which 3 were waited for; matrix products, arithmetic and copies ran while one was open for 3% of the time, Pallas kernels for 0%

profile of v10, /device:TPU:72, one launch (start us, length us, event | category | flops | bytes accessed | tf_op | source)
XLA Modules:
  0.0 88.0 jit_solution(5782945497696014917)
XLA Ops:
  0.0 0.7 convert_bitcast_fusion
  0.7 0.1 copy.81
  0.8 0.1 convert_element_type.65
  0.9 0.7 maximum_bitcast_fusion.7
  1.6 0.9 %broadcast_in_dim.32 = bf16[4,8,4,1024]{3,0,2,1:T(4,128)(2,1)S(1)} broadcast(bf16[4,8,1024]{2,0,1:T(4,128)(2,1)} %bitcast.99), dimensions={0,1,3} | broadcast | bytes 327680 | tf_op jit(solution)/shard_map/broadcast_in_dim | solution.py:105
  2.6 0.1 copy.105
  2.7 0.1 maximum_bitcast_fusion
  2.7 0.5 broadcast.106
  3.2 0.8 reduce.11
  4.0 1.0 %reshape.197 = bf16[32,2,2240]{2,1,0:T(2,128)(2,1)} reshape(bf16[32,4480]{1,0:T(8,128)(2,1)S(1)} %reduce.11) | data formatting | bytes 573440
  5.0 10.2 %all-to-all-start = ((bf16[32,2,2240]{2,1,0:T(2,128)(2,1)}), bf16[32,2,2240]{2,1,0:T(2,128)(2,1)S(1)}, u32[]{:S(2)}, u32[]{:S(2)}) async-start(bf16[32,2,2240]{2,1,0:T(2,128)(2,1)} %reshape.197), calls=%async_computation | async-start | bytes 589824 | tf_op jit(solution)/shard_map/all_to_all | solution.py:116
  15.9 0.9 %constant_dynamic-slice_fusion.1 = (bf16[256,128]{1,0:T(8,128)(2,1)S(1)}, bf16[256,128]{1,0:T(8,128)(2,1)S(1)}) fusion(bf16[256,1024]{1,0:T(8,128)(2,1)} %param.12, s32[]{:T(128)S(6)} %select_n.47, bf16[256,1024]{1,0:T(8,128)(2,1)} %param.11), kind=kLoop, calls=%fused_computation.89 | loop fusion | bytes 262148 | tf_op jit(solution)/shard_map/dynamic_slice | solution.py:134
  16.8 11.3 %all-to-all-done = bf16[32,2,2240]{2,1,0:T(2,128)(2,1)S(1)} async-done(((bf16[32,2,2240]{2,1,0:T(2,128)(2,1)}), bf16[32,2,2240]{2,1,0:T(2,128)(2,1)S(1)}, u32[]{:S(2)}, u32[]{:S(2)}) %all-to-all-start) | async-done | bytes 286752 | tf_op jit(solution)/shard_map/all_to_all | solution.py:116
  28.1 0.4 reshape.198
  28.6 1.3 %copy.83 = bf16[32,1,4480]{0,2,1:T(8,128)(2,1)S(1)} copy(bf16[32,1,4480]{2,1,0:T(2,128)(2,1)S(1)} %reshape.198) | data formatting | bytes 573440 | tf_op jit(solution)/shard_map/all_to_all | solution.py:116
  29.9 0.1 fusion.44
  30.0 0.1 slice.138
  30.0 0.1 copy.87
  30.1 0.1 copy.84
  30.2 0.1 reshape.158
  30.4 0.1 reshape_reshape.7
  30.4 0.3 copy.88
  30.8 0.1 copy.85
  30.8 0.1 copy.86
  30.9 0.2 reshape_reshape.8
  31.1 1.9 %collective-permute-start = (bf16[128,1026]{1,0:T(8,128)(2,1)S(1)}, bf16[128,1026]{1,0:T(8,128)(2,1)S(1)}, u32[]{:S(2)}, u32[]{:S(2)}) collective-permute-start(bf16[128,1026]{1,0:T(8,128)(2,1)S(1)} %pad_maximum_fusion), channel_id=1, source_target_pairs={{0,4},{4,0},{8,12},{12,8},{1,5},{5,1},{9,13},{13,9},{2,6},{6,2},{1... | collective-permute-start | bytes 787976 | tf_op jit(solution)/shard_map/ppermute | solution.py:52
  33.1 0.8 broadcast_in_dim.62
  33.9 10.1 %all-to-all-start.1 = ((bf16[16,49,256]{2,1,0:T(8,128)(2,1)}), bf16[16,49,256]{2,1,0:T(8,128)(2,1)S(1)}, u32[]{:S(2)}, u32[]{:S(2)}) async-start(bf16[16,49,256]{2,1,0:T(8,128)(2,1)} %bitcast.15), calls=%async_computation.1 | async-start | bytes 917504 | tf_op jit(solution)/shard_map/all_to_all | solution.py:159
  44.0 0.1 add_compare_fusion
  44.1 0.1 reshape.193
  44.2 0.1 reshape.160
  44.4 0.2 fusion.24
  44.5 0.0 collective-permute-done
  44.6 0.2 copy.90
  44.7 0.2 copy.92
  45.0 0.2 fusion.23
  45.1 12.3 %all-to-all-done.1 = bf16[16,49,256]{2,1,0:T(8,128)(2,1)S(1)} async-done(((bf16[16,49,256]{2,1,0:T(8,128)(2,1)}), bf16[16,49,256]{2,1,0:T(8,128)(2,1)S(1)}, u32[]{:S(2)}, u32[]{:S(2)}) %all-to-all-start.1) | async-done | bytes 401440 | tf_op jit(solution)/shard_map/all_to_all | solution.py:159
  57.5 0.1 reshape.175
  57.6 0.2 fusion.21
  57.9 0.1 broadcast_compare_fusion
  58.0 0.1 pad_add_fusion
  58.1 1.2 %select_reduce_fusion = (f32[256,8]{0,1:T(8,128)S(1)}, f32[256,8,768]{2,0,1:T(8,128)S(1)}) fusion(pred[256,768]{1,0:T(8,128)(4,1)S(1)} %pad_add_fusion, bf16[256,128]{1,0:T(8,128)(2,1)S(1)} %get-tuple-element.17, bf16[512,128]{1,0:T(8,128)(2,1)S(1)} %get-tuple-element.15, bf16[128,8,128]{2,0,1:T(8,128)(2,1)S(1)} %copy.92, bf16[128,8,128]{2,0,1:T(8,128)(2,1)S(1)} %copy.91), kind=kOutput, calls=%fused_computation.1 | convolution fusion | flops 408811520 | bytes 7217152 | tf_op jit(solution)/shard_map/thd,nd->thn/dot_general | solution.py:41
  59.3 1.8 %fusion = f32[256,8]{0,1:T(8,128)S(1)} fusion(f32[256,8,768]{2,0,1:T(8,128)S(1)} %get-tuple-element.30, f32[256,8]{0,1:T(8,128)S(1)} %get-tuple-element.29, pred[256,768]{1,0:T(8,128)(4,1)S(1)} %pad_add_fusion), kind=kLoop, calls=%fused_computation.2 | loop fusion | flops 6289408 | bytes 6504448 | tf_op jit(solution)/shard_map/reduce_sum | solution.py:44
  61.2 1.6 %fusion.5 = f32[256,8,128]{0,2,1:T(8,128)S(1)} fusion(f32[256,8,768]{2,0,1:T(8,128)S(1)} %get-tuple-element.30, f32[256,8]{0,1:T(8,128)S(1)} %get-tuple-element.29, pred[256,768]{1,0:T(8,128)(4,1)S(1)} %pad_add_fusion, f32[256,8]{0,1:T(8,128)S(1)} %fusion, bf16[256,128]{1,0:T(8,128)(2,1)S(1)} %get-tuple-element.16, bf16[512,128]{1,0:T(8,128)(2,1)S(1)} %get-tuple-element.14), kind=kOutput, calls=%fused_computation.6 | convolution fusion | flops 409600000 | bytes 7749632 | tf_op jit(solution)/shard_map/thn,nd->thd/dot_general | solution.py:45
  62.9 3.4 %collective-permute-start.1 = (bf16[128,1152]{0,1:T(8,128)(2,1)S(1)}, bf16[128,1152]{0,1:T(8,128)(2,1)S(1)}, u32[]{:S(2)}, u32[]{:S(2)}) collective-permute-start(bf16[128,1152]{0,1:T(8,128)(2,1)S(1)} %fusion.16), channel_id=1, source_target_pairs={{0,4},{4,0},{8,12},{12,8},{1,5},{5,1},{9,13},{13,9},{2,6},{6,2},{1... | collective-permute-start | bytes 884744 | tf_op jit(solution)/shard_map/ppermute | solution.py:52
  66.3 1.2 %collective-permute-done.1 = bf16[128,1152]{0,1:T(8,128)(2,1)S(1)} collective-permute-done((bf16[128,1152]{0,1:T(8,128)(2,1)S(1)}, bf16[128,1152]{0,1:T(8,128)(2,1)S(1)}, u32[]{:S(2)}, u32[]{:S(2)}) %collective-permute-start.1) | collective-permute-done | bytes 294944 | tf_op jit(solution)/shard_map/ppermute | solution.py:52
  67.6 0.1 fusion.15
  67.7 0.2 copy.94
  67.9 0.1 concatenate.56
  68.0 0.1 copy.104
  68.1 0.1 pad_maximum_fusion.1
  68.3 17.9 %all_to_all.22 = bf16[32,4,1152]{2,1,0:T(4,128)(2,1)S(1)} all-to-all(bf16[32,4,1152]{2,1,0:T(4,128)(2,1)S(1)} %pad_maximum_fusion.1), channel_id=1, replica_groups=mesh['seq'=32,'row'=4,'col'=4] {'seq'}, dimensions={0} | all-to-all | bytes 589824 | tf_op jit(solution)/shard_map/all_to_all | solution.py:190
  86.2 0.1 reshape.181
  86.3 0.2 reduce_sum.51
  86.6 0.2 mul.93
  86.8 0.2 mul.94
  87.0 0.2 multiply_reduce_fusion
  87.1 0.1 reduce_sum.53
  87.2 0.1 copy_bitcast_fusion.1
  87.3 0.7 copy.111
  (42 shorter events, 0.5 us)
Async XLA Ops:
  5.0 23.1 %all-to-all-start = ((bf16[32,2,2240]{2,1,0:T(2,128)(2,1)}), bf16[32,2,2240]{2,1,0:T(2,128)(2,1)S(1)}, u32[]{:S(2)}, u32[]{:S(2)}) async-start(bf16[32,2,2240]{2,1,0:T(2,128)(2,1)} %reshape.197), calls=%async_computation | async-start | bytes 589824 | tf_op jit(solution)/shard_map/all_to_all | solution.py:116
  31.1 13.4 %collective-permute-start = (bf16[128,1026]{1,0:T(8,128)(2,1)S(1)}, bf16[128,1026]{1,0:T(8,128)(2,1)S(1)}, u32[]{:S(2)}, u32[]{:S(2)}) collective-permute-start(bf16[128,1026]{1,0:T(8,128)(2,1)S(1)} %pad_maximum_fusion), channel_id=1, source_target_pairs={{0,4},{4,0},{8,12},{12,8},{1,5},{5,1},{9,13},{13,9},{2,6},{6,2},{1... | collective-permute-start | bytes 787976 | tf_op jit(solution)/shard_map/ppermute | solution.py:52
  33.9 23.6 %all-to-all-start.1 = ((bf16[16,49,256]{2,1,0:T(8,128)(2,1)}), bf16[16,49,256]{2,1,0:T(8,128)(2,1)S(1)}, u32[]{:S(2)}, u32[]{:S(2)}) async-start(bf16[16,49,256]{2,1,0:T(8,128)(2,1)} %bitcast.15), calls=%async_computation.1 | async-start | bytes 917504 | tf_op jit(solution)/shard_map/all_to_all | solution.py:159
  62.9 4.6 %collective-permute-start.1 = (bf16[128,1152]{0,1:T(8,128)(2,1)S(1)}, bf16[128,1152]{0,1:T(8,128)(2,1)S(1)}, u32[]{:S(2)}, u32[]{:S(2)}) collective-permute-start(bf16[128,1152]{0,1:T(8,128)(2,1)S(1)} %fusion.16), channel_id=1, source_target_pairs={{0,4},{4,0},{8,12},{12,8},{1,5},{5,1},{9,13},{13,9},{2,6},{6,2},{1... | collective-permute-start | bytes 884744 | tf_op jit(solution)/shard_map/ppermute | solution.py:52

commit v11 on v10

--- a/solution.py
+++ b/solution.py
@@ -94,10 +94,6 @@
     quad = group_size // heads_dev
     quads = seq_count // quad
     u = seq_index % quad
-    core = lax.axis_index("row") % 2
-    part = u * 2 + core
-    parts = quad * 2
-    core_pairs = [(r, r ^ 1) for r in range(row_count)]
     width = 2 * HD
     quad_heads = group_size
 
@@ -122,12 +118,6 @@
     own_pos = decode(got_codes.reshape(slab_rows, 2))
     slab_codes = lax.dynamic_index_in_dim(got_codes, u, 1, keepdims=False)
 
-    partner_q = swap(
-        jnp.concatenate([query_block.reshape(slab_rows, -1), got_codes.reshape(slab_rows, 2)], axis=1), "row", core_pairs
-    )
-    partner_block = partner_q[:, : quad_heads * HD].reshape(slab_rows, quad_heads, HD)
-    partner_pos = decode(partner_q[:, quad_heads * HD :])
-
     cache_block = jnp.concatenate(
         [
             lax.dynamic_slice_in_dim(cache_keys, kv_first * HD, HD, 1),
@@ -136,55 +126,27 @@
         axis=1,
     )
     cache_len = cache_block.shape[0]
-    part_cache = cache_len // parts
-    half_slab = seq_count // 2
-    code_rows = jnp.pad(slab_codes.reshape(2, half_slab * 2), ((0, 0), (0, width - half_slab * 2)))
-    cache_pair = lax.dynamic_slice_in_dim(cache_block, u * 2 * part_cache, 2 * part_cache, 0)
-    halves = jnp.stack(
-        [
-            jnp.concatenate(
-                [
-                    cache_pair[b * part_cache : (b + 1) * part_cache],
-                    slab_kv[b * half_slab : (b + 1) * half_slab],
-                    code_rows[b : b + 1],
-                ],
-                axis=0,
-            )
-            for b in range(2)
-        ]
+    part_cache = cache_len // quad
+    code_row = jnp.pad(slab_codes.reshape(1, seq_count * 2), ((0, 0), (0, width - seq_count * 2)))
+    block = jnp.concatenate(
+        [lax.dynamic_slice_in_dim(cache_block, u * part_cache, part_cache, 0), slab_kv, code_row], axis=0
     )
-    per_dest = jnp.broadcast_to(
-        halves[None, :, None], (row_count // 2, 2, col_count) + halves.shape[1:]
-    ).reshape((cell_count,) + halves.shape[1:])
-    every = lax.all_to_all(per_dest, cell_axes, 0, 0, tiled=True)
+    every = gather_cells(block, cell_axes, cell_count)
     cache_got = every[:, :part_cache].reshape(-1, width)
-    slab_got = every[:, part_cache : part_cache + half_slab].reshape(-1, width)
-    key_pos_slab = decode(every[:, part_cache + half_slab, : 2 * half_slab].reshape(-1, 2))
+    slab_got = every[:, part_cache : part_cache + seq_count].reshape(-1, width)
+    key_pos_slab = decode(every[:, part_cache + seq_count, : 2 * seq_count].reshape(-1, 2))
     key_pos_cache = (
         jnp.arange(cell_count, dtype=jnp.int32)[:, None] * cache_len
-        + part * part_cache
+        + u * part_cache
         + jnp.arange(part_cache, dtype=jnp.int32)[None, :]
     ).reshape(-1)
     keys = jnp.concatenate([cache_got[:, :HD], slab_got[:, :HD]], axis=0)
     values = jnp.concatenate([cache_got[:, HD:], slab_got[:, HD:]], axis=0)
 
-    both_q = jnp.concatenate([query_block, partner_block], axis=0)
-    both_pos = jnp.concatenate([own_pos, partner_pos], axis=0)
     row_max, row_sum, summed = partial_attention(
-        both_q, both_pos, keys, values, key_pos_cache, key_pos_slab, cache_got.shape[0], first_pos
+        query_block, own_pos, keys, values, key_pos_cache, key_pos_slab, cache_got.shape[0], first_pos
     )
-
-    log_all = row_max + jnp.log(row_sum)
-    normed_all = summed / row_sum[..., None]
-    theirs = coded_partial(normed_all[slab_rows:], log_all[slab_rows:])
-    other_normed, other_log = decode_partial(swap(theirs, "row", core_pairs), quad_heads)
-    mine_log = log_all[:slab_rows]
-    top = jnp.maximum(mine_log, other_log)
-    w_mine = jnp.exp(mine_log - top)
-    w_other = jnp.exp(other_log - top)
-    total = w_mine + w_other
-    combined = (normed_all[:slab_rows] * w_mine[..., None] + other_normed * w_other[..., None]) / total[..., None]
-    partial = coded_partial(combined, top + jnp.log(total))
+    partial = coded_partial(summed / row_sum[..., None], row_max + jnp.log(row_sum))
     split_at = quad_heads * HD
 
     back = lax.all_to_all(partial.reshape(seq_count, tok_rows, -1), "seq", 0, 0, tiled=True)

time: 88.5 us -> 89.7 us (1.014)
  the two profiles are of different devices: /device:TPU:72 before, /device:TPU:73 now
where the time goes in v11:
time: 89.7 us; the launch traced here: 89.3 us
  waiting for transfers between devices  32 us (36%)
  starting transfers between devices  21.5 us (24%)
  blocking collectives  17.5 us (20%)
  local copies, waits for them, and re-layouts  9.45 us (11%)
  other arithmetic  5.16 us (6%)
  matrix products  2.56 us (3%)
  between operations  1.04 us (1%)
    all_to_all x1, waiting for transfers between devices, gather_cells(): return lax.all_to_all(spread, cell_axes, 0, 0, tiled=True)  21.1 us
    all_to_all x1, blocking collectives, on_device(): lax.all_to_all(partial.reshape(seq_count, tok_rows, -1), 'seq', 0, 0, til...  17.5 us
    all_to_all x1, starting transfers between devices, gather_cells(): return lax.all_to_all(spread, cell_axes, 0, 0, tiled=True)  11.9 us
    all_to_all x1, waiting for transfers between devices, on_device(): recv = lax.all_to_all(send, 'seq', 0, 0, tiled=True)  10.9 us
    all_to_all x1, starting transfers between devices, on_device(): recv = lax.all_to_all(send, 'seq', 0, 0, tiled=True)  9.6 us
    unnamed x6, local copies, waits for them, and re-layouts  2.35 us
  transfers between devices with their start and end apart: 2, of which 2 were waited for; matrix products, arithmetic and copies ran while one was open for 2% of the time, Pallas kernels for 0%

profile of v11, /device:TPU:73, one launch (start us, length us, event | category | flops | bytes accessed | tf_op | source)
XLA Modules:
  0.0 89.3 jit_solution(14919746820772486513)
XLA Ops:
  0.0 0.7 convert_bitcast_fusion
  0.7 0.1 copy.65
  0.8 0.1 convert_element_type.73
  0.9 0.7 maximum_bitcast_fusion.5
  1.6 0.9 %broadcast_in_dim.56 = bf16[4,8,4,1024]{3,0,2,1:T(4,128)(2,1)S(1)} broadcast(bf16[4,8,1024]{2,0,1:T(4,128)(2,1)} %bitcast.75), dimensions={0,1,3} | broadcast | bytes 327680 | tf_op jit(solution)/shard_map/broadcast_in_dim | solution.py:101
  2.6 0.1 copy.82
  2.7 0.1 maximum_bitcast_fusion.4
  2.7 0.5 broadcast.90
  3.2 0.8 reduce.9
  4.0 1.0 %reshape.209 = bf16[32,2,2240]{2,1,0:T(2,128)(2,1)} reshape(bf16[32,4480]{1,0:T(8,128)(2,1)S(1)} %reduce.9) | data formatting | bytes 573440
  5.0 9.6 %all-to-all-start = ((bf16[32,2,2240]{2,1,0:T(2,128)(2,1)}), bf16[32,2,2240]{2,1,0:T(2,128)(2,1)S(1)}, u32[]{:S(2)}, u32[]{:S(2)}) async-start(bf16[32,2,2240]{2,1,0:T(2,128)(2,1)} %reshape.209), calls=%async_computation | async-start | bytes 589824 | tf_op jit(solution)/shard_map/all_to_all | solution.py:112
  14.7 0.9 constant_dynamic-slice_fusion.1
  15.6 10.9 %all-to-all-done = bf16[32,2,2240]{2,1,0:T(2,128)(2,1)S(1)} async-done(((bf16[32,2,2240]{2,1,0:T(2,128)(2,1)}), bf16[32,2,2240]{2,1,0:T(2,128)(2,1)S(1)}, u32[]{:S(2)}, u32[]{:S(2)}) %all-to-all-start) | async-done | bytes 286752 | tf_op jit(solution)/shard_map/all_to_all | solution.py:112
  26.5 0.4 reshape.210
  27.0 1.3 %copy.67 = bf16[32,1,4480]{0,2,1:T(8,128)(2,1)S(1)} copy(bf16[32,1,4480]{2,1,0:T(2,128)(2,1)S(1)} %reshape.210) | data formatting | bytes 573440 | tf_op jit(solution)/shard_map/all_to_all | solution.py:112
  28.3 0.1 copy.68
  28.4 0.1 reshape.182
  28.5 0.1 copy.69
  28.6 1.0 %broadcast_in_dim.59 = bf16[16,97,256]{2,1,0:T(8,128)(2,1)} broadcast(bf16[97,256]{1,0:T(8,128)(2,1)S(1)} %fusion.21), dimensions={1,2} | broadcast | bytes 844288 | tf_op jit(solution)/shard_map/broadcast_in_dim | solution.py:18
  29.6 11.9 %all-to-all-start.1 = ((bf16[16,97,256]{2,1,0:T(8,128)(2,1)}), bf16[16,97,256]{2,1,0:T(8,128)(2,1)S(1)}, u32[]{:S(2)}, u32[]{:S(2)}) async-start(bf16[16,97,256]{2,1,0:T(8,128)(2,1)} %broadcast_in_dim.59), calls=%async_computation.1 | async-start | bytes 1703936 | tf_op jit(solution)/shard_map/all_to_all | solution.py:19
  42.1 0.1 add_compare_fusion
  42.2 0.1 reshape.205
  42.3 0.1 slice.71
  42.4 0.1 copy.70
  42.5 0.1 reshape.192
  42.5 0.3 copy.71
  42.9 0.1 reshape.183
  43.0 0.2 fusion.20
  43.2 21.1 %all-to-all-done.1 = bf16[16,97,256]{2,1,0:T(8,128)(2,1)S(1)} async-done(((bf16[16,97,256]{2,1,0:T(8,128)(2,1)}), bf16[16,97,256]{2,1,0:T(8,128)(2,1)S(1)}, u32[]{:S(2)}, u32[]{:S(2)}) %all-to-all-start.1) | async-done | bytes 794656 | tf_op jit(solution)/shard_map/all_to_all | solution.py:19
  64.3 0.3 reshape.191
  64.6 0.2 fusion.16
  65.0 0.1 broadcast_compare_fusion
  65.1 0.1 pad_add_fusion
  65.2 1.2 %select_reduce_fusion = (f32[128,8]{0,1:T(8,128)S(1)}, f32[128,8,1536]{2,0,1:T(8,128)S(1)}) fusion(pred[128,1536]{1,0:T(8,128)(4,1)S(1)} %pad_add_fusion, bf16[512,128]{1,0:T(8,128)(2,1)S(1)} %get-tuple-element.12, bf16[1024,128]{1,0:T(8,128)(2,1)S(1)} %get-tuple-element.10, bf16[128,8,128]{2,1,0:T(8,128)(2,1)S(1)} %reshape.183), kind=kOutput, calls=%fused_computation.1 | convolution fusion | flops 408157184 | bytes 7147520 | tf_op jit(solution)/shard_map/thd,nd->thn/dot_general | solution.py:41
  66.4 1.6 %fusion = f32[128,8]{0,1:T(8,128)S(1)} fusion(f32[128,8,1536]{2,0,1:T(8,128)S(1)} %get-tuple-element.19, f32[128,8]{0,1:T(8,128)S(1)} %get-tuple-element.18, pred[128,1536]{1,0:T(8,128)(4,1)S(1)} %pad_add_fusion), kind=kLoop, calls=%fused_computation.2 | loop fusion | flops 6290432 | bytes 6496256 | tf_op jit(solution)/shard_map/reduce_sum | solution.py:44
  68.0 1.3 %fusion.8 = bf16[128,8,128]{2,0,1:T(8,128)(2,1)S(1)} fusion(f32[128,8,1536]{2,0,1:T(8,128)S(1)} %get-tuple-element.19, f32[128,8]{0,1:T(8,128)S(1)} %get-tuple-element.18, pred[128,1536]{1,0:T(8,128)(4,1)S(1)} %pad_add_fusion, bf16[512,128]{1,0:T(8,128)(2,1)S(1)} %get-tuple-element.11, bf16[1024,128]{1,0:T(8,128)(2,1)S(1)} %get-tuple-element.9, ...), kind=kOutput, calls=%fused_computation.7 | convolution fusion | flops 409993216 | bytes 7151616 | tf_op jit(solution)/shard_map/thn,nd->thd/dot_general | solution.py:45
  69.3 0.2 copy.73
  69.5 0.1 concatenate.36
  69.6 0.1 copy.81
  69.7 0.1 pad_maximum_fusion
  69.9 17.5 %all_to_all.22 = bf16[32,4,1152]{2,1,0:T(4,128)(2,1)S(1)} all-to-all(bf16[32,4,1152]{2,1,0:T(4,128)(2,1)S(1)} %pad_maximum_fusion), channel_id=1, replica_groups=mesh['seq'=32,'row'=4,'col'=4] {'seq'}, dimensions={0} | all-to-all | bytes 589824 | tf_op jit(solution)/shard_map/all_to_all | solution.py:152
  87.4 0.1 reshape.194
  87.6 0.2 reduce_sum.41
  87.8 0.2 mul.64
  88.0 0.2 mul.65
  88.2 0.2 multiply_reduce_fusion
  88.4 0.1 reduce_sum.43
  88.5 0.1 copy_bitcast_fusion.1
  88.6 0.7 copy.92
  (25 shorter events, 0.4 us)
Async XLA Ops:
  5.0 21.5 %all-to-all-start = ((bf16[32,2,2240]{2,1,0:T(2,128)(2,1)}), bf16[32,2,2240]{2,1,0:T(2,128)(2,1)S(1)}, u32[]{:S(2)}, u32[]{:S(2)}) async-start(bf16[32,2,2240]{2,1,0:T(2,128)(2,1)} %reshape.209), calls=%async_computation | async-start | bytes 589824 | tf_op jit(solution)/shard_map/all_to_all | solution.py:112
  29.6 34.7 %all-to-all-start.1 = ((bf16[16,97,256]{2,1,0:T(8,128)(2,1)}), bf16[16,97,256]{2,1,0:T(8,128)(2,1)S(1)}, u32[]{:S(2)}, u32[]{:S(2)}) async-start(bf16[16,97,256]{2,1,0:T(8,128)(2,1)} %broadcast_in_dim.59), calls=%async_computation.1 | async-start | bytes 1703936 | tf_op jit(solution)/shard_map/all_to_all | solution.py:19

commit v12 on v8

--- a/solution.py
+++ b/solution.py
@@ -5,6 +5,8 @@
 import jax.numpy as jnp
 from jax import lax
 from jax.sharding import PartitionSpec as P
+from jax.experimental import pallas as pl
+from jax.experimental.pallas import tpu as pltpu
 
 HQ = 64
 KVH = 8
@@ -55,6 +57,42 @@
 def decode(codes):
     codes = codes.astype(jnp.float32)
     return codes[..., 0] * code_base + codes[..., 1]
+
+
+def send_kernel(q_ref, k_ref, v_ref, p_ref, o_ref):
+    seq_count = o_ref.shape[0]
+    tok_rows = q_ref.shape[0]
+    half = tok_rows // 2
+    q_width = q_ref.shape[1] // (seq_count // 2)
+    q_len = tok_rows * q_width
+    lanes = lax.broadcasted_iota(jnp.int32, (1, 128), 1)
+    row = jnp.zeros((1, 128), jnp.float32)
+    for t in range(tok_rows):
+        pos = p_ref[0, t]
+        row = jnp.where(lanes == 2 * t, (pos // code_base).astype(jnp.float32), row)
+        row = jnp.where(lanes == 2 * t + 1, (pos % code_base).astype(jnp.float32), row)
+    row = row.astype(o_ref.dtype)
+    for s in range(seq_count):
+        group, pair, head = s // 2, s % 2, s // (seq_count // KVH)
+        for t in range(tok_rows):
+            o_ref[s : s + 1, t * q_width : (t + 1) * q_width] = q_ref[t : t + 1, group * q_width : (group + 1) * q_width]
+        for t in range(half):
+            k = pair * half + t
+            base = q_len + t * 2 * HD
+            o_ref[s : s + 1, base : base + HD] = k_ref[k : k + 1, head * HD : (head + 1) * HD]
+            o_ref[s : s + 1, base + HD : base + 2 * HD] = v_ref[k : k + 1, head * HD : (head + 1) * HD]
+        o_ref[s : s + 1, q_len + half * 2 * HD :] = row
+
+
+def build_send(queries, new_keys, new_values, positions, seq_count):
+    tok_rows = queries.shape[0]
+    width = tok_rows * (queries.shape[1] // (seq_count // 2)) + (tok_rows // 2) * 2 * HD + 128
+    return pl.pallas_call(
+        send_kernel,
+        in_specs=[pl.BlockSpec(memory_space=pltpu.VMEM)] * 3 + [pl.BlockSpec(memory_space=pltpu.SMEM)],
+        out_specs=pl.BlockSpec(memory_space=pltpu.VMEM),
+        out_shape=jax.ShapeDtypeStruct((seq_count, width), queries.dtype),
+    )(queries, new_keys, new_values, positions.reshape(1, -1))
 
 
 def on_device(queries, new_keys, new_values, positions, cache_keys, cache_values, slab_start):
@@ -79,21 +117,7 @@
     pair_heads = 2 * heads_dev
     half_tok = tok_rows // 2
 
-    q_pairs = queries.reshape(tok_rows, seq_count // 2, 1, pair_heads * HD)
-    q_part = jnp.broadcast_to(q_pairs, (tok_rows, seq_count // 2, 2, pair_heads * HD)).reshape(tok_rows, seq_count, -1)
-    kv_local = jnp.concatenate(
-        [new_keys.reshape(tok_rows, KVH, 1, HD), new_values.reshape(tok_rows, KVH, 1, HD)], axis=2
-    ).reshape(2, half_tok, KVH, 1, width)
-    repeat = seq_count // (2 * KVH)
-    kv_part = jnp.broadcast_to(
-        kv_local.transpose(2, 3, 0, 1, 4)[:, :, None], (KVH, 1, repeat, 2, half_tok, width)
-    ).reshape(seq_count, half_tok * width)
-    codes = jnp.stack([positions // code_base, positions % code_base], axis=1).astype(jnp.bfloat16)
-    codes = jnp.pad(codes.reshape(1, tok_rows * 2), ((0, 0), (0, 128 - tok_rows * 2)))
-    send = jnp.concatenate(
-        [q_part.transpose(1, 0, 2).reshape(seq_count, -1), kv_part, jnp.broadcast_to(codes, (seq_count, 128))],
-        axis=1,
-    )
+    send = build_send(queries, new_keys, new_values, positions, seq_count)
     recv = lax.all_to_all(send, "seq", 0, 0, tiled=True)
     q_len = tok_rows * pair_heads * HD
     kvp_len = half_tok * width

time: 88.5 us -> 88.5 us (level)
  local copies, waits for them, and re-layouts: 9.99 us -> 8.1 us
  Pallas kernels: 0 us -> 1.81 us
    pallas_call x0 -> x1, Pallas kernels: none -> 1.81 us  [build_send(): pl.pallas_call(send_kernel, in_specs=[pl.BlockSpec(memory_space=pltpu.VME...]
    broadcast_in_dim x4 -> x0, local copies, waits for them, and re-layouts: 0.93 us -> none  [the longest x1 0.88 us: on_device(): jnp.broadcast_to(q_pairs, (tok_rows, seq_count // 2, 2, pair_heads * HD))]
where the time goes in v12:
time: 88.5 us; the launch traced here: 88 us
  waiting for transfers between devices  29.4 us (33%)
  starting transfers between devices  24.8 us (28%)
  blocking collectives  14.9 us (17%)
  local copies, waits for them, and re-layouts  8.1 us (9%)
  other arithmetic  5 us (6%)
  matrix products  2.82 us (3%)
  Pallas kernels  1.81 us (2%)
  between operations  1.09 us (1%)
    all_to_all x1, waiting for transfers between devices, on_device(): every = lax.all_to_all(per_dest, cell_axes, 0, 0, tiled=True)  17.7 us
    all_to_all x1, blocking collectives, on_device(): lax.all_to_all(partial.reshape(seq_count, tok_rows, -1), 'seq', 0, 0, til...  14.9 us
    all_to_all x1, starting transfers between devices, on_device(): every = lax.all_to_all(per_dest, cell_axes, 0, 0, tiled=True)  10.4 us
    all_to_all x1, starting transfers between devices, on_device(): recv = lax.all_to_all(send, 'seq', 0, 0, tiled=True)  10.2 us
    all_to_all x1, waiting for transfers between devices, on_device(): recv = lax.all_to_all(send, 'seq', 0, 0, tiled=True)  9.71 us
    ppermute x2, starting transfers between devices, swap(): return lax.ppermute(x, axes, pairs)  4.23 us
    ppermute x2, waiting for transfers between devices, swap(): return lax.ppermute(x, axes, pairs)  2.05 us
    pallas_call x1, Pallas kernels, build_send(): pl.pallas_call(send_kernel, in_specs=[pl.BlockSpec(memory_space=pltpu.VME...  1.81 us
  transfers between devices with their start and end apart: 4, of which 4 were waited for; matrix products, arithmetic and copies ran while one was open for 3% of the time, Pallas kernels for 0%

profile of v12, /device:TPU:8, one launch (start us, length us, event | category | flops | bytes accessed | tf_op | source)
XLA Modules:
  0.0 88.0 jit_solution(1635693254601888512)
XLA Ops:
  0.0 0.0 copy-start
  0.0 1.8 %shard_map.73 = bf16[32,2688]{1,0:T(8,128)(2,1)} custom-call(bf16[4,8192]{1,0:T(4,128)(2,1)} %q_ref.1, bf16[4,1024]{1,0:T(4,128)(2,1)} %k_ref.1, bf16[4,1024]{1,0:T(4,128)(2,1)} %v_ref.1, s32[1,4]{1,0:T(1,128)} %bitcast.90), custom_call_target="tpu_custom_call" | custom-call | tf_op jit(solution)/shard_map/pallas_call | solution.py:90
  1.8 0.5 broadcast.60
  2.3 1.6 %reduce.10 = bf16[32,2688]{1,0:T(8,128)(2,1)S(1)} reduce(bf16[32,1,2688]{2,0,1:T(8,128)(2,1)} %bitcast.83, bf16[]{:T(256)} %broadcast.60), dimensions={1}, to_apply=%copy.56.reduce_sub_computation | reduce | bytes 344066 | tf_op jit(solution)/shard_map/all_to_all | solution.py:121
  4.0 0.9 reshape.180
  4.8 10.2 %all-to-all-start = ((bf16[32,2,1344]{2,1,0:T(2,128)(2,1)}), bf16[32,2,1344]{2,1,0:T(2,128)(2,1)S(1)}, u32[]{:S(2)}, u32[]{:S(2)}) async-start(bf16[32,2,1344]{2,1,0:T(2,128)(2,1)} %reshape.180), calls=%async_computation | async-start | bytes 360448 | tf_op jit(solution)/shard_map/all_to_all | solution.py:121
  15.0 0.0 copy-done
  15.1 0.9 constant_dynamic-slice_fusion.1
  16.0 9.7 %all-to-all-done = bf16[32,2,1344]{2,1,0:T(2,128)(2,1)S(1)} async-done(((bf16[32,2,1344]{2,1,0:T(2,128)(2,1)}), bf16[32,2,1344]{2,1,0:T(2,128)(2,1)S(1)}, u32[]{:S(2)}, u32[]{:S(2)}) %all-to-all-start) | async-done | bytes 172064 | tf_op jit(solution)/shard_map/all_to_all | solution.py:121
  25.7 0.2 reshape.181
  25.9 1.1 %copy.57 = bf16[32,1,2688]{0,2,1:T(8,128)(2,1)S(1)} copy(bf16[32,1,2688]{2,1,0:T(2,128)(2,1)S(1)} %reshape.181) | data formatting | bytes 344064 | tf_op jit(solution)/shard_map/all_to_all | solution.py:121
  27.0 0.1 fusion.43
  27.1 0.1 copy.59
  27.2 0.1 reshape_reshape.10
  27.4 0.1 copy.58
  27.5 0.1 copy.60
  27.6 1.0 %broadcast_in_dim.23 = bf16[2,2,4,97,256]{4,3,2,1,0:T(8,128)(2,1)} broadcast(bf16[2,97,256]{2,1,0:T(8,128)(2,1)S(1)} %pad_maximum_fusion.3), dimensions={1,3,4} | broadcast | bytes 893952 | tf_op jit(solution)/shard_map/broadcast_in_dim | solution.py:162
  28.6 10.4 %all-to-all-start.1 = ((bf16[16,97,256]{2,1,0:T(8,128)(2,1)}), bf16[16,97,256]{2,1,0:T(8,128)(2,1)S(1)}, u32[]{:S(2)}, u32[]{:S(2)}) async-start(bf16[16,97,256]{2,1,0:T(8,128)(2,1)} %bitcast.7), calls=%async_computation.1 | async-start | bytes 1703936 | tf_op jit(solution)/shard_map/all_to_all | solution.py:165
  39.7 0.1 copy.61
  39.8 0.1 reshape_reshape.11
  39.9 0.2 copy.62
  40.1 0.1 reshape_reshape.12
  40.2 2.3 %collective-permute-start = (bf16[128,514]{1,0:T(8,128)(2,1)S(1)}, bf16[128,514]{1,0:T(8,128)(2,1)S(1)}, u32[]{:S(2)}, u32[]{:S(2)}) collective-permute-start(bf16[128,514]{1,0:T(8,128)(2,1)S(1)} %pad_maximum_fusion.1), channel_id=1, source_target_pairs={{0,4},{4,0},{8,12},{12,8},{1,5},{5,1},{9,13},{13,9},{2,6},{6,2},{1... | collective-permute-start | bytes 394760 | tf_op jit(solution)/shard_map/ppermute | solution.py:54
  42.5 0.1 add_compare_fusion
  42.6 0.1 reshape.177
  42.7 0.1 reshape.148
  42.8 0.2 fusion.24
  43.0 0.5 collective-permute-done
  43.5 0.1 copy.64
  43.7 0.1 copy.66
  43.8 0.2 fusion.23
  44.0 17.7 %all-to-all-done.1 = bf16[16,97,256]{2,1,0:T(8,128)(2,1)S(1)} async-done(((bf16[16,97,256]{2,1,0:T(8,128)(2,1)}), bf16[16,97,256]{2,1,0:T(8,128)(2,1)S(1)}, u32[]{:S(2)}, u32[]{:S(2)}) %all-to-all-start.1) | async-done | bytes 794656 | tf_op jit(solution)/shard_map/all_to_all | solution.py:165
  61.7 0.3 reshape.161
  62.0 0.2 fusion.12
  62.4 0.1 broadcast_compare_fusion
  62.5 0.1 pad_add_fusion
  62.7 1.3 %select_reduce_fusion = (f32[256,4]{0,1:T(4,128)S(1)}, f32[256,4,1536]{2,0,1:T(8,128)S(1)}) fusion(pred[256,1536]{1,0:T(8,128)(4,1)S(1)} %pad_add_fusion, bf16[512,128]{1,0:T(8,128)(2,1)S(1)} %get-tuple-element.20, bf16[1024,128]{1,0:T(8,128)(2,1)S(1)} %get-tuple-element.16, bf16[128,4,128]{2,0,1:T(8,128)(2,1)S(1)} %copy.66, bf16[128,4,128]{2,0,1:T(8,128)(2,1)S(1)} %copy.65), kind=kOutput, calls=%fused_computation.1 | convolution fusion | flops 408681472 | bytes 7344128 | tf_op jit(solution)/shard_map/thd,nd->thn/dot_general | solution.py:43
  64.0 1.8 %fusion = f32[256,4]{0,1:T(4,128)S(1)} fusion(f32[256,4,1536]{2,0,1:T(8,128)S(1)} %get-tuple-element.28, f32[256,4]{0,1:T(4,128)S(1)} %get-tuple-element.27, pred[256,1536]{1,0:T(8,128)(4,1)S(1)} %pad_add_fusion), kind=kLoop, calls=%fused_computation.2 | loop fusion | flops 6290432 | bytes 6692864 | tf_op jit(solution)/shard_map/reduce_sum | solution.py:46
  65.8 1.5 %fusion.2 = f32[256,4,128]{0,2,1:T(8,128)S(1)} fusion(f32[256,4,1536]{2,0,1:T(8,128)S(1)} %get-tuple-element.28, f32[256,4]{0,1:T(4,128)S(1)} %get-tuple-element.27, pred[256,1536]{1,0:T(8,128)(4,1)S(1)} %pad_add_fusion, bf16[512,128]{1,0:T(8,128)(2,1)S(1)} %get-tuple-element.19, bf16[1024,128]{1,0:T(8,128)(2,1)S(1)} %get-tuple-element.15), kind=kOutput, calls=%fused_computation.4 | convolution fusion | flops 409731072 | bytes 7606272 | tf_op jit(solution)/shard_map/thn,nd->thd/dot_general | solution.py:47
  67.4 1.9 %collective-permute-start.1 = (f32[128,520]{0,1:T(8,128)S(1)}, f32[128,520]{0,1:T(8,128)S(1)}, u32[]{:S(2)}, u32[]{:S(2)}) collective-permute-start(f32[128,520]{0,1:T(8,128)S(1)} %pad_maximum_fusion), channel_id=1, source_target_pairs={{0,4},{4,0},{8,12},{12,8},{1,5},{5,1},{9,13},{13,9},{2,6},{6,2},{1... | collective-permute-start | bytes 798728 | tf_op jit(solution)/shard_map/ppermute | solution.py:54
  69.3 1.5 %collective-permute-done.1 = f32[128,520]{0,1:T(8,128)S(1)} collective-permute-done((f32[128,520]{0,1:T(8,128)S(1)}, f32[128,520]{0,1:T(8,128)S(1)}, u32[]{:S(2)}, u32[]{:S(2)}) %collective-permute-start.1) | collective-permute-done | bytes 266272 | tf_op jit(solution)/shard_map/ppermute | solution.py:54
  70.9 0.1 fusion.16
  70.9 0.1 copy.68
  71.1 0.1 concatenate.48
  71.2 0.1 copy.81
  71.3 0.1 pad_maximum_fusion.2
  71.4 14.9 %all_to_all.22 = bf16[32,4,640]{2,1,0:T(4,128)(2,1)S(1)} all-to-all(bf16[32,4,640]{2,1,0:T(4,128)(2,1)S(1)} %pad_maximum_fusion.2), channel_id=1, replica_groups=mesh['seq'=32,'row'=4,'col'=4] {'seq'}, dimensions={0} | all-to-all | bytes 327680 | tf_op jit(solution)/shard_map/all_to_all | solution.py:210
  86.4 0.1 copy.79
  86.6 0.1 copy.75
  86.7 0.1 copy.74
  86.8 0.1 copy.72
  86.9 0.2 reshape.163
  87.1 0.3 fusion.25
  87.4 0.7 reshape.160
  (39 shorter events, 0.6 us)
Async XLA Ops:
  0.0 15.0 %copy-start = (bf16[256,1024]{1,0:T(8,128)(2,1)S(1)}, bf16[256,1024]{1,0:T(8,128)(2,1)}, u32[]{:S(2)}) copy-start(bf16[256,1024]{1,0:T(8,128)(2,1)} %param.11) | copy-start | bytes 1572868
  4.8 20.8 %all-to-all-start = ((bf16[32,2,1344]{2,1,0:T(2,128)(2,1)}), bf16[32,2,1344]{2,1,0:T(2,128)(2,1)S(1)}, u32[]{:S(2)}, u32[]{:S(2)}) async-start(bf16[32,2,1344]{2,1,0:T(2,128)(2,1)} %reshape.180), calls=%async_computation | async-start | bytes 360448 | tf_op jit(solution)/shard_map/all_to_all | solution.py:121
  28.6 33.1 %all-to-all-start.1 = ((bf16[16,97,256]{2,1,0:T(8,128)(2,1)}), bf16[16,97,256]{2,1,0:T(8,128)(2,1)S(1)}, u32[]{:S(2)}, u32[]{:S(2)}) async-start(bf16[16,97,256]{2,1,0:T(8,128)(2,1)} %bitcast.7), calls=%async_computation.1 | async-start | bytes 1703936 | tf_op jit(solution)/shard_map/all_to_all | solution.py:165
  40.2 3.3 %collective-permute-start = (bf16[128,514]{1,0:T(8,128)(2,1)S(1)}, bf16[128,514]{1,0:T(8,128)(2,1)S(1)}, u32[]{:S(2)}, u32[]{:S(2)}) collective-permute-start(bf16[128,514]{1,0:T(8,128)(2,1)S(1)} %pad_maximum_fusion.1), channel_id=1, source_target_pairs={{0,4},{4,0},{8,12},{12,8},{1,5},{5,1},{9,13},{13,9},{2,6},{6,2},{1... | collective-permute-start | bytes 394760 | tf_op jit(solution)/shard_map/ppermute | solution.py:54
  67.4 3.4 %collective-permute-start.1 = (f32[128,520]{0,1:T(8,128)S(1)}, f32[128,520]{0,1:T(8,128)S(1)}, u32[]{:S(2)}, u32[]{:S(2)}) collective-permute-start(f32[128,520]{0,1:T(8,128)S(1)} %pad_maximum_fusion), channel_id=1, source_target_pairs={{0,4},{4,0},{8,12},{12,8},{1,5},{5,1},{9,13},{13,9},{2,6},{6,2},{1... | collective-permute-start | bytes 798728 | tf_op jit(solution)/shard_map/ppermute | solution.py:54

commit v13 on v12

--- a/solution.py
+++ b/solution.py
@@ -64,7 +64,6 @@
     tok_rows = q_ref.shape[0]
     half = tok_rows // 2
     q_width = q_ref.shape[1] // (seq_count // 2)
-    q_len = tok_rows * q_width
     lanes = lax.broadcasted_iota(jnp.int32, (1, 128), 1)
     row = jnp.zeros((1, 128), jnp.float32)
     for t in range(tok_rows):
@@ -72,26 +71,28 @@
         row = jnp.where(lanes == 2 * t, (pos // code_base).astype(jnp.float32), row)
         row = jnp.where(lanes == 2 * t + 1, (pos % code_base).astype(jnp.float32), row)
     row = row.astype(o_ref.dtype)
+    zeros = jnp.zeros((1, 128), o_ref.dtype)
     for s in range(seq_count):
         group, pair, head = s // 2, s % 2, s // (seq_count // KVH)
-        for t in range(tok_rows):
-            o_ref[s : s + 1, t * q_width : (t + 1) * q_width] = q_ref[t : t + 1, group * q_width : (group + 1) * q_width]
-        for t in range(half):
-            k = pair * half + t
-            base = q_len + t * 2 * HD
-            o_ref[s : s + 1, base : base + HD] = k_ref[k : k + 1, head * HD : (head + 1) * HD]
-            o_ref[s : s + 1, base + HD : base + 2 * HD] = v_ref[k : k + 1, head * HD : (head + 1) * HD]
-        o_ref[s : s + 1, q_len + half * 2 * HD :] = row
+        for h in range(2):
+            for j in range(half):
+                t = h * half + j
+                o_ref[s, h : h + 1, j * q_width : (j + 1) * q_width] = q_ref[t : t + 1, group * q_width : (group + 1) * q_width]
+            k = pair * half + h
+            base = half * q_width
+            o_ref[s, h : h + 1, base : base + HD] = k_ref[k : k + 1, head * HD : (head + 1) * HD]
+            o_ref[s, h : h + 1, base + HD : base + 2 * HD] = v_ref[k : k + 1, head * HD : (head + 1) * HD]
+            o_ref[s, h : h + 1, base + 2 * HD :] = row if h == 0 else zeros
 
 
 def build_send(queries, new_keys, new_values, positions, seq_count):
     tok_rows = queries.shape[0]
-    width = tok_rows * (queries.shape[1] // (seq_count // 2)) + (tok_rows // 2) * 2 * HD + 128
+    width = (tok_rows // 2) * (queries.shape[1] // (seq_count // 2)) + 2 * HD + 128
     return pl.pallas_call(
         send_kernel,
         in_specs=[pl.BlockSpec(memory_space=pltpu.VMEM)] * 3 + [pl.BlockSpec(memory_space=pltpu.SMEM)],
         out_specs=pl.BlockSpec(memory_space=pltpu.VMEM),
-        out_shape=jax.ShapeDtypeStruct((seq_count, width), queries.dtype),
+        out_shape=jax.ShapeDtypeStruct((seq_count, 2, width), queries.dtype),
     )(queries, new_keys, new_values, positions.reshape(1, -1))
 
 
@@ -119,12 +120,11 @@
 
     send = build_send(queries, new_keys, new_values, positions, seq_count)
     recv = lax.all_to_all(send, "seq", 0, 0, tiled=True)
-    q_len = tok_rows * pair_heads * HD
-    kvp_len = half_tok * width
+    q_half = half_tok * pair_heads * HD
     slab_rows = seq_count * tok_rows
-    query_block = recv[:, :q_len].reshape(slab_rows, pair_heads, HD)
-    slab_kv = recv[:, q_len : q_len + kvp_len].reshape(seq_count * half_tok, width)
-    got_codes = recv[:, q_len + kvp_len : q_len + kvp_len + tok_rows * 2].reshape(seq_count, tok_rows, 2)
+    query_block = recv[:, :, :q_half].reshape(slab_rows, pair_heads, HD)
+    slab_kv = recv[:, :, q_half : q_half + width].reshape(seq_count * half_tok, width)
+    got_codes = recv[:, 0, q_half + width : q_half + width + tok_rows * 2].reshape(seq_count, tok_rows, 2)
     own_pos = decode(got_codes.reshape(slab_rows, 2))
     slab_codes = lax.dynamic_slice_in_dim(got_codes, parity * half_tok, half_tok, 1).reshape(seq_count * half_tok, 2)
 

time: 88.5 us -> 83.9 us (0.948)
  local copies, waits for them, and re-layouts: 8.1 us -> 5.1 us
  other arithmetic: 5 us -> 3.37 us
    all_to_all x1 -> x0, other arithmetic: 1.63 us -> none  [on_device(): recv = lax.all_to_all(send, 'seq', 0, 0, tiled=True)]
    all_to_all x2 -> x0, local copies, waits for them, and re-layouts: 1.59 us -> none  [on_device(): recv = lax.all_to_all(send, 'seq', 0, 0, tiled=True)]
    unnamed x6 -> x4, local copies, waits for them, and re-layouts: 1.36 us -> 0.28 us
where the time goes in v13:
time: 83.9 us; the launch traced here: 83.5 us
  waiting for transfers between devices  29.7 us (35%)
  starting transfers between devices  24.8 us (30%)
  blocking collectives  14.9 us (18%)
  local copies, waits for them, and re-layouts  5.1 us (6%)
  other arithmetic  3.37 us (4%)
  matrix products  2.82 us (3%)
  Pallas kernels  1.74 us (2%)
  between operations  1.05 us (1%)
    all_to_all x1, waiting for transfers between devices, on_device(): every = lax.all_to_all(per_dest, cell_axes, 0, 0, tiled=True)  17.9 us
    all_to_all x1, blocking collectives, on_device(): lax.all_to_all(partial.reshape(seq_count, tok_rows, -1), 'seq', 0, 0, til...  14.9 us
    all_to_all x1, starting transfers between devices, on_device(): every = lax.all_to_all(per_dest, cell_axes, 0, 0, tiled=True)  10.4 us
    all_to_all x1, starting transfers between devices, on_device(): recv = lax.all_to_all(send, 'seq', 0, 0, tiled=True)  10.2 us
    all_to_all x1, waiting for transfers between devices, on_device(): recv = lax.all_to_all(send, 'seq', 0, 0, tiled=True)  9.73 us
    ppermute x2, starting transfers between devices, swap(): return lax.ppermute(x, axes, pairs)  4.23 us
    ppermute x2, waiting for transfers between devices, swap(): return lax.ppermute(x, axes, pairs)  2.03 us
    reduce_sum x1, other arithmetic, partial_attention(): row_sum = jnp.sum(exponent, axis=-1)  1.81 us
  transfers between devices with their start and end apart: 4, of which 4 were waited for; matrix products, arithmetic and copies ran while one was open for 3% of the time, Pallas kernels for 0%

profile of v13, /device:TPU:8, one launch (start us, length us, event | category | flops | bytes accessed | tf_op | source)
XLA Modules:
  0.0 83.5 jit_solution(3822849246603154940)
XLA Ops:
  0.0 0.0 copy-start
  0.0 1.7 %shard_map.73 = bf16[32,2,1408]{2,1,0:T(2,128)(2,1)} custom-call(bf16[4,8192]{1,0:T(4,128)(2,1)} %q_ref.1, bf16[4,1024]{1,0:T(4,128)(2,1)} %k_ref.1, bf16[4,1024]{1,0:T(4,128)(2,1)} %v_ref.1, s32[1,4]{1,0:T(1,128)} %bitcast.84), custom_call_target="tpu_custom_call" | custom-call | tf_op jit(solution)/shard_map/pallas_call | solution.py:91
  1.7 10.2 %all-to-all-start = ((bf16[32,2,1408]{2,1,0:T(2,128)(2,1)}), bf16[32,2,1408]{2,1,0:T(2,128)(2,1)S(1)}, u32[]{:S(2)}, u32[]{:S(2)}) async-start(bf16[32,2,1408]{2,1,0:T(2,128)(2,1)} %shard_map.73), calls=%async_computation | async-start | bytes 360448 | tf_op jit(solution)/shard_map/all_to_all | solution.py:122
  11.9 0.0 copy-done
  12.0 0.9 %constant_dynamic-slice_fusion.1 = bf16[256,128]{1,0:T(8,128)(2,1)S(1)} fusion(bf16[256,1024]{1,0:T(8,128)(2,1)} %param.12, s32[]{:T(128)S(6)} %select_n.35), kind=kLoop, calls=%fused_computation.75 | loop fusion | bytes 131076 | tf_op jit(solution)/shard_map/dynamic_slice | solution.py:140
  12.9 9.7 %all-to-all-done = bf16[32,2,1408]{2,1,0:T(2,128)(2,1)S(1)} async-done(((bf16[32,2,1408]{2,1,0:T(2,128)(2,1)}), bf16[32,2,1408]{2,1,0:T(2,128)(2,1)S(1)}, u32[]{:S(2)}, u32[]{:S(2)}) %all-to-all-start) | async-done | bytes 180256 | tf_op jit(solution)/shard_map/all_to_all | solution.py:122
  22.6 0.1 slice_reduce_fusion
  22.6 0.1 copy.41
  22.7 0.1 copy.42
  22.9 0.1 reshape_reshape.6
  23.1 1.0 %broadcast_in_dim.23 = bf16[2,2,4,97,256]{4,3,2,1,0:T(8,128)(2,1)} broadcast(bf16[2,97,256]{2,1,0:T(8,128)(2,1)S(1)} %pad_maximum_fusion.3), dimensions={1,3,4} | broadcast | bytes 893952 | tf_op jit(solution)/shard_map/broadcast_in_dim | solution.py:162
  24.1 10.4 %all-to-all-start.1 = ((bf16[16,97,256]{2,1,0:T(8,128)(2,1)}), bf16[16,97,256]{2,1,0:T(8,128)(2,1)S(1)}, u32[]{:S(2)}, u32[]{:S(2)}) async-start(bf16[16,97,256]{2,1,0:T(8,128)(2,1)} %bitcast.5), calls=%async_computation.1 | async-start | bytes 1703936 | tf_op jit(solution)/shard_map/all_to_all | solution.py:165
  35.2 0.1 reshape_reshape_squeeze.4
  35.3 0.1 slice.175
  35.4 0.1 reshape_reshape.7
  35.5 2.3 %collective-permute-start = (bf16[128,514]{1,0:T(8,128)(2,1)S(1)}, bf16[128,514]{1,0:T(8,128)(2,1)S(1)}, u32[]{:S(2)}, u32[]{:S(2)}) collective-permute-start(bf16[128,514]{1,0:T(8,128)(2,1)S(1)} %pad_maximum_fusion.1), channel_id=1, source_target_pairs={{0,4},{4,0},{8,12},{12,8},{1,5},{5,1},{9,13},{13,9},{2,6},{6,2},{1... | collective-permute-start | bytes 394760 | tf_op jit(solution)/shard_map/ppermute | solution.py:54
  37.8 0.1 add_compare_fusion
  37.9 0.1 reshape.172
  38.0 0.1 reshape.142
  38.1 0.2 fusion.24
  38.3 0.5 collective-permute-done
  38.8 0.1 copy.43
  38.9 0.1 copy.45
  39.1 0.2 fusion.23
  39.3 17.9 %all-to-all-done.1 = bf16[16,97,256]{2,1,0:T(8,128)(2,1)S(1)} async-done(((bf16[16,97,256]{2,1,0:T(8,128)(2,1)}), bf16[16,97,256]{2,1,0:T(8,128)(2,1)S(1)}, u32[]{:S(2)}, u32[]{:S(2)}) %all-to-all-start.1) | async-done | bytes 794656 | tf_op jit(solution)/shard_map/all_to_all | solution.py:165
  57.2 0.3 reshape.155
  57.5 0.2 fusion.12
  57.9 0.1 broadcast_compare_fusion
  58.0 0.1 pad_add_fusion
  58.2 1.3 %select_reduce_fusion = (f32[256,4]{0,1:T(4,128)S(1)}, f32[256,4,1536]{2,0,1:T(8,128)S(1)}) fusion(pred[256,1536]{1,0:T(8,128)(4,1)S(1)} %pad_add_fusion, bf16[512,128]{1,0:T(8,128)(2,1)S(1)} %get-tuple-element.18, bf16[1024,128]{1,0:T(8,128)(2,1)S(1)} %get-tuple-element.14, bf16[128,4,128]{2,0,1:T(8,128)(2,1)S(1)} %copy.45, bf16[128,4,128]{2,0,1:T(8,128)(2,1)S(1)} %copy.44), kind=kOutput, calls=%fused_computation.1 | convolution fusion | flops 408681472 | bytes 7344128 | tf_op jit(solution)/shard_map/thd,nd->thn/dot_general | solution.py:43
  59.5 1.8 %fusion = f32[256,4]{0,1:T(4,128)S(1)} fusion(f32[256,4,1536]{2,0,1:T(8,128)S(1)} %get-tuple-element.30, f32[256,4]{0,1:T(4,128)S(1)} %get-tuple-element.29, pred[256,1536]{1,0:T(8,128)(4,1)S(1)} %pad_add_fusion), kind=kLoop, calls=%fused_computation.2 | loop fusion | flops 6290432 | bytes 6692864 | tf_op jit(solution)/shard_map/reduce_sum | solution.py:46
  61.3 1.5 %fusion.2 = f32[256,4,128]{0,2,1:T(8,128)S(1)} fusion(f32[256,4,1536]{2,0,1:T(8,128)S(1)} %get-tuple-element.30, f32[256,4]{0,1:T(4,128)S(1)} %get-tuple-element.29, pred[256,1536]{1,0:T(8,128)(4,1)S(1)} %pad_add_fusion, bf16[512,128]{1,0:T(8,128)(2,1)S(1)} %get-tuple-element.17, bf16[1024,128]{1,0:T(8,128)(2,1)S(1)} %get-tuple-element.13), kind=kOutput, calls=%fused_computation.4 | convolution fusion | flops 409731072 | bytes 7606272 | tf_op jit(solution)/shard_map/thn,nd->thd/dot_general | solution.py:47
  62.9 1.9 %collective-permute-start.1 = (f32[128,520]{0,1:T(8,128)S(1)}, f32[128,520]{0,1:T(8,128)S(1)}, u32[]{:S(2)}, u32[]{:S(2)}) collective-permute-start(f32[128,520]{0,1:T(8,128)S(1)} %pad_maximum_fusion), channel_id=1, source_target_pairs={{0,4},{4,0},{8,12},{12,8},{1,5},{5,1},{9,13},{13,9},{2,6},{6,2},{1... | collective-permute-start | bytes 798728 | tf_op jit(solution)/shard_map/ppermute | solution.py:54
  64.8 1.5 %collective-permute-done.1 = f32[128,520]{0,1:T(8,128)S(1)} collective-permute-done((f32[128,520]{0,1:T(8,128)S(1)}, f32[128,520]{0,1:T(8,128)S(1)}, u32[]{:S(2)}, u32[]{:S(2)}) %collective-permute-start.1) | collective-permute-done | bytes 266272 | tf_op jit(solution)/shard_map/ppermute | solution.py:54
  66.3 0.1 fusion.16
  66.4 0.1 copy.47
  66.5 0.1 concatenate.48
  66.7 0.1 copy.60
  66.8 0.1 pad_maximum_fusion.2
  66.9 14.9 %all_to_all.15 = bf16[32,4,640]{2,1,0:T(4,128)(2,1)S(1)} all-to-all(bf16[32,4,640]{2,1,0:T(4,128)(2,1)S(1)} %pad_maximum_fusion.2), channel_id=1, replica_groups=mesh['seq'=32,'row'=4,'col'=4] {'seq'}, dimensions={0} | all-to-all | bytes 327680 | tf_op jit(solution)/shard_map/all_to_all | solution.py:210
  81.9 0.1 copy.58
  82.1 0.1 copy.54
  82.2 0.1 copy.53
  82.3 0.1 copy.51
  82.4 0.2 reshape.157
  82.6 0.3 fusion.25
  82.8 0.7 reshape.154
  (38 shorter events, 0.6 us)
Async XLA Ops:
  0.0 11.9 %copy-start = (bf16[256,1024]{1,0:T(8,128)(2,1)S(1)}, bf16[256,1024]{1,0:T(8,128)(2,1)}, u32[]{:S(2)}) copy-start(bf16[256,1024]{1,0:T(8,128)(2,1)} %param.11) | copy-start | bytes 1572868
  1.7 20.8 %all-to-all-start = ((bf16[32,2,1408]{2,1,0:T(2,128)(2,1)}), bf16[32,2,1408]{2,1,0:T(2,128)(2,1)S(1)}, u32[]{:S(2)}, u32[]{:S(2)}) async-start(bf16[32,2,1408]{2,1,0:T(2,128)(2,1)} %shard_map.73), calls=%async_computation | async-start | bytes 360448 | tf_op jit(solution)/shard_map/all_to_all | solution.py:122
  24.1 33.1 %all-to-all-start.1 = ((bf16[16,97,256]{2,1,0:T(8,128)(2,1)}), bf16[16,97,256]{2,1,0:T(8,128)(2,1)S(1)}, u32[]{:S(2)}, u32[]{:S(2)}) async-start(bf16[16,97,256]{2,1,0:T(8,128)(2,1)} %bitcast.5), calls=%async_computation.1 | async-start | bytes 1703936 | tf_op jit(solution)/shard_map/all_to_all | solution.py:165
  35.5 3.3 %collective-permute-start = (bf16[128,514]{1,0:T(8,128)(2,1)S(1)}, bf16[128,514]{1,0:T(8,128)(2,1)S(1)}, u32[]{:S(2)}, u32[]{:S(2)}) collective-permute-start(bf16[128,514]{1,0:T(8,128)(2,1)S(1)} %pad_maximum_fusion.1), channel_id=1, source_target_pairs={{0,4},{4,0},{8,12},{12,8},{1,5},{5,1},{9,13},{13,9},{2,6},{6,2},{1... | collective-permute-start | bytes 394760 | tf_op jit(solution)/shard_map/ppermute | solution.py:54
  62.9 3.4 %collective-permute-start.1 = (f32[128,520]{0,1:T(8,128)S(1)}, f32[128,520]{0,1:T(8,128)S(1)}, u32[]{:S(2)}, u32[]{:S(2)}) collective-permute-start(f32[128,520]{0,1:T(8,128)S(1)} %pad_maximum_fusion), channel_id=1, source_target_pairs={{0,4},{4,0},{8,12},{12,8},{1,5},{5,1},{9,13},{13,9},{2,6},{6,2},{1... | collective-permute-start | bytes 798728 | tf_op jit(solution)/shard_map/ppermute | solution.py:54

commit v14 on v13

--- a/solution.py
+++ b/solution.py
@@ -174,26 +174,25 @@
     keys = jnp.concatenate([cache_got[:, :HD], slab_got[:, :HD]], axis=0)
     values = jnp.concatenate([cache_got[:, HD:], slab_got[:, HD:]], axis=0)
 
-    both_q = jnp.concatenate([query_block, partner_block], axis=0)
-    both_pos = jnp.concatenate([own_pos, partner_pos], axis=0)
-    row_max, row_sum, summed = partial_attention(
-        both_q, both_pos, keys, values, key_pos_cache, key_pos_slab, cache_got.shape[0], first_pos
-    )
-
-    theirs = jnp.concatenate(
-        [summed[slab_rows:].reshape(slab_rows, -1), row_max[slab_rows:], row_sum[slab_rows:]], axis=1
-    )
+    cache_count = cache_got.shape[0]
+    their_max, their_sum, their_summed = partial_attention(
+        partner_block, partner_pos, keys, values, key_pos_cache, key_pos_slab, cache_count, first_pos
+    )
+    theirs = jnp.concatenate([their_summed.reshape(slab_rows, -1), their_max, their_sum], axis=1)
     got = swap(theirs, "row", core_pairs)
+    mine_max, mine_sum, mine_summed = partial_attention(
+        query_block, own_pos, keys, values, key_pos_cache, key_pos_slab, cache_count, first_pos
+    )
+
     split_at = pair_heads * HD
     other_summed = got[:, :split_at].reshape(slab_rows, pair_heads, HD)
     other_max = got[:, split_at : split_at + pair_heads]
     other_sum = got[:, split_at + pair_heads :]
-    mine_max = row_max[:slab_rows]
     top = jnp.maximum(mine_max, other_max)
     scale_mine = jnp.exp(mine_max - top)
     scale_other = jnp.exp(other_max - top)
-    numerator = summed[:slab_rows] * scale_mine[..., None] + other_summed * scale_other[..., None]
-    denominator = row_sum[:slab_rows] * scale_mine + other_sum * scale_other
+    numerator = mine_summed * scale_mine[..., None] + other_summed * scale_other[..., None]
+    denominator = mine_sum * scale_mine + other_sum * scale_other
     normed = (numerator / denominator[..., None]).astype(jnp.bfloat16).reshape(slab_rows, -1)
     log_weight = top + jnp.log(denominator)
     pieces = []

time: 83.9 us -> 83.1 us (level)
  waiting for transfers between devices: 29.7 us -> 28.3 us
    ppermute x2, waiting for transfers between devices: 2.03 us -> 0.56 us  [swap(): return lax.ppermute(x, axes, pairs)]
    reduce_sum x1 -> x2, other arithmetic: 1.81 us -> 1.56 us  [partial_attention(): row_sum = jnp.sum(exponent, axis=-1)]
  transfers between devices with their start and end apart: 4 -> 4, of which waited for: 4 -> 3; matrix products, arithmetic and copies ran while one was open for 3% -> 5% of each run, Pallas kernels for 0% -> 0%
where the time goes in v14:
time: 83.1 us; the launch traced here: 82.7 us
  waiting for transfers between devices  28.3 us (34%)
  starting transfers between devices  24.8 us (30%)
  blocking collectives  15.3 us (18%)
  local copies, waits for them, and re-layouts  5.03 us (6%)
  other arithmetic  3.34 us (4%)
  matrix products  3.12 us (4%)
  Pallas kernels  1.74 us (2%)
  between operations  1.05 us (1%)
    all_to_all x1, waiting for transfers between devices, on_device(): every = lax.all_to_all(per_dest, cell_axes, 0, 0, tiled=True)  18.1 us
    all_to_all x1, blocking collectives, on_device(): lax.all_to_all(partial.reshape(seq_count, tok_rows, -1), 'seq', 0, 0, til...  15.3 us
    all_to_all x1, starting transfers between devices, on_device(): every = lax.all_to_all(per_dest, cell_axes, 0, 0, tiled=True)  10.4 us
    all_to_all x1, starting transfers between devices, on_device(): recv = lax.all_to_all(send, 'seq', 0, 0, tiled=True)  10.2 us
    all_to_all x1, waiting for transfers between devices, on_device(): recv = lax.all_to_all(send, 'seq', 0, 0, tiled=True)  9.73 us
    ppermute x2, starting transfers between devices, swap(): return lax.ppermute(x, axes, pairs)  4.23 us
    pallas_call x1, Pallas kernels, build_send(): pl.pallas_call(send_kernel, in_specs=[pl.BlockSpec(memory_space=pltpu.VME...  1.74 us
  transfers between devices with their start and end apart: 4, of which 3 were waited for; matrix products, arithmetic and copies ran while one was open for 5% of the time, Pallas kernels for 0%

profile of v14, /device:TPU:8, one launch (start us, length us, event | category | flops | bytes accessed | tf_op | source)
XLA Modules:
  0.0 82.7 jit_solution(12283461941037682625)
XLA Ops:
  0.0 0.0 copy-start
  0.0 1.7 %shard_map.73 = bf16[32,2,1408]{2,1,0:T(2,128)(2,1)} custom-call(bf16[4,8192]{1,0:T(4,128)(2,1)} %q_ref.1, bf16[4,1024]{1,0:T(4,128)(2,1)} %k_ref.1, bf16[4,1024]{1,0:T(4,128)(2,1)} %v_ref.1, s32[1,4]{1,0:T(1,128)} %bitcast.92), custom_call_target="tpu_custom_call" | custom-call | tf_op jit(solution)/shard_map/pallas_call | solution.py:91
  1.7 10.2 %all-to-all-start = ((bf16[32,2,1408]{2,1,0:T(2,128)(2,1)}), bf16[32,2,1408]{2,1,0:T(2,128)(2,1)S(1)}, u32[]{:S(2)}, u32[]{:S(2)}) async-start(bf16[32,2,1408]{2,1,0:T(2,128)(2,1)} %shard_map.73), calls=%async_computation | async-start | bytes 360448 | tf_op jit(solution)/shard_map/all_to_all | solution.py:122
  11.9 0.0 copy-done
  12.0 0.9 %constant_dynamic-slice_fusion.1 = bf16[256,128]{1,0:T(8,128)(2,1)S(1)} fusion(bf16[256,1024]{1,0:T(8,128)(2,1)} %param.12, s32[]{:T(128)S(6)} %select_n.41), kind=kLoop, calls=%fused_computation.78 | loop fusion | bytes 131076 | tf_op jit(solution)/shard_map/dynamic_slice | solution.py:140
  12.9 9.7 %all-to-all-done = bf16[32,2,1408]{2,1,0:T(2,128)(2,1)S(1)} async-done(((bf16[32,2,1408]{2,1,0:T(2,128)(2,1)}), bf16[32,2,1408]{2,1,0:T(2,128)(2,1)S(1)}, u32[]{:S(2)}, u32[]{:S(2)}) %all-to-all-start) | async-done | bytes 180256 | tf_op jit(solution)/shard_map/all_to_all | solution.py:122
  22.6 0.1 slice_reduce_fusion
  22.6 0.1 copy.59
  22.7 0.1 copy.60
  22.9 0.1 reshape_reshape.6
  23.1 1.0 %broadcast_in_dim.33 = bf16[2,2,4,97,256]{4,3,2,1,0:T(8,128)(2,1)} broadcast(bf16[2,97,256]{2,1,0:T(8,128)(2,1)S(1)} %pad_maximum_fusion.3), dimensions={1,3,4} | broadcast | bytes 893952 | tf_op jit(solution)/shard_map/broadcast_in_dim | solution.py:162
  24.1 10.4 %all-to-all-start.1 = ((bf16[16,97,256]{2,1,0:T(8,128)(2,1)}), bf16[16,97,256]{2,1,0:T(8,128)(2,1)S(1)}, u32[]{:S(2)}, u32[]{:S(2)}) async-start(bf16[16,97,256]{2,1,0:T(8,128)(2,1)} %bitcast.5), calls=%async_computation.1 | async-start | bytes 1703936 | tf_op jit(solution)/shard_map/all_to_all | solution.py:165
  35.2 0.1 reshape_reshape_squeeze.4
  35.3 0.1 slice.151
  35.4 0.1 reshape_reshape.7
  35.5 2.3 %collective-permute-start = (bf16[128,514]{1,0:T(8,128)(2,1)S(1)}, bf16[128,514]{1,0:T(8,128)(2,1)S(1)}, u32[]{:S(2)}, u32[]{:S(2)}) collective-permute-start(bf16[128,514]{1,0:T(8,128)(2,1)S(1)} %pad_maximum_fusion.1), channel_id=1, source_target_pairs={{0,4},{4,0},{8,12},{12,8},{1,5},{5,1},{9,13},{13,9},{2,6},{6,2},{1... | collective-permute-start | bytes 394760 | tf_op jit(solution)/shard_map/ppermute | solution.py:54
  37.8 0.1 add_compare_fusion
  37.9 0.1 reshape.168
  38.0 0.1 reshape.137
  38.1 0.2 fusion.23
  38.2 0.6 collective-permute-done
  38.8 0.1 copy.62
  38.9 0.2 fusion.22
  39.1 18.1 %all-to-all-done.1 = bf16[16,97,256]{2,1,0:T(8,128)(2,1)S(1)} async-done(((bf16[16,97,256]{2,1,0:T(8,128)(2,1)}), bf16[16,97,256]{2,1,0:T(8,128)(2,1)S(1)}, u32[]{:S(2)}, u32[]{:S(2)}) %all-to-all-start.1) | async-done | bytes 794656 | tf_op jit(solution)/shard_map/all_to_all | solution.py:165
  57.2 0.3 reshape.150
  57.5 0.2 fusion.14
  57.9 0.1 broadcast_compare_fusion
  58.0 0.1 pad_add_fusion.1
  58.2 0.8 %select_reduce_fusion = (f32[128,4]{0,1:T(4,128)S(1)}, f32[128,4,1536]{2,0,1:T(8,128)S(1)}) fusion(pred[128,1536]{1,0:T(8,128)(4,1)S(1)} %get-tuple-element.25, bf16[128,4,128]{0,2,1:T(8,128)(2,1)S(1)} %bitcast.89, bf16[512,128]{1,0:T(8,128)(2,1)S(1)} %get-tuple-element.16, bf16[1024,128]{1,0:T(8,128)(2,1)S(1)} %get-tuple-element.14), kind=kOutput, calls=%fused_computation.3 | convolution fusion | flops 204471808 | bytes 3868672 | tf_op jit(solution)/shard_map/thd,nd->thn/dot_general | solution.py:43
  59.0 0.8 fusion.2
  59.8 0.8 %fusion.4 = f32[128,4,128]{0,2,1:T(8,128)S(1)} fusion(f32[128,4,1536]{2,0,1:T(8,128)S(1)} %get-tuple-element.34, f32[128,4]{0,1:T(4,128)S(1)} %get-tuple-element.33, pred[128,1536]{1,0:T(8,128)(4,1)S(1)} %get-tuple-element.25, bf16[512,128]{1,0:T(8,128)(2,1)S(1)} %get-tuple-element.15, bf16[1024,128]{1,0:T(8,128)(2,1)S(1)} %get-tuple-element.13), kind=kOutput, calls=%fused_computation.10 | convolution fusion | flops 204472320 | bytes 3999744 | tf_op jit(solution)/shard_map/thn,nd->thd/dot_general | solution.py:47
  60.6 1.9 %collective-permute-start.1 = (f32[128,520]{0,1:T(8,128)S(1)}, f32[128,520]{0,1:T(8,128)S(1)}, u32[]{:S(2)}, u32[]{:S(2)}) collective-permute-start(f32[128,520]{0,1:T(8,128)S(1)} %pad_maximum_fusion), channel_id=1, source_target_pairs={{0,4},{4,0},{8,12},{12,8},{1,5},{5,1},{9,13},{13,9},{2,6},{6,2},{1... | collective-permute-start | bytes 798728 | tf_op jit(solution)/shard_map/ppermute | solution.py:54
  62.6 0.8 select_reduce_fusion.1
  63.3 0.7 fusion.6
  64.0 0.8 fusion
  64.8 0.0 collective-permute-done.1
  64.9 0.1 copy.65
  65.0 0.3 divide_convert_fusion
  65.3 0.1 copy.66
  65.4 0.1 concatenate.44
  65.5 0.1 copy.67
  65.7 0.1 pad_maximum_fusion.2
  65.7 15.3 %all_to_all.15 = bf16[32,4,640]{2,1,0:T(4,128)(2,1)S(1)} all-to-all(bf16[32,4,640]{2,1,0:T(4,128)(2,1)S(1)} %pad_maximum_fusion.2), channel_id=1, replica_groups=mesh['seq'=32,'row'=4,'col'=4] {'seq'}, dimensions={0} | all-to-all | bytes 327680 | tf_op jit(solution)/shard_map/all_to_all | solution.py:209
  81.0 0.1 copy.78
  81.2 0.1 copy.72
  81.4 0.1 copy.71
  81.5 0.1 copy.70
  81.6 0.2 reshape.152
  81.7 0.3 fusion.24
  82.0 0.7 reshape.149
  (33 shorter events, 0.5 us)
Async XLA Ops:
  0.0 11.9 %copy-start = (bf16[256,1024]{1,0:T(8,128)(2,1)S(1)}, bf16[256,1024]{1,0:T(8,128)(2,1)}, u32[]{:S(2)}) copy-start(bf16[256,1024]{1,0:T(8,128)(2,1)} %param.11) | copy-start | bytes 1572868
  1.7 20.8 %all-to-all-start = ((bf16[32,2,1408]{2,1,0:T(2,128)(2,1)}), bf16[32,2,1408]{2,1,0:T(2,128)(2,1)S(1)}, u32[]{:S(2)}, u32[]{:S(2)}) async-start(bf16[32,2,1408]{2,1,0:T(2,128)(2,1)} %shard_map.73), calls=%async_computation | async-start | bytes 360448 | tf_op jit(solution)/shard_map/all_to_all | solution.py:122
  24.1 33.1 %all-to-all-start.1 = ((bf16[16,97,256]{2,1,0:T(8,128)(2,1)}), bf16[16,97,256]{2,1,0:T(8,128)(2,1)S(1)}, u32[]{:S(2)}, u32[]{:S(2)}) async-start(bf16[16,97,256]{2,1,0:T(8,128)(2,1)} %bitcast.5), calls=%async_computation.1 | async-start | bytes 1703936 | tf_op jit(solution)/shard_map/all_to_all | solution.py:165
  35.5 3.3 %collective-permute-start = (bf16[128,514]{1,0:T(8,128)(2,1)S(1)}, bf16[128,514]{1,0:T(8,128)(2,1)S(1)}, u32[]{:S(2)}, u32[]{:S(2)}) collective-permute-start(bf16[128,514]{1,0:T(8,128)(2,1)S(1)} %pad_maximum_fusion.1), channel_id=1, source_target_pairs={{0,4},{4,0},{8,12},{12,8},{1,5},{5,1},{9,13},{13,9},{2,6},{6,2},{1... | collective-permute-start | bytes 394760 | tf_op jit(solution)/shard_map/ppermute | solution.py:54
  60.6 4.2 %collective-permute-start.1 = (f32[128,520]{0,1:T(8,128)S(1)}, f32[128,520]{0,1:T(8,128)S(1)}, u32[]{:S(2)}, u32[]{:S(2)}) collective-permute-start(f32[128,520]{0,1:T(8,128)S(1)} %pad_maximum_fusion), channel_id=1, source_target_pairs={{0,4},{4,0},{8,12},{12,8},{1,5},{5,1},{9,13},{13,9},{2,6},{6,2},{1... | collective-permute-start | bytes 798728 | tf_op jit(solution)/shard_map/ppermute | solution.py:54

commit v15 on v14

--- a/solution.py
+++ b/solution.py
@@ -159,10 +159,13 @@
             for b in range(2)
         ]
     )
+    chunk_rows = halves.shape[1] * width // 128
+    halves = halves.reshape(2, chunk_rows, 128)
     per_dest = jnp.broadcast_to(
         halves[None, :, None], (row_count // 2, 2, col_count) + halves.shape[1:]
     ).reshape((cell_count,) + halves.shape[1:])
     every = lax.all_to_all(per_dest, cell_axes, 0, 0, tiled=True)
+    every = every.reshape(cell_count, -1, width)
     cache_got = every[:, :part_cache].reshape(-1, width)
     slab_got = every[:, part_cache : part_cache + half_slab].reshape(-1, width)
     key_pos_slab = decode(every[:, part_cache + half_slab, : 2 * half_slab].reshape(-1, 2))

time: 83.1 us -> 82.7 us (level)
  no operation moved by 1% of the time
where the time goes in v15:
time: 82.7 us; the launch traced here: 82.3 us
  waiting for transfers between devices  27.6 us (33%)
  starting transfers between devices  24.8 us (30%)
  blocking collectives  15.2 us (18%)
  local copies, waits for them, and re-layouts  5.37 us (6%)
  other arithmetic  3.33 us (4%)
  matrix products  3.11 us (4%)
  Pallas kernels  1.74 us (2%)
  between operations  1.07 us (1%)
    all_to_all x1, waiting for transfers between devices, on_device(): every = lax.all_to_all(per_dest, cell_axes, 0, 0, tiled=True)  17.3 us
    all_to_all x1, blocking collectives, on_device(): lax.all_to_all(partial.reshape(seq_count, tok_rows, -1), 'seq', 0, 0, til...  15.2 us
    all_to_all x1, starting transfers between devices, on_device(): every = lax.all_to_all(per_dest, cell_axes, 0, 0, tiled=True)  10.4 us
    all_to_all x1, starting transfers between devices, on_device(): recv = lax.all_to_all(send, 'seq', 0, 0, tiled=True)  10.2 us
    all_to_all x1, waiting for transfers between devices, on_device(): recv = lax.all_to_all(send, 'seq', 0, 0, tiled=True)  9.73 us
    ppermute x2, starting transfers between devices, swap(): return lax.ppermute(x, axes, pairs)  4.23 us
    pallas_call x1, Pallas kernels, build_send(): pl.pallas_call(send_kernel, in_specs=[pl.BlockSpec(memory_space=pltpu.VME...  1.74 us
  transfers between devices with their start and end apart: 4, of which 3 were waited for; matrix products, arithmetic and copies ran while one was open for 5% of the time, Pallas kernels for 0%

profile of v15, /device:TPU:8, one launch (start us, length us, event | category | flops | bytes accessed | tf_op | source)
XLA Modules:
  0.0 82.3 jit_solution(8896277507180084001)
XLA Ops:
  0.0 0.0 copy-start
  0.0 1.7 %shard_map.73 = bf16[32,2,1408]{2,1,0:T(2,128)(2,1)} custom-call(bf16[4,8192]{1,0:T(4,128)(2,1)} %q_ref.1, bf16[4,1024]{1,0:T(4,128)(2,1)} %k_ref.1, bf16[4,1024]{1,0:T(4,128)(2,1)} %v_ref.1, s32[1,4]{1,0:T(1,128)} %bitcast.90), custom_call_target="tpu_custom_call" | custom-call | tf_op jit(solution)/shard_map/pallas_call | solution.py:91
  1.7 10.2 %all-to-all-start = ((bf16[32,2,1408]{2,1,0:T(2,128)(2,1)}), bf16[32,2,1408]{2,1,0:T(2,128)(2,1)S(1)}, u32[]{:S(2)}, u32[]{:S(2)}) async-start(bf16[32,2,1408]{2,1,0:T(2,128)(2,1)} %shard_map.73), calls=%async_computation | async-start | bytes 360448 | tf_op jit(solution)/shard_map/all_to_all | solution.py:122
  11.9 0.0 copy-done
  12.0 0.9 %constant_dynamic-slice_fusion.1 = bf16[256,128]{1,0:T(8,128)(2,1)S(1)} fusion(bf16[256,1024]{1,0:T(8,128)(2,1)} %param.12, s32[]{:T(128)S(6)} %select_n.41), kind=kLoop, calls=%fused_computation.78 | loop fusion | bytes 131076 | tf_op jit(solution)/shard_map/dynamic_slice | solution.py:140
  12.9 9.7 %all-to-all-done = bf16[32,2,1408]{2,1,0:T(2,128)(2,1)S(1)} async-done(((bf16[32,2,1408]{2,1,0:T(2,128)(2,1)}), bf16[32,2,1408]{2,1,0:T(2,128)(2,1)S(1)}, u32[]{:S(2)}, u32[]{:S(2)}) %all-to-all-start) | async-done | bytes 180256 | tf_op jit(solution)/shard_map/all_to_all | solution.py:122
  22.6 0.1 slice_reduce_fusion
  22.6 0.1 copy.53
  22.7 0.1 copy.54
  22.9 0.1 reshape_reshape.6
  23.2 1.0 %broadcast_in_dim.63 = bf16[2,2,4,194,128]{4,3,2,1,0:T(8,128)(2,1)} broadcast(bf16[2,194,128]{2,1,0:T(8,128)(2,1)S(1)} %maximum_bitcast_fusion.6), dimensions={1,3,4} | broadcast | bytes 893952 | tf_op jit(solution)/shard_map/broadcast_in_dim | solution.py:164
  24.2 10.4 %all-to-all-start.1 = ((bf16[16,194,128]{2,1,0:T(8,128)(2,1)}), bf16[16,194,128]{2,1,0:T(8,128)(2,1)S(1)}, u32[]{:S(2)}, u32[]{:S(2)}) async-start(bf16[16,194,128]{2,1,0:T(8,128)(2,1)} %bitcast.4), calls=%async_computation.1 | async-start | bytes 1638400 | tf_op jit(solution)/shard_map/all_to_all | solution.py:167
  35.3 0.1 reshape_reshape_squeeze.4
  35.3 0.1 slice.151
  35.4 0.1 reshape_reshape.7
  35.6 2.3 %collective-permute-start = (bf16[128,514]{1,0:T(8,128)(2,1)S(1)}, bf16[128,514]{1,0:T(8,128)(2,1)S(1)}, u32[]{:S(2)}, u32[]{:S(2)}) collective-permute-start(bf16[128,514]{1,0:T(8,128)(2,1)S(1)} %pad_maximum_fusion.1), channel_id=1, source_target_pairs={{0,4},{4,0},{8,12},{12,8},{1,5},{5,1},{9,13},{13,9},{2,6},{6,2},{1... | collective-permute-start | bytes 394760 | tf_op jit(solution)/shard_map/ppermute | solution.py:54
  37.9 0.1 add_compare_fusion
  38.0 0.1 reshape.175
  38.1 0.1 reshape.144
  38.2 0.2 fusion.23
  38.3 0.6 collective-permute-done
  38.9 0.1 copy.56
  39.0 0.2 fusion.22
  39.2 17.3 %all-to-all-done.1 = bf16[16,194,128]{2,1,0:T(8,128)(2,1)S(1)} async-done(((bf16[16,194,128]{2,1,0:T(8,128)(2,1)}), bf16[16,194,128]{2,1,0:T(8,128)(2,1)S(1)}, u32[]{:S(2)}, u32[]{:S(2)}) %all-to-all-start.1) | async-done | bytes 794656 | tf_op jit(solution)/shard_map/all_to_all | solution.py:167
  56.6 0.3 reshape.143
  56.9 0.3 reshape.157
  57.2 0.2 fusion.14
  57.5 0.1 broadcast_compare_fusion
  57.7 0.1 pad_add_fusion.1
  57.8 0.8 %select_reduce_fusion = (f32[128,4]{0,1:T(4,128)S(1)}, f32[128,4,1536]{2,0,1:T(8,128)S(1)}) fusion(pred[128,1536]{1,0:T(8,128)(4,1)S(1)} %get-tuple-element.25, bf16[128,4,128]{0,2,1:T(8,128)(2,1)S(1)} %bitcast.87, bf16[512,128]{1,0:T(8,128)(2,1)S(1)} %get-tuple-element.16, bf16[1024,128]{1,0:T(8,128)(2,1)S(1)} %get-tuple-element.14), kind=kOutput, calls=%fused_computation.3 | convolution fusion | flops 204471808 | bytes 3868672 | tf_op jit(solution)/shard_map/thd,nd->thn/dot_general | solution.py:43
  58.6 0.8 fusion.2
  59.4 0.8 %fusion.4 = f32[128,4,128]{0,2,1:T(8,128)S(1)} fusion(f32[128,4,1536]{2,0,1:T(8,128)S(1)} %get-tuple-element.34, f32[128,4]{0,1:T(4,128)S(1)} %get-tuple-element.33, pred[128,1536]{1,0:T(8,128)(4,1)S(1)} %get-tuple-element.25, bf16[512,128]{1,0:T(8,128)(2,1)S(1)} %get-tuple-element.15, bf16[1024,128]{1,0:T(8,128)(2,1)S(1)} %get-tuple-element.13), kind=kOutput, calls=%fused_computation.10 | convolution fusion | flops 204472320 | bytes 3999744 | tf_op jit(solution)/shard_map/thn,nd->thd/dot_general | solution.py:47
  60.3 1.9 %collective-permute-start.1 = (f32[128,520]{0,1:T(8,128)S(1)}, f32[128,520]{0,1:T(8,128)S(1)}, u32[]{:S(2)}, u32[]{:S(2)}) collective-permute-start(f32[128,520]{0,1:T(8,128)S(1)} %pad_maximum_fusion), channel_id=1, source_target_pairs={{0,4},{4,0},{8,12},{12,8},{1,5},{5,1},{9,13},{13,9},{2,6},{6,2},{1... | collective-permute-start | bytes 798728 | tf_op jit(solution)/shard_map/ppermute | solution.py:54
  62.2 0.8 select_reduce_fusion.1
  63.0 0.7 fusion.6
  63.7 0.8 fusion
  64.5 0.0 collective-permute-done.1
  64.5 0.1 copy.59
  64.6 0.3 divide_convert_fusion
  64.9 0.1 copy.60
  65.0 0.1 concatenate.45
  65.1 0.1 copy.61
  65.3 0.1 pad_maximum_fusion.2
  65.4 15.2 %all_to_all.15 = bf16[32,4,640]{2,1,0:T(4,128)(2,1)S(1)} all-to-all(bf16[32,4,640]{2,1,0:T(4,128)(2,1)S(1)} %pad_maximum_fusion.2), channel_id=1, replica_groups=mesh['seq'=32,'row'=4,'col'=4] {'seq'}, dimensions={0} | all-to-all | bytes 327680 | tf_op jit(solution)/shard_map/all_to_all | solution.py:212
  80.7 0.1 copy.72
  80.9 0.1 copy.66
  81.0 0.1 copy.65
  81.1 0.1 copy.64
  81.2 0.2 reshape.159
  81.4 0.3 fusion.24
  81.7 0.7 reshape.156
  (35 shorter events, 0.6 us)
Async XLA Ops:
  0.0 11.9 %copy-start = (bf16[256,1024]{1,0:T(8,128)(2,1)S(1)}, bf16[256,1024]{1,0:T(8,128)(2,1)}, u32[]{:S(2)}) copy-start(bf16[256,1024]{1,0:T(8,128)(2,1)} %param.11) | copy-start | bytes 1572868
  1.7 20.8 %all-to-all-start = ((bf16[32,2,1408]{2,1,0:T(2,128)(2,1)}), bf16[32,2,1408]{2,1,0:T(2,128)(2,1)S(1)}, u32[]{:S(2)}, u32[]{:S(2)}) async-start(bf16[32,2,1408]{2,1,0:T(2,128)(2,1)} %shard_map.73), calls=%async_computation | async-start | bytes 360448 | tf_op jit(solution)/shard_map/all_to_all | solution.py:122
  24.2 32.4 %all-to-all-start.1 = ((bf16[16,194,128]{2,1,0:T(8,128)(2,1)}), bf16[16,194,128]{2,1,0:T(8,128)(2,1)S(1)}, u32[]{:S(2)}, u32[]{:S(2)}) async-start(bf16[16,194,128]{2,1,0:T(8,128)(2,1)} %bitcast.4), calls=%async_computation.1 | async-start | bytes 1638400 | tf_op jit(solution)/shard_map/all_to_all | solution.py:167
  35.6 3.3 %collective-permute-start = (bf16[128,514]{1,0:T(8,128)(2,1)S(1)}, bf16[128,514]{1,0:T(8,128)(2,1)S(1)}, u32[]{:S(2)}, u32[]{:S(2)}) collective-permute-start(bf16[128,514]{1,0:T(8,128)(2,1)S(1)} %pad_maximum_fusion.1), channel_id=1, source_target_pairs={{0,4},{4,0},{8,12},{12,8},{1,5},{5,1},{9,13},{13,9},{2,6},{6,2},{1... | collective-permute-start | bytes 394760 | tf_op jit(solution)/shard_map/ppermute | solution.py:54
  60.3 4.2 %collective-permute-start.1 = (f32[128,520]{0,1:T(8,128)S(1)}, f32[128,520]{0,1:T(8,128)S(1)}, u32[]{:S(2)}, u32[]{:S(2)}) collective-permute-start(f32[128,520]{0,1:T(8,128)S(1)} %pad_maximum_fusion), channel_id=1, source_target_pairs={{0,4},{4,0},{8,12},{12,8},{1,5},{5,1},{9,13},{13,9},{2,6},{6,2},{1... | collective-permute-start | bytes 798728 | tf_op jit(solution)/shard_map/ppermute | solution.py:54

commit v16 on v15

--- a/solution.py
+++ b/solution.py
@@ -209,21 +209,21 @@
     coded = jnp.pad(coded, ((0, 0), (0, code_width - coded.shape[1])))
     partial = jnp.concatenate([normed, coded], axis=1)
 
-    back = lax.all_to_all(partial.reshape(seq_count, tok_rows, -1), "seq", 0, 0, tiled=True)
-    back = back.reshape(seq_count // 2, 2, tok_rows, -1)
-    half_num = back[..., :split_at].astype(jnp.float32).reshape(seq_count // 2, 2, tok_rows, pair_heads, HD)
+    back = lax.all_to_all(partial.reshape(seq_count, tok_rows, -1), "seq", 0, 2, tiled=True)
+    back = back.reshape(tok_rows, seq_count // 2, 2, -1)
+    half_num = back[..., :split_at].astype(jnp.float32).reshape(tok_rows, seq_count // 2, 2, pair_heads, HD)
     half_log = (
         back[..., split_at : split_at + 3 * pair_heads]
         .astype(jnp.float32)
-        .reshape(seq_count // 2, 2, tok_rows, 3, pair_heads)
+        .reshape(tok_rows, seq_count // 2, 2, 3, pair_heads)
         .sum(axis=3)
     )
-    best = jnp.maximum(half_log[:, 0], half_log[:, 1])
-    w0 = jnp.exp(half_log[:, 0] - best)
-    w1 = jnp.exp(half_log[:, 1] - best)
-    num = half_num[:, 0] * w0[..., None] + half_num[:, 1] * w1[..., None]
+    best = jnp.maximum(half_log[:, :, 0], half_log[:, :, 1])
+    w0 = jnp.exp(half_log[:, :, 0] - best)
+    w1 = jnp.exp(half_log[:, :, 1] - best)
+    num = half_num[:, :, 0] * w0[..., None] + half_num[:, :, 1] * w1[..., None]
     context = (num / (w0 + w1)[..., None]).astype(jnp.bfloat16)
-    return context.transpose(1, 0, 2, 3).reshape(tok_rows, -1)
+    return context.reshape(tok_rows, -1)
 
 
 def pl_cdiv(a, b):

time: 82.7 us -> 83.4 us (level)
  no operation moved by 1% of the time
where the time goes in v16:
time: 83.4 us; the launch traced here: 83 us
  waiting for transfers between devices  27.6 us (33%)
  starting transfers between devices  24.8 us (30%)
  blocking collectives  15.2 us (18%)
  local copies, waits for them, and re-layouts  5.55 us (7%)
  other arithmetic  3.78 us (5%)
  matrix products  3.13 us (4%)
  Pallas kernels  1.68 us (2%)
  between operations  1.18 us (1%)
    all_to_all x1, waiting for transfers between devices, on_device(): every = lax.all_to_all(per_dest, cell_axes, 0, 0, tiled=True)  17.3 us
    all_to_all x1, blocking collectives, on_device(): lax.all_to_all(partial.reshape(seq_count, tok_rows, -1), 'seq', 0, 2, til...  15.2 us
    all_to_all x1, starting transfers between devices, on_device(): every = lax.all_to_all(per_dest, cell_axes, 0, 0, tiled=True)  10.4 us
    all_to_all x1, starting transfers between devices, on_device(): recv = lax.all_to_all(send, 'seq', 0, 0, tiled=True)  10.2 us
    all_to_all x1, waiting for transfers between devices, on_device(): recv = lax.all_to_all(send, 'seq', 0, 0, tiled=True)  9.7 us
    ppermute x2, starting transfers between devices, swap(): return lax.ppermute(x, axes, pairs)  4.23 us
    pallas_call x1, Pallas kernels, build_send(): pl.pallas_call(send_kernel, in_specs=[pl.BlockSpec(memory_space=pltpu.VME...  1.68 us
  transfers between devices with their start and end apart: 4, of which 3 were waited for; matrix products, arithmetic and copies ran while one was open for 5% of the time, Pallas kernels for 0%

profile of v16, /device:TPU:8, one launch (start us, length us, event | category | flops | bytes accessed | tf_op | source)
XLA Modules:
  0.0 83.0 jit_solution(8129132275962496449)
XLA Ops:
  0.0 1.7 %shard_map.73 = bf16[32,2,1408]{2,1,0:T(2,128)(2,1)} custom-call(bf16[4,8192]{1,0:T(4,128)(2,1)} %q_ref.1, bf16[4,1024]{1,0:T(4,128)(2,1)} %k_ref.1, bf16[4,1024]{1,0:T(4,128)(2,1)} %v_ref.1, s32[1,4]{1,0:T(1,128)} %bitcast.70), custom_call_target="tpu_custom_call" | custom-call | tf_op jit(solution)/shard_map/pallas_call | solution.py:91
  1.7 10.2 %all-to-all-start = ((bf16[32,2,1408]{2,1,0:T(2,128)(2,1)}), bf16[32,2,1408]{2,1,0:T(2,128)(2,1)S(1)}, u32[]{:S(2)}, u32[]{:S(2)}) async-start(bf16[32,2,1408]{2,1,0:T(2,128)(2,1)} %shard_map.73), calls=%async_computation | async-start | bytes 360448 | tf_op jit(solution)/shard_map/all_to_all | solution.py:122
  11.9 0.9 %constant_dynamic-slice_fusion.1 = (bf16[256,128]{1,0:T(8,128)(2,1)S(1)}, bf16[256,128]{1,0:T(8,128)(2,1)S(1)}) fusion(bf16[256,1024]{1,0:T(8,128)(2,1)} %param.12, s32[]{:T(128)S(6)} %select_n.41, bf16[256,1024]{1,0:T(8,128)(2,1)} %param.11), kind=kLoop, calls=%fused_computation.71 | loop fusion | bytes 262148 | tf_op jit(solution)/shard_map/dynamic_slice | solution.py:140
  12.8 9.7 %all-to-all-done = bf16[32,2,1408]{2,1,0:T(2,128)(2,1)S(1)} async-done(((bf16[32,2,1408]{2,1,0:T(2,128)(2,1)}), bf16[32,2,1408]{2,1,0:T(2,128)(2,1)S(1)}, u32[]{:S(2)}, u32[]{:S(2)}) %all-to-all-start) | async-done | bytes 180256 | tf_op jit(solution)/shard_map/all_to_all | solution.py:122
  22.5 0.1 slice_reduce_fusion
  22.6 0.1 copy.54
  22.7 0.1 copy.55
  22.8 0.1 reshape_reshape.6
  23.1 1.0 %broadcast_in_dim.63 = bf16[2,2,4,194,128]{4,3,2,1,0:T(8,128)(2,1)} broadcast(bf16[2,194,128]{2,1,0:T(8,128)(2,1)S(1)} %maximum_bitcast_fusion.6), dimensions={1,3,4} | broadcast | bytes 893952 | tf_op jit(solution)/shard_map/broadcast_in_dim | solution.py:164
  24.1 10.4 %all-to-all-start.1 = ((bf16[16,194,128]{2,1,0:T(8,128)(2,1)}), bf16[16,194,128]{2,1,0:T(8,128)(2,1)S(1)}, u32[]{:S(2)}, u32[]{:S(2)}) async-start(bf16[16,194,128]{2,1,0:T(8,128)(2,1)} %bitcast.4), calls=%async_computation.1 | async-start | bytes 1638400 | tf_op jit(solution)/shard_map/all_to_all | solution.py:167
  35.2 0.1 reshape_reshape_squeeze.4
  35.3 0.1 slice.151
  35.4 0.1 reshape_reshape.7
  35.5 2.3 %collective-permute-start = (bf16[128,514]{1,0:T(8,128)(2,1)S(1)}, bf16[128,514]{1,0:T(8,128)(2,1)S(1)}, u32[]{:S(2)}, u32[]{:S(2)}) collective-permute-start(bf16[128,514]{1,0:T(8,128)(2,1)S(1)} %pad_maximum_fusion.1), channel_id=1, source_target_pairs={{0,4},{4,0},{8,12},{12,8},{1,5},{5,1},{9,13},{13,9},{2,6},{6,2},{1... | collective-permute-start | bytes 394760 | tf_op jit(solution)/shard_map/ppermute | solution.py:54
  37.8 0.1 add_compare_fusion
  37.9 0.1 reshape.178
  38.0 0.1 reshape.148
  38.1 0.2 fusion.19
  38.3 0.6 collective-permute-done
  38.9 0.1 copy.57
  39.0 0.2 fusion.18
  39.2 17.3 %all-to-all-done.1 = bf16[16,194,128]{2,1,0:T(8,128)(2,1)S(1)} async-done(((bf16[16,194,128]{2,1,0:T(8,128)(2,1)}), bf16[16,194,128]{2,1,0:T(8,128)(2,1)S(1)}, u32[]{:S(2)}, u32[]{:S(2)}) %all-to-all-start.1) | async-done | bytes 794656 | tf_op jit(solution)/shard_map/all_to_all | solution.py:167
  56.5 0.3 reshape.147
  56.9 0.3 reshape.160
  57.2 0.2 fusion.14
  57.5 0.1 broadcast_compare_fusion
  57.6 0.1 pad_add_fusion.1
  57.8 0.8 %select_reduce_fusion = (f32[128,4]{0,1:T(4,128)S(1)}, f32[128,4,1536]{2,0,1:T(8,128)S(1)}) fusion(pred[128,1536]{1,0:T(8,128)(4,1)S(1)} %get-tuple-element.29, bf16[128,4,128]{0,2,1:T(8,128)(2,1)S(1)} %bitcast.66, bf16[512,128]{1,0:T(8,128)(2,1)S(1)} %get-tuple-element.18, bf16[1024,128]{1,0:T(8,128)(2,1)S(1)} %get-tuple-element.14), kind=kOutput, calls=%fused_computation.3 | convolution fusion | flops 204471808 | bytes 3868672 | tf_op jit(solution)/shard_map/thd,nd->thn/dot_general | solution.py:43
  58.6 0.8 fusion.2
  59.4 0.8 fusion.4
  60.2 1.9 %collective-permute-start.1 = (f32[128,520]{0,1:T(8,128)S(1)}, f32[128,520]{0,1:T(8,128)S(1)}, u32[]{:S(2)}, u32[]{:S(2)}) collective-permute-start(f32[128,520]{0,1:T(8,128)S(1)} %pad_maximum_fusion), channel_id=1, source_target_pairs={{0,4},{4,0},{8,12},{12,8},{1,5},{5,1},{9,13},{13,9},{2,6},{6,2},{1... | collective-permute-start | bytes 798728 | tf_op jit(solution)/shard_map/ppermute | solution.py:54
  62.2 0.8 select_reduce_fusion.1
  62.9 0.7 fusion.6
  63.6 0.8 fusion
  64.4 0.0 collective-permute-done.1
  64.4 0.1 copy.60
  64.6 0.3 divide_convert_fusion
  64.9 0.1 copy.61
  65.0 0.1 concatenate.45
  65.1 0.1 copy.62
  65.3 0.1 pad_maximum_fusion.2
  65.3 15.2 %all_to_all.25 = bf16[32,4,640]{2,1,0:T(4,128)(2,1)S(1)} all-to-all(bf16[32,4,640]{2,1,0:T(4,128)(2,1)S(1)} %pad_maximum_fusion.2), channel_id=1, replica_groups=mesh['seq'=32,'row'=4,'col'=4] {'seq'}, dimensions={0} | all-to-all | bytes 327680 | tf_op jit(solution)/shard_map/all_to_all | solution.py:212
  80.6 0.1 copy.76
  80.9 0.1 copy.70
  81.0 0.1 copy.69
  81.1 0.1 copy.67
  81.2 0.1 mul.113
  81.3 0.1 mul.114
  81.4 0.1 mul.116
  81.5 0.1 mul.117
  81.6 0.1 div.32
  81.8 0.1 div.33
  81.8 0.2 reshape.162
  82.1 0.1 squeeze.11
  82.2 0.1 squeeze.27
  82.3 0.7 fusion.16
  (39 shorter events, 0.6 us)
Async XLA Ops:
  1.7 20.8 %all-to-all-start = ((bf16[32,2,1408]{2,1,0:T(2,128)(2,1)}), bf16[32,2,1408]{2,1,0:T(2,128)(2,1)S(1)}, u32[]{:S(2)}, u32[]{:S(2)}) async-start(bf16[32,2,1408]{2,1,0:T(2,128)(2,1)} %shard_map.73), calls=%async_computation | async-start | bytes 360448 | tf_op jit(solution)/shard_map/all_to_all | solution.py:122
  24.1 32.4 %all-to-all-start.1 = ((bf16[16,194,128]{2,1,0:T(8,128)(2,1)}), bf16[16,194,128]{2,1,0:T(8,128)(2,1)S(1)}, u32[]{:S(2)}, u32[]{:S(2)}) async-start(bf16[16,194,128]{2,1,0:T(8,128)(2,1)} %bitcast.4), calls=%async_computation.1 | async-start | bytes 1638400 | tf_op jit(solution)/shard_map/all_to_all | solution.py:167
  35.5 3.3 %collective-permute-start = (bf16[128,514]{1,0:T(8,128)(2,1)S(1)}, bf16[128,514]{1,0:T(8,128)(2,1)S(1)}, u32[]{:S(2)}, u32[]{:S(2)}) collective-permute-start(bf16[128,514]{1,0:T(8,128)(2,1)S(1)} %pad_maximum_fusion.1), channel_id=1, source_target_pairs={{0,4},{4,0},{8,12},{12,8},{1,5},{5,1},{9,13},{13,9},{2,6},{6,2},{1... | collective-permute-start | bytes 394760 | tf_op jit(solution)/shard_map/ppermute | solution.py:54
  60.2 4.2 %collective-permute-start.1 = (f32[128,520]{0,1:T(8,128)S(1)}, f32[128,520]{0,1:T(8,128)S(1)}, u32[]{:S(2)}, u32[]{:S(2)}) collective-permute-start(f32[128,520]{0,1:T(8,128)S(1)} %pad_maximum_fusion), channel_id=1, source_target_pairs={{0,4},{4,0},{8,12},{12,8},{1,5},{5,1},{9,13},{13,9},{2,6},{6,2},{1... | collective-permute-start | bytes 798728 | tf_op jit(solution)/shard_map/ppermute | solution.py:54
